TPU v7x, 128 devices: a whole 4x4x4 slice. The times are simulated.
128 devices in a mesh: row: 8 (over z_hi, x), col: 16 (over z_lo, y, core).
Axes of the slice: x: 4, y: 4, z: 4 (z_hi: 2, z_lo: 2; z = z_hi * 2 + z_lo), core: 2. Of those that a mesh axis runs over, the one named last changes fastest.
Arguments:
- tokens: bfloat16 [1024, 8192], P(('row', 'col')), may hold values from -6 to 6
- gain: float32 [8192], replicated, may hold values from 0.5 to 1.5
- grad_out: bfloat16 [1024, 8192], P(('row', 'col')), may hold values from -4 to 4
- pre_gate: bfloat16 [1024, 28672], P('col', 'row'), may hold values from -6 to 6
- pre_up: bfloat16 [1024, 28672], P('col', 'row'), may hold values from -6 to 6
- gate_weight: bfloat16 [8192, 28672], P('col', 'row'), may hold values from -0.0625 to 0.0625
- up_weight: bfloat16 [8192, 28672], P('col', 'row'), may hold values from -0.0625 to 0.0625
- down_weight: bfloat16 [28672, 8192], P('row', 'col'), may hold values from -0.03125 to 0.03125
Outputs:
- grad_tokens: bfloat16 [1024, 8192], P(('row', 'col'))
- grad_gain: float32 [8192], replicated
- grad_gate: bfloat16 [8192, 28672], P('col', 'row')
- grad_up: bfloat16 [8192, 28672], P('col', 'row')
- grad_down: bfloat16 [28672, 8192], P('row', 'col')
All inputs are finite; a program needn't handle non-finite values.
Results may differ from a plain program's by a relative error of at most 0.0057.
Values may be sent and summed in bfloat16 or wider, within the bound.
No kernel may reach another device: no remote copies, remote signals or barrier semaphores. Data moves between devices by JAX's collectives and lax.ppermute only.
A program may use at most 192 MiB of HBM per device.

v0:
```python
import jax
import jax.numpy as jnp
from jax import lax
from jax.sharding import PartitionSpec as P

epsilon = 1e-05


def swiglu_grads(hidden_grad, pre_gate, pre_up):
    gate_wide = pre_gate.astype(jnp.float32)
    up_wide = pre_up.astype(jnp.float32)
    sigmoid = jax.nn.sigmoid(gate_wide)
    silu = gate_wide * sigmoid
    hidden = (silu * up_wide).astype(jnp.bfloat16)
    up_grad = (hidden_grad * silu).astype(jnp.bfloat16)
    gate_grad = (hidden_grad * up_wide * sigmoid * (1.0 + gate_wide * (1.0 - sigmoid))).astype(
        jnp.bfloat16
    )
    return (hidden, gate_grad, up_grad)


def local(tokens, gain, grad_out, pre_gate, pre_up, gate_weight, up_weight, down_weight):
    tokens_wide = tokens.astype(jnp.float32)
    inverse_rms = lax.rsqrt(jnp.mean(tokens_wide * tokens_wide, axis=1, keepdims=True) + epsilon)
    normed = tokens_wide * inverse_rms
    scaled = (normed * gain).astype(jnp.bfloat16)
    grid_input, grid_grad = (
        lax.all_to_all(scaled, "col", split_axis=1, concat_axis=0, tiled=True),
        lax.all_to_all(grad_out, "col", split_axis=1, concat_axis=0, tiled=True),
    )
    all_input, all_grad = (
        lax.all_gather(grid_input, "row", axis=0, tiled=True),
        lax.all_gather(grid_grad, "row", axis=0, tiled=True),
    )
    partial_grad = jnp.einsum(
        "td,fd->tf", all_grad, down_weight, preferred_element_type=jnp.float32
    )
    summed_grad = lax.psum(partial_grad, "col")
    hidden_piece, gate_piece, up_piece = swiglu_grads(
        summed_grad,
        lax.all_gather(pre_gate, "col", axis=0, tiled=True),
        lax.all_gather(pre_up, "col", axis=0, tiled=True),
    )
    down_total = jnp.einsum("tf,td->fd", hidden_piece, all_grad, preferred_element_type=jnp.float32)
    gate_total = jnp.einsum("td,tf->df", all_input, gate_piece, preferred_element_type=jnp.float32)
    up_total = jnp.einsum("td,tf->df", all_input, up_piece, preferred_element_type=jnp.float32)
    new_rows = jnp.einsum("tf,df->td", gate_piece, gate_weight, preferred_element_type=jnp.float32)
    new_rows = new_rows + jnp.einsum(
        "tf,df->td", up_piece, up_weight, preferred_element_type=jnp.float32
    )
    back_rows = new_rows
    results = (down_total, gate_total, up_total, back_rows)
    down_total, gate_total, up_total, back_rows = results
    grid_back = lax.psum_scatter(back_rows, "row", scatter_dimension=0, tiled=True)
    normed_grad = lax.all_to_all(grid_back, "col", split_axis=0, concat_axis=1, tiled=True)
    grad_gain = lax.psum(jnp.sum(normed_grad * normed, axis=0), ("row", "col"))
    scaled_grad = normed_grad * gain
    inner = jnp.mean(scaled_grad * normed, axis=1, keepdims=True)
    grad_tokens = (
        grad_out.astype(jnp.float32) + inverse_rms * (scaled_grad - normed * inner)
    ).astype(jnp.bfloat16)
    return (
        grad_tokens,
        grad_gain,
        gate_total.astype(jnp.bfloat16),
        up_total.astype(jnp.bfloat16),
        down_total.astype(jnp.bfloat16),
    )


def solution(mesh):
    in_specs = (
        P(("row", "col"), None),
        P(),
        P(("row", "col"), None),
        P("col", "row"),
        P("col", "row"),
        P("col", "row"),
        P("col", "row"),
        P("row", "col"),
    )
    out_specs = (P(("row", "col"), None), P(), P("col", "row"), P("col", "row"), P("row", "col"))
    return jax.shard_map(local, mesh=mesh, in_specs=in_specs, out_specs=out_specs, check_vma=False)
```

profile of v0, /device:TPU:1, one launch (start us, length us, event | category | flops | bytes accessed | tf_op | source)
XLA Modules:
  0.0 565.8 jit_solution(3937982184247556598)
XLA Ops:
  7.2 0.0 all-gather.5.cloned.1.call-start
  7.2 13.5 %all_to_all.57 = bf16[8,16,512]{2,0,1:T(8,128)(2,1)} all-to-all(bf16[8,16,512]{2,0,1:T(8,128)(2,1)} %bitcast.27), channel_id=1, replica_groups=mesh['row'=8,'col'=16] {'col'}, dimensions={1} | all-to-all | bytes 262144 | tf_op jit(solution)/shard_map/all_to_all | solution.py:29
  20.7 0.0 all-gather.5.cloned.1.call-update
  20.7 0.0 all-gather.7.cloned.1.call-start
  20.8 0.7 all-gather.7.cloned.1.call-update
  21.5 0.0 all-gather.9.cloned.1.call-start
  21.5 0.7 all-gather.9.cloned.1.call-update
  22.2 0.0 all-reduce.2.cloned.1.call-start
  22.3 43.9 %all-gather.5.cloned.1.call-done = bf16[1024,512]{1,0:T(8,128)(2,1)} async-done(((bf16[128,512]{1,0:T(8,128)(2,1)}), bf16[1024,512]{1,0:T(8,128)(2,1)}) %all-gather.5.cloned.1.call-update) | async-done | bytes 1048592 | tf_op jit(solution)/shard_map/all_gather | solution.py:33
  66.2 11.5 %fusion.26 = f32[1024,3584]{1,0:T(8,128)} fusion(bf16[1024,512]{1,0:T(8,128)(2,1)} %all-gather.5.cloned.1.call-done, bf16[3584,512]{1,0:T(8,128)(2,1)} %param.15), kind=kOutput, calls=%fused_computation.36 | convolution fusion | flops 3758096384 | bytes 19398656 | tf_op jit(solution)/shard_map/td,fd->tf/dot_general | solution.py:35
  77.7 0.0 all-reduce.2.cloned.1.call-update
  77.7 0.0 reduce-scatter.2.cloned.1.call-start
  77.8 38.1 %all-gather.7.cloned.1.call-done = bf16[1024,3584]{1,0:T(8,128)(2,1)} async-done(((bf16[64,3584]{1,0:T(8,128)(2,1)}), bf16[1024,3584]{1,0:T(8,128)(2,1)}) %all-gather.7.cloned.1.call-update) | async-done | bytes 7340048 | tf_op jit(solution)/shard_map/all_gather | solution.py:42
  115.8 49.7 %all-gather.9.cloned.1.call-done = bf16[1024,3584]{1,0:T(8,128)(2,1)} async-done(((bf16[64,3584]{1,0:T(8,128)(2,1)}), bf16[1024,3584]{1,0:T(8,128)(2,1)}) %all-gather.9.cloned.1.call-update) | async-done | bytes 7340048 | tf_op jit(solution)/shard_map/all_gather | solution.py:41
  165.6 177.7 %all-reduce.2.cloned.1.call-done = f32[1024,3584]{1,0:T(8,128)} async-done(((f32[1024,3584]{1,0:T(8,128)}), f32[1024,3584]{1,0:T(8,128)}) %all-reduce.2.cloned.1.call-update) | async-done | bytes 14680080 | tf_op jit(solution)/shard_map/psum | solution.py:38
  343.3 0.0 copy-start.6
  343.3 12.5 %multiply_convert_fusion = (bf16[1024,3584]{1,0:T(8,128)(2,1)S(1)}, bf16[1024,3584]{1,0:T(8,128)(2,1)S(1)}) fusion(f32[1024,3584]{1,0:T(8,128)} %all-reduce.2.cloned.1.call-done, bf16[1024,3584]{1,0:T(8,128)(2,1)} %all-gather.9.cloned.1.call-done, bf16[1024,3584]{1,0:T(8,128)(2,1)} %all-gather.7.cloned.1.call-done), kind=kLoop, calls=%fused_computation.13 | loop fusion | flops 55050240 | bytes 44040192 | tf_op jit(solution)/shard_map/convert_element_type | solution.py:15
  355.8 0.0 copy-start
  355.8 0.0 copy-start.1
  355.8 0.0 copy-done.6
  355.8 0.0 copy-start.7
  355.8 4.0 fusion.27
  359.8 0.0 copy-done
  359.8 2.0 copy-done.1
  361.8 0.0 copy-done.7
  361.8 0.0 copy-start.2
  361.8 5.3 convolution_add_fusion
  367.1 0.0 reduce-scatter.2.cloned.1.call-update
  367.1 75.7 %reduce-scatter.2.cloned.1.call-done = f32[128,512]{1,0:T(8,128)} async-done(((f32[1024,512]{1,0:T(8,128)}), f32[128,512]{1,0:T(8,128)}) %reduce-scatter.2.cloned.1.call-update) | async-done | bytes 262160 | tf_op jit(solution)/shard_map/reduce_scatter | solution.py:54
  442.8 6.5 %all-to-all-start.1 = ((f32[16,8,512]{2,1,0:T(8,128)}), f32[16,8,512]{2,1,0:T(8,128)S(1)}, u32[]{:S(2)}, u32[]{:S(2)}) async-start(f32[16,8,512]{2,1,0:T(8,128)} %bitcast.28), calls=%async_computation.2 | async-start | bytes 524288 | tf_op jit(solution)/shard_map/all_to_all | solution.py:55
  449.3 0.0 copy-done.2
  449.3 0.2 fusion.24
  449.5 7.0 %all-to-all-done.1 = f32[16,8,512]{2,1,0:T(8,128)S(1)} async-done(((f32[16,8,512]{2,1,0:T(8,128)}), f32[16,8,512]{2,1,0:T(8,128)S(1)}, u32[]{:S(2)}, u32[]{:S(2)}) %all-to-all-start.1) | async-done | bytes 262176 | tf_op jit(solution)/shard_map/all_to_all | solution.py:55
  456.5 0.0 copy-done.5
  456.5 0.9 fusion.22
  457.5 4.0 all-to-all-start.2
  461.5 0.2 all-gather.11.cloned.1.call-start
  461.8 0.0 copy-done.8
  461.8 10.3 %fusion.10 = bf16[3584,512]{1,0:T(8,128)(2,1)} fusion(bf16[1024,512]{1,0:T(8,128)(2,1)S(1)} %copy-done.8, bf16[1024,3584]{1,0:T(8,128)(2,1)} %all-gather.7.cloned.1.call-done, bf16[1024,3584]{1,0:T(8,128)(2,1)} %all-gather.9.cloned.1.call-done), kind=kOutput, calls=%fused_computation.15 | convolution fusion | flops 3789291520 | bytes 19398656 | tf_op jit(solution)/shard_map/tf,td->fd/dot_general | solution.py:44
  472.1 0.0 all-to-all-done.2
  472.1 0.7 copy-done.3
  472.7 0.0 all-gather.11.cloned.1.call-update
  472.8 67.5 %psum.15 = f32[8192]{0:T(1024)} all-reduce(f32[8192]{0:T(1024)S(1)} %get-tuple-element.5), channel_id=1, replica_groups=mesh['row'=8,'col'=16] {'row','col'}, use_global_device_ids=true, to_apply=%region_5.0 | all-reduce | flops 8192 | bytes 65536 | tf_op jit(solution)/shard_map/psum | solution.py:56
  540.3 0.0 copy-done.4
  540.3 0.8 fusion.21
  541.1 9.3 %convolution_convert_fusion = bf16[512,3584]{1,0:T(8,128)(2,1)} fusion(bf16[1024,512]{1,0:T(8,128)(2,1)} %all-gather.11.cloned.1.call-done, bf16[1024,3584]{1,0:T(8,128)(2,1)} %copy-done.1), kind=kOutput, calls=%fused_computation.16 | convolution fusion | flops 3759931392 | bytes 12058624 | tf_op jit(solution)/shard_map/td,tf->df/dot_general | solution.py:46
  550.4 0.0 copy-done.9
  550.4 8.5 %convolution_convert_fusion.1 = bf16[512,3584]{1,0:T(8,128)(2,1)} fusion(bf16[1024,512]{1,0:T(8,128)(2,1)S(1)} %copy-done.9, bf16[1024,3584]{1,0:T(8,128)(2,1)} %copy-done), kind=kOutput, calls=%fused_computation.17 | convolution fusion | flops 3759931392 | bytes 12058624 | tf_op jit(solution)/shard_map/td,tf->df/dot_general | solution.py:45
  (8 shorter events, 0.0 us)
Async XLA Ops:
  7.2 59.0 %all-gather.5.cloned.1.call-start = ((), (), s32[]{:S(2)}) async-start(), calls=%async_computation.4 | async-start | bytes 1179648 | tf_op jit(solution)/shard_map/all_gather | solution.py:33
  20.7 95.1 %all-gather.7.cloned.1.call-start = ((), (), s32[]{:S(2)}) async-start(), calls=%async_computation.6 | async-start | bytes 7798784 | tf_op jit(solution)/shard_map/all_gather | solution.py:42
  21.5 144.1 %all-gather.9.cloned.1.call-start = ((), (), s32[]{:S(2)}) async-start(), calls=%async_computation.7 | async-start | bytes 7798784 | tf_op jit(solution)/shard_map/all_gather | solution.py:41
  22.2 321.1 %all-reduce.2.cloned.1.call-start = ((), (), s32[]{:S(2)}) async-start(), calls=%async_computation.5 | async-start | bytes 29360128 | tf_op jit(solution)/shard_map/psum | solution.py:38
  77.7 365.1 %reduce-scatter.2.cloned.1.call-start = ((), (), s32[]{:S(2)}) async-start(), calls=%async_computation.8 | async-start | bytes 2359296 | tf_op jit(solution)/shard_map/reduce_scatter | solution.py:54
  343.3 12.5 %copy-start.6 = (bf16[512,3584]{1,0:T(8,128)(2,1)S(1)}, bf16[512,3584]{1,0:T(8,128)(2,1)}, u32[]{:S(2)}) copy-start(bf16[512,3584]{1,0:T(8,128)(2,1)} %param.13) | copy-start | bytes 11010052
  355.8 4.0 copy-start
  355.8 6.0 %copy-start.1 = (bf16[1024,3584]{1,0:T(8,128)(2,1)}, bf16[1024,3584]{1,0:T(8,128)(2,1)S(1)}, u32[]{:S(2)}) copy-start(bf16[1024,3584]{1,0:T(8,128)(2,1)S(1)} %get-tuple-element.7) | copy-start | bytes 22020100
  355.8 6.0 %copy-start.7 = (bf16[512,3584]{1,0:T(8,128)(2,1)S(1)}, bf16[512,3584]{1,0:T(8,128)(2,1)}, u32[]{:S(2)}) copy-start(bf16[512,3584]{1,0:T(8,128)(2,1)} %param.14) | copy-start | bytes 11010052
  361.8 87.6 %copy-start.2 = (bf16[8,8192]{1,0:T(8,128)(2,1)S(1)}, bf16[8,8192]{1,0:T(8,128)(2,1)}, u32[]{:S(2)}) copy-start(bf16[8,8192]{1,0:T(8,128)(2,1)} %param.8) | copy-start | bytes 393220
  361.8 94.8 %copy-start.5 = (f32[8192]{0:T(1024)S(1)}, f32[8192]{0:T(1024)}, u32[]{:S(2)}) copy-start(f32[8192]{0:T(1024)} %param.9) | copy-start | bytes 98308
  361.8 100.0 %copy-start.8 = (bf16[1024,512]{1,0:T(8,128)(2,1)S(1)}, bf16[1024,512]{1,0:T(8,128)(2,1)}, u32[]{:S(2)}) copy-start(bf16[1024,512]{1,0:T(8,128)(2,1)} %all-gather.5.cloned.1.call-done) | copy-start | bytes 3145732
  442.8 13.7 %all-to-all-start.1 = ((f32[16,8,512]{2,1,0:T(8,128)}), f32[16,8,512]{2,1,0:T(8,128)S(1)}, u32[]{:S(2)}, u32[]{:S(2)}) async-start(f32[16,8,512]{2,1,0:T(8,128)} %bitcast.28), calls=%async_computation.2 | async-start | bytes 524288 | tf_op jit(solution)/shard_map/all_to_all | solution.py:55
  457.5 14.6 %all-to-all-start.2 = ((bf16[8,16,512]{2,0,1:T(8,128)(2,1)}), bf16[8,16,512]{2,0,1:T(8,128)(2,1)S(1)}, u32[]{:S(2)}, u32[]{:S(2)}) async-start(bf16[8,16,512]{2,0,1:T(8,128)(2,1)} %bitcast.7), calls=%async_computation.3 | async-start | bytes 262144 | tf_op jit(solution)/shard_map/all_to_all | solution.py:28
  461.5 78.8 %copy-start.4 = (bf16[8,8192]{1,0:T(8,128)(2,1)S(1)}, bf16[8,8192]{1,0:T(8,128)(2,1)}, u32[]{:S(2)}) copy-start(bf16[8,8192]{1,0:T(8,128)(2,1)} %param.10) | copy-start | bytes 393220
  461.5 79.6 %all-gather.11.cloned.1.call-start = ((), (), s32[]{:S(2)}) async-start(), calls=%async_computation.9 | async-start | bytes 1179648 | tf_op jit(solution)/shard_map/all_gather | solution.py:32
  472.1 0.7 copy-start.3
  541.1 9.3 %copy-start.9 = (bf16[1024,512]{1,0:T(8,128)(2,1)S(1)}, bf16[1024,512]{1,0:T(8,128)(2,1)}, u32[]{:S(2)}) copy-start(bf16[1024,512]{1,0:T(8,128)(2,1)} %all-gather.11.cloned.1.call-done) | copy-start | bytes 3145732
Sparse Core Ops, SparseCore 0:
  20.8 45.2 all-gather.4
  67.9 47.9 all-gather.6
  117.5 47.9 all-gather.8
  168.0 175.2 all-reduce.1
  367.2 75.5 reduce-scatter.1
  472.9 45.2 all-gather.10
where the time goes:
time: 566 us
  waiting for transfers between devices  394 us (70%)
  blocking collectives  81 us (14%)
  matrix products  48.9 us (9%)
  other arithmetic  14.4 us (3%)
  between operations  14.2 us (3%)
  starting transfers between devices  11 us (2%)
    psum x1, waiting for transfers between devices, local(): summed_grad = lax.psum(partial_grad, 'col')  178 us
    reduce_scatter x1, waiting for transfers between devices, local(): lax.psum_scatter(back_rows, 'row', scatter_dimension=0, tiled=True)  75.7 us
    psum x1, blocking collectives, local(): grad_gain = lax.psum(jnp.sum(normed_grad * normed, axis=0), ('row', 'col'))  67.5 us
    all_gather x1, waiting for transfers between devices, local(): lax.all_gather(pre_gate, 'col', axis=0, tiled=True)  49.7 us
    all_gather x1, waiting for transfers between devices, local(): lax.all_gather(grid_grad, 'row', axis=0, tiled=True)  43.9 us
    all_gather x1, waiting for transfers between devices, local(): lax.all_gather(pre_up, 'col', axis=0, tiled=True)  38.1 us
    all_to_all x1, blocking collectives, local(): lax.all_to_all(grad_out, 'col', split_axis=1, concat_axis=0, tiled=True)  13.5 us
    convert_element_type x1, other arithmetic, swiglu_grads(): up_grad = (hidden_grad * silu).astype(jnp.bfloat16)  12.5 us
  transfers between devices with their start and end apart: 8, of which 6 were waited for; matrix products, arithmetic and copies ran while one was open for 4% of the time, Pallas kernels for 0%

commit v1 on v0

--- a/solution.py
+++ b/solution.py
@@ -35,25 +35,22 @@
     partial_grad = jnp.einsum(
         "td,fd->tf", all_grad, down_weight, preferred_element_type=jnp.float32
     )
-    summed_grad = lax.psum(partial_grad, "col")
-    hidden_piece, gate_piece, up_piece = swiglu_grads(
-        summed_grad,
-        lax.all_gather(pre_gate, "col", axis=0, tiled=True),
-        lax.all_gather(pre_up, "col", axis=0, tiled=True),
-    )
-    down_total = jnp.einsum("tf,td->fd", hidden_piece, all_grad, preferred_element_type=jnp.float32)
-    gate_total = jnp.einsum("td,tf->df", all_input, gate_piece, preferred_element_type=jnp.float32)
-    up_total = jnp.einsum("td,tf->df", all_input, up_piece, preferred_element_type=jnp.float32)
+    block_grad = lax.psum_scatter(partial_grad, "col", scatter_dimension=0, tiled=True)
+    hidden_block, gate_block, up_block = swiglu_grads(block_grad, pre_gate, pre_up)
+    gate_piece = lax.all_gather(gate_block, "col", axis=0, tiled=True)
+    up_piece = lax.all_gather(up_block, "col", axis=0, tiled=True)
+    hidden_piece = lax.all_gather(hidden_block, "col", axis=0, tiled=True)
     new_rows = jnp.einsum("tf,df->td", gate_piece, gate_weight, preferred_element_type=jnp.float32)
     new_rows = new_rows + jnp.einsum(
         "tf,df->td", up_piece, up_weight, preferred_element_type=jnp.float32
     )
-    back_rows = new_rows
-    results = (down_total, gate_total, up_total, back_rows)
-    down_total, gate_total, up_total, back_rows = results
-    grid_back = lax.psum_scatter(back_rows, "row", scatter_dimension=0, tiled=True)
+    gate_total = jnp.einsum("td,tf->df", all_input, gate_piece, preferred_element_type=jnp.float32)
+    up_total = jnp.einsum("td,tf->df", all_input, up_piece, preferred_element_type=jnp.float32)
+    down_total = jnp.einsum("tf,td->fd", hidden_piece, all_grad, preferred_element_type=jnp.float32)
+    grid_back = lax.psum_scatter(new_rows, "row", scatter_dimension=0, tiled=True)
     normed_grad = lax.all_to_all(grid_back, "col", split_axis=0, concat_axis=1, tiled=True)
-    grad_gain = lax.psum(jnp.sum(normed_grad * normed, axis=0), ("row", "col"))
+    gain_terms = jnp.sum(normed_grad * normed, axis=0)
+    grad_gain = lax.psum(lax.psum(gain_terms, "col"), "row")
     scaled_grad = normed_grad * gain
     inner = jnp.mean(scaled_grad * normed, axis=1, keepdims=True)
     grad_tokens = (

time: 566 us -> 545 us (0.963)
  waiting for transfers between devices: 394 us -> 354 us
  blocking collectives: 81 us -> 101 us
  other arithmetic: 14.4 us -> 4.57 us
  matrix products: 48.9 us -> 57.5 us
    psum x1 -> x0, waiting for transfers between devices: 178 us -> none  [local(): summed_grad = lax.psum(partial_grad, 'col')]
    reduce_scatter x1 -> x2, waiting for transfers between devices: 75.7 us -> 162 us  [the longest x1 86.7 us: local(): lax.psum_scatter(partial_grad, 'col', scatter_dimension=0, tiled=True)]
    all_gather x2 -> x3, waiting for transfers between devices: 87.8 us -> 134 us  [the longest x1 49.3 us: local(): gate_piece = lax.all_gather(gate_block, 'col', axis=0, tiled=True)]
    psum x1 -> x2, blocking collectives: 67.5 us -> 87.2 us  [local(): grad_gain = lax.psum(lax.psum(gain_terms, 'col'), 'row')]
    all_gather x1, waiting for transfers between devices: 0.01 us -> 12.2 us  [local(): lax.all_gather(grid_input, 'row', axis=0, tiled=True)]
    convert_element_type x1, other arithmetic: 12.5 us -> 2.66 us  [swiglu_grads(): up_grad = (hidden_grad * silu).astype(jnp.bfloat16)]
    all_to_all x1, waiting for transfers between devices: 7 us -> 0.01 us  [local(): lax.all_to_all(grid_back, 'col', split_axis=0, concat_axis=1, tiled=True)]
  transfers between devices with their start and end apart: 8 -> 9, of which waited for: 6 -> 7; matrix products, arithmetic and copies ran while one was open for 4% -> 3% of each run, Pallas kernels for 0% -> 0%
where the time goes in v1:
time: 545 us; the launch traced here: 543 us
  waiting for transfers between devices  354 us (65%)
  blocking collectives  101 us (19%)
  matrix products  57.5 us (11%)
  between operations  14.2 us (3%)
  starting transfers between devices  11.6 us (2%)
    psum x2, blocking collectives, local(): grad_gain = lax.psum(lax.psum(gain_terms, 'col'), 'row')  87.2 us
    reduce_scatter x1, waiting for transfers between devices, local(): lax.psum_scatter(partial_grad, 'col', scatter_dimension=0, tiled=True)  86.7 us
    reduce_scatter x1, waiting for transfers between devices, local(): lax.psum_scatter(new_rows, 'row', scatter_dimension=0, tiled=True)  75 us
    all_gather x1, waiting for transfers between devices, local(): gate_piece = lax.all_gather(gate_block, 'col', axis=0, tiled=True)  49.3 us
    all_gather x1, waiting for transfers between devices, local(): lax.all_gather(grid_grad, 'row', axis=0, tiled=True)  45.4 us
    all_gather x1, waiting for transfers between devices, local(): hidden_piece = lax.all_gather(hidden_block, 'col', axis=0, tiled=True)  43.6 us
    all_gather x1, waiting for transfers between devices, local(): up_piece = lax.all_gather(up_block, 'col', axis=0, tiled=True)  40.7 us
    all_to_all x1, blocking collectives, local(): lax.all_to_all(grad_out, 'col', split_axis=1, concat_axis=0, tiled=True)  13.5 us
  transfers between devices with their start and end apart: 9, of which 7 were waited for; matrix products, arithmetic and copies ran while one was open for 3% of the time, Pallas kernels for 0%

profile of v1, /device:TPU:1, one launch (start us, length us, event | category | flops | bytes accessed | tf_op | source)
XLA Modules:
  0.0 543.3 jit_solution(9490995752814410187)
XLA Ops:
  7.2 0.0 all-gather.6.cloned.1.call-start
  7.2 13.5 %all_to_all.57 = bf16[8,16,512]{2,0,1:T(8,128)(2,1)} all-to-all(bf16[8,16,512]{2,0,1:T(8,128)(2,1)} %bitcast.28), channel_id=1, replica_groups=mesh['row'=8,'col'=16] {'col'}, dimensions={1} | all-to-all | bytes 262144 | tf_op jit(solution)/shard_map/all_to_all | solution.py:29
  20.7 0.0 all-gather.6.cloned.1.call-update
  20.7 0.0 reduce-scatter.3.cloned.1.call-start
  20.8 45.4 %all-gather.6.cloned.1.call-done = bf16[1024,512]{1,0:T(8,128)(2,1)} async-done(((bf16[128,512]{1,0:T(8,128)(2,1)}), bf16[1024,512]{1,0:T(8,128)(2,1)}) %all-gather.6.cloned.1.call-update) | async-done | bytes 1048592 | tf_op jit(solution)/shard_map/all_gather | solution.py:33
  66.2 11.6 %fusion.20 = f32[1024,3584]{1,0:T(8,128)} fusion(bf16[1024,512]{1,0:T(8,128)(2,1)} %all-gather.6.cloned.1.call-done, bf16[3584,512]{1,0:T(8,128)(2,1)} %param.15), kind=kOutput, calls=%fused_computation.34 | convolution fusion | flops 3758096384 | bytes 19398656 | tf_op jit(solution)/shard_map/td,fd->tf/dot_general | solution.py:35
  77.7 0.0 copy-start.3
  77.7 0.0 reduce-scatter.3.cloned.1.call-update
  77.8 0.0 all-gather.8.cloned.1.call-start
  77.8 86.7 %reduce-scatter.3.cloned.1.call-done = f32[64,3584]{1,0:T(8,128)} async-done(((f32[1024,3584]{1,0:T(8,128)}), f32[64,3584]{1,0:T(8,128)}) %reduce-scatter.3.cloned.1.call-update) | async-done | bytes 917520 | tf_op jit(solution)/shard_map/reduce_scatter | solution.py:38
  164.5 0.0 copy-done.3
  164.6 0.0 copy-done.4
  164.6 2.7 multiply_convert_fusion
  167.2 0.0 all-gather.8.cloned.1.call-update
  167.2 0.0 all-gather.10.cloned.1.call-start
  167.3 0.5 all-gather.10.cloned.1.call-update
  167.8 0.0 reduce-scatter.5.cloned.1.call-start
  167.9 49.3 %all-gather.8.cloned.1.call-done = bf16[1024,3584]{1,0:T(8,128)(2,1)} async-done(((bf16[64,3584]{1,0:T(8,128)(2,1)}), bf16[1024,3584]{1,0:T(8,128)(2,1)}) %all-gather.8.cloned.1.call-update) | async-done | bytes 7340048 | tf_op jit(solution)/shard_map/all_gather | solution.py:40
  217.1 9.4 %fusion.21 = f32[1024,512]{1,0:T(8,128)} fusion(bf16[1024,3584]{1,0:T(8,128)(2,1)} %all-gather.8.cloned.1.call-done, bf16[512,3584]{1,0:T(8,128)(2,1)} %param.13), kind=kOutput, calls=%fused_computation.35 | convolution fusion | flops 3758096384 | bytes 13107200 | tf_op jit(solution)/shard_map/tf,df->td/dot_general | solution.py:43
  226.6 40.7 %all-gather.10.cloned.1.call-done = bf16[1024,3584]{1,0:T(8,128)(2,1)} async-done(((bf16[64,3584]{1,0:T(8,128)(2,1)}), bf16[1024,3584]{1,0:T(8,128)(2,1)}) %all-gather.10.cloned.1.call-update) | async-done | bytes 7340048 | tf_op jit(solution)/shard_map/all_gather | solution.py:41
  267.3 10.1 %convolution_add_fusion = f32[1024,512]{1,0:T(8,128)} fusion(f32[1024,512]{1,0:T(8,128)} %fusion.21, bf16[1024,3584]{1,0:T(8,128)(2,1)} %all-gather.10.cloned.1.call-done, bf16[512,3584]{1,0:T(8,128)(2,1)} %param.14), kind=kOutput, calls=%fused_computation.3 | convolution fusion | flops 3758620672 | bytes 15204352 | tf_op jit(solution)/shard_map/tf,df->td/dot_general | solution.py:44
  277.4 0.0 reduce-scatter.5.cloned.1.call-update
  277.4 0.0 all-gather.14.cloned.1.call-start
  277.5 0.5 all-gather.14.cloned.1.call-update
  278.0 0.0 copy-done
  278.0 0.2 fusion.19
  278.2 75.0 %reduce-scatter.5.cloned.1.call-done = f32[128,512]{1,0:T(8,128)} async-done(((f32[1024,512]{1,0:T(8,128)}), f32[128,512]{1,0:T(8,128)}) %reduce-scatter.5.cloned.1.call-update) | async-done | bytes 262160 | tf_op jit(solution)/shard_map/reduce_scatter | solution.py:50
  353.2 6.5 %all-to-all-start.1 = ((f32[16,8,512]{2,1,0:T(8,128)}), f32[16,8,512]{2,1,0:T(8,128)S(1)}, u32[]{:S(2)}, u32[]{:S(2)}) async-start(f32[16,8,512]{2,1,0:T(8,128)} %bitcast.29), calls=%async_computation.3 | async-start | bytes 524288 | tf_op jit(solution)/shard_map/all_to_all | solution.py:51
  359.7 0.0 copy-start.2
  359.7 43.6 %all-gather.14.cloned.1.call-done = bf16[1024,3584]{1,0:T(8,128)(2,1)} async-done(((bf16[64,3584]{1,0:T(8,128)(2,1)}), bf16[1024,3584]{1,0:T(8,128)(2,1)}) %all-gather.14.cloned.1.call-update) | async-done | bytes 7340048 | tf_op jit(solution)/shard_map/all_gather | solution.py:42
  403.3 0.0 copy-done.6
  403.3 8.6 %convolution_convert_fusion = bf16[3584,512]{1,0:T(8,128)(2,1)} fusion(bf16[1024,3584]{1,0:T(8,128)(2,1)} %all-gather.14.cloned.1.call-done, bf16[1024,512]{1,0:T(8,128)(2,1)S(1)} %copy-done.6), kind=kOutput, calls=%fused_computation | convolution fusion | flops 3759931392 | bytes 12058624 | tf_op jit(solution)/shard_map/tf,td->fd/dot_general | solution.py:49
  411.9 0.0 all-to-all-done.1
  411.9 0.0 copy-done.5
  411.9 0.9 fusion.17
  412.8 4.9 all-to-all-start.2
  417.7 0.0 all-gather.12.cloned.1.call-start
  417.7 52.2 %psum.14 = f32[8192]{0:T(1024)S(1)} all-reduce(f32[8192]{0:T(1024)S(1)} %get-tuple-element.5), channel_id=1, replica_groups=mesh['row'=8,'col'=16] {'col'}, use_global_device_ids=true, to_apply=%region_5.0 | all-reduce | flops 8192 | bytes 65536 | tf_op jit(solution)/shard_map/psum | solution.py:53
  469.9 0.0 all-to-all-done.2
  469.9 0.7 copy-done.1
  470.6 0.0 all-gather.12.cloned.1.call-update
  470.6 35.0 %psum.15 = f32[8192]{0:T(1024)} all-reduce(f32[8192]{0:T(1024)S(1)} %psum.14), channel_id=1, replica_groups=mesh['row'=8,'col'=16] {'row'}, use_global_device_ids=true, to_apply=%region_6.0 | all-reduce | flops 8192 | bytes 65536 | tf_op jit(solution)/shard_map/psum | solution.py:53
  505.6 0.0 copy-done.2
  505.6 0.8 fusion.16
  506.4 12.2 %all-gather.12.cloned.1.call-done = bf16[1024,512]{1,0:T(8,128)(2,1)} async-done(((bf16[128,512]{1,0:T(8,128)(2,1)}), bf16[1024,512]{1,0:T(8,128)(2,1)}) %all-gather.12.cloned.1.call-update) | async-done | bytes 1048592 | tf_op jit(solution)/shard_map/all_gather | solution.py:32
  518.6 9.3 %convolution_convert_fusion.2 = bf16[512,3584]{1,0:T(8,128)(2,1)} fusion(bf16[1024,512]{1,0:T(8,128)(2,1)} %all-gather.12.cloned.1.call-done, bf16[1024,3584]{1,0:T(8,128)(2,1)} %all-gather.8.cloned.1.call-done), kind=kOutput, calls=%fused_computation.2 | convolution fusion | flops 3759931392 | bytes 12058624 | tf_op jit(solution)/shard_map/td,tf->df/dot_general | solution.py:47
  527.9 0.0 copy-done.7
  527.9 8.5 %convolution_convert_fusion.1 = bf16[512,3584]{1,0:T(8,128)(2,1)} fusion(bf16[1024,512]{1,0:T(8,128)(2,1)S(1)} %copy-done.7, bf16[1024,3584]{1,0:T(8,128)(2,1)} %all-gather.10.cloned.1.call-done), kind=kOutput, calls=%fused_computation.1 | convolution fusion | flops 3759931392 | bytes 12058624 | tf_op jit(solution)/shard_map/td,tf->df/dot_general | solution.py:48
  (8 shorter events, 0.0 us)
Async XLA Ops:
  7.2 59.0 %all-gather.6.cloned.1.call-start = ((), (), s32[]{:S(2)}) async-start(), calls=%async_computation.5 | async-start | bytes 1179648 | tf_op jit(solution)/shard_map/all_gather | solution.py:33
  20.7 143.8 %reduce-scatter.3.cloned.1.call-start = ((), (), s32[]{:S(2)}) async-start(), calls=%async_computation.6 | async-start | bytes 15597568 | tf_op jit(solution)/shard_map/reduce_scatter | solution.py:38
  77.7 86.8 %copy-start.3 = (bf16[64,3584]{1,0:T(8,128)(2,1)S(1)}, bf16[64,3584]{1,0:T(8,128)(2,1)}, u32[]{:S(2)}) copy-start(bf16[64,3584]{1,0:T(8,128)(2,1)} %param.11) | copy-start | bytes 1376260
  77.7 86.8 %copy-start.4 = (bf16[64,3584]{1,0:T(8,128)(2,1)S(1)}, bf16[64,3584]{1,0:T(8,128)(2,1)}, u32[]{:S(2)}) copy-start(bf16[64,3584]{1,0:T(8,128)(2,1)} %param.12) | copy-start | bytes 1376260
  77.8 139.4 %all-gather.8.cloned.1.call-start = ((), (), s32[]{:S(2)}) async-start(), calls=%async_computation.7 | async-start | bytes 7798784 | tf_op jit(solution)/shard_map/all_gather | solution.py:40
  167.2 100.1 %all-gather.10.cloned.1.call-start = ((), (), s32[]{:S(2)}) async-start(), calls=%async_computation.8 | async-start | bytes 7798784 | tf_op jit(solution)/shard_map/all_gather | solution.py:41
  167.8 185.4 %reduce-scatter.5.cloned.1.call-start = ((), (), s32[]{:S(2)}) async-start(), calls=%async_computation.9 | async-start | bytes 2359296 | tf_op jit(solution)/shard_map/reduce_scatter | solution.py:50
  226.6 51.4 %copy-start = (bf16[8,8192]{1,0:T(8,128)(2,1)S(1)}, bf16[8,8192]{1,0:T(8,128)(2,1)}, u32[]{:S(2)}) copy-start(bf16[8,8192]{1,0:T(8,128)(2,1)} %param.8) | copy-start | bytes 393220
  226.6 176.8 %copy-start.6 = (bf16[1024,512]{1,0:T(8,128)(2,1)S(1)}, bf16[1024,512]{1,0:T(8,128)(2,1)}, u32[]{:S(2)}) copy-start(bf16[1024,512]{1,0:T(8,128)(2,1)} %all-gather.6.cloned.1.call-done) | copy-start | bytes 3145732
  277.4 125.9 %all-gather.14.cloned.1.call-start = ((), (), s32[]{:S(2)}) async-start(), calls=%async_computation.11 | async-start | bytes 7798784 | tf_op jit(solution)/shard_map/all_gather | solution.py:42
  353.2 58.7 %all-to-all-start.1 = ((f32[16,8,512]{2,1,0:T(8,128)}), f32[16,8,512]{2,1,0:T(8,128)S(1)}, u32[]{:S(2)}, u32[]{:S(2)}) async-start(f32[16,8,512]{2,1,0:T(8,128)} %bitcast.29), calls=%async_computation.3 | async-start | bytes 524288 | tf_op jit(solution)/shard_map/all_to_all | solution.py:51
  359.7 52.2 %copy-start.5 = (f32[8192]{0:T(1024)S(1)}, f32[8192]{0:T(1024)}, u32[]{:S(2)}) copy-start(f32[8192]{0:T(1024)} %param.9) | copy-start | bytes 98308
  359.7 145.9 %copy-start.2 = (bf16[8,8192]{1,0:T(8,128)(2,1)S(1)}, bf16[8,8192]{1,0:T(8,128)(2,1)}, u32[]{:S(2)}) copy-start(bf16[8,8192]{1,0:T(8,128)(2,1)} %param.10) | copy-start | bytes 393220
  412.8 57.1 %all-to-all-start.2 = ((bf16[8,16,512]{2,0,1:T(8,128)(2,1)}), bf16[8,16,512]{2,0,1:T(8,128)(2,1)S(1)}, u32[]{:S(2)}, u32[]{:S(2)}) async-start(bf16[8,16,512]{2,0,1:T(8,128)(2,1)} %bitcast.7), calls=%async_computation.4 | async-start | bytes 262144 | tf_op jit(solution)/shard_map/all_to_all | solution.py:28
  417.7 100.9 %all-gather.12.cloned.1.call-start = ((), (), s32[]{:S(2)}) async-start(), calls=%async_computation.10 | async-start | bytes 1179648 | tf_op jit(solution)/shard_map/all_gather | solution.py:32
  469.9 0.7 copy-start.1
  518.6 9.3 %copy-start.7 = (bf16[1024,512]{1,0:T(8,128)(2,1)S(1)}, bf16[1024,512]{1,0:T(8,128)(2,1)}, u32[]{:S(2)}) copy-start(bf16[1024,512]{1,0:T(8,128)(2,1)} %all-gather.12.cloned.1.call-done) | copy-start | bytes 3145732
Sparse Core Ops, SparseCore 0:
  20.8 45.2 all-gather.5
  77.9 86.6 reduce-scatter.2
  167.4 49.7 all-gather.7
  219.3 47.9 all-gather.9
  277.5 75.6 reduce-scatter.4
  355.4 47.9 all-gather.13
  470.7 47.8 all-gather.11

commit v2 on v1

--- a/solution.py
+++ b/solution.py
@@ -19,19 +19,24 @@
     return (hidden, gate_grad, up_grad)
 
 
+def row_gather(x):
+    rows = lax.axis_size("row")
+    copies = jnp.broadcast_to(x[None], (rows,) + x.shape)
+    got = lax.all_to_all(copies, "row", split_axis=0, concat_axis=0, tiled=True)
+    return got.reshape((rows * x.shape[0],) + x.shape[1:])
+
+
 def local(tokens, gain, grad_out, pre_gate, pre_up, gate_weight, up_weight, down_weight):
+    cols = lax.axis_size("col")
+    rows = lax.axis_size("row")
     tokens_wide = tokens.astype(jnp.float32)
     inverse_rms = lax.rsqrt(jnp.mean(tokens_wide * tokens_wide, axis=1, keepdims=True) + epsilon)
     normed = tokens_wide * inverse_rms
-    scaled = (normed * gain).astype(jnp.bfloat16)
-    grid_input, grid_grad = (
-        lax.all_to_all(scaled, "col", split_axis=1, concat_axis=0, tiled=True),
-        lax.all_to_all(grad_out, "col", split_axis=1, concat_axis=0, tiled=True),
-    )
-    all_input, all_grad = (
-        lax.all_gather(grid_input, "row", axis=0, tiled=True),
-        lax.all_gather(grid_grad, "row", axis=0, tiled=True),
-    )
+    tile = gate_weight.shape[0]
+    gain_tile = lax.dynamic_slice_in_dim(gain, lax.axis_index("col") * tile, tile)
+    grid_normed = lax.all_to_all(normed, "col", split_axis=1, concat_axis=0, tiled=True)
+    grid_grad = lax.all_to_all(grad_out, "col", split_axis=1, concat_axis=0, tiled=True)
+    all_grad = row_gather(grid_grad)
     partial_grad = jnp.einsum(
         "td,fd->tf", all_grad, down_weight, preferred_element_type=jnp.float32
     )
@@ -40,17 +45,32 @@
     gate_piece = lax.all_gather(gate_block, "col", axis=0, tiled=True)
     up_piece = lax.all_gather(up_block, "col", axis=0, tiled=True)
     hidden_piece = lax.all_gather(hidden_block, "col", axis=0, tiled=True)
+    all_normed = row_gather(grid_normed)
+    all_input = (all_normed * gain_tile).astype(jnp.bfloat16)
     new_rows = jnp.einsum("tf,df->td", gate_piece, gate_weight, preferred_element_type=jnp.float32)
     new_rows = new_rows + jnp.einsum(
         "tf,df->td", up_piece, up_weight, preferred_element_type=jnp.float32
     )
+    gain_part = jnp.sum(new_rows * all_normed, axis=0)
+    tokens_all = new_rows.shape[0]
+    blocks = new_rows.reshape(rows, tokens_all // rows, tile)
+    extra = jnp.zeros((rows, 8, tile), jnp.float32).at[:, 0, :].set(gain_part)
+    sent = jnp.concatenate([blocks, extra], axis=1)
+    got = lax.all_to_all(sent, "row", split_axis=0, concat_axis=0, tiled=True)
+    summed = jnp.sum(got, axis=0)
+    grid_back = summed[: tokens_all // rows]
+    gain_tile_grad = summed[tokens_all // rows]
+    per_col = grid_back.reshape(cols, -1, tile)
+    mine = per_col.shape[1]
+    sent2 = jnp.concatenate(
+        [per_col, jnp.broadcast_to(gain_tile_grad[None, None, :], (cols, 1, tile))], axis=1
+    )
+    got2 = lax.all_to_all(sent2, "col", split_axis=0, concat_axis=0, tiled=True)
+    normed_grad = got2[:, :mine, :].transpose(1, 0, 2).reshape(mine, cols * tile)
+    grad_gain = got2[:, mine, :].reshape(cols * tile)
     gate_total = jnp.einsum("td,tf->df", all_input, gate_piece, preferred_element_type=jnp.float32)
     up_total = jnp.einsum("td,tf->df", all_input, up_piece, preferred_element_type=jnp.float32)
     down_total = jnp.einsum("tf,td->fd", hidden_piece, all_grad, preferred_element_type=jnp.float32)
-    grid_back = lax.psum_scatter(new_rows, "row", scatter_dimension=0, tiled=True)
-    normed_grad = lax.all_to_all(grid_back, "col", split_axis=0, concat_axis=1, tiled=True)
-    gain_terms = jnp.sum(normed_grad * normed, axis=0)
-    grad_gain = lax.psum(lax.psum(gain_terms, "col"), "row")
     scaled_grad = normed_grad * gain
     inner = jnp.mean(scaled_grad * normed, axis=1, keepdims=True)
     grad_tokens = (

time: 545 us -> 360 us (0.66)
  waiting for transfers between devices: 354 us -> 213 us
  blocking collectives: 101 us -> 50.2 us
  starting transfers between devices: 11.6 us -> 17.7 us
    psum x2 -> x0, blocking collectives: 87.2 us -> none  [local(): grad_gain = lax.psum(lax.psum(gain_terms, 'col'), 'row')]
    reduce_scatter x1 -> x0, waiting for transfers between devices: 75 us -> none  [local(): lax.psum_scatter(new_rows, 'row', scatter_dimension=0, tiled=True)]
    all_gather x2 -> x0, waiting for transfers between devices: 57.6 us -> none  [the longest x1 45.4 us: local(): lax.all_gather(grid_grad, 'row', axis=0, tiled=True)]
    all_to_all x0 -> x2, blocking collectives: none -> 36.8 us  [the longest x1 23.2 us: row_gather(): got = lax.all_to_all(copies, 'row', split_axis=0, concat_axis=0, tiled=True)]
    all_gather x1, waiting for transfers between devices: 43.6 us -> 21.8 us  [local(): hidden_piece = lax.all_gather(hidden_block, 'col', axis=0, tiled=True)]
    all_to_all x2 -> x3, waiting for transfers between devices: 0.01 us -> 16.9 us  [the longest x1 16.9 us: local(): got = lax.all_to_all(sent, 'row', split_axis=0, concat_axis=0, tiled=True)]
    all_to_all x2 -> x3, starting transfers between devices: 11.3 us -> 17.6 us  [the longest x1 6.42 us: local(): got = lax.all_to_all(sent, 'row', split_axis=0, concat_axis=0, tiled=True)]
  transfers between devices with their start and end apart: 9 -> 7, of which waited for: 7 -> 5; matrix products, arithmetic and copies ran while one was open for 3% -> 14% of each run, Pallas kernels for 0% -> 0%
where the time goes in v2:
time: 360 us; the launch traced here: 359 us
  waiting for transfers between devices  213 us (59%)
  matrix products  54 us (15%)
  blocking collectives  50.2 us (14%)
  starting transfers between devices  17.7 us (5%)
  between operations  13.9 us (4%)
  other arithmetic  6.71 us (2%)
    reduce_scatter x1, waiting for transfers between devices, local(): lax.psum_scatter(partial_grad, 'col', scatter_dimension=0, tiled=True)  83 us
    all_gather x1, waiting for transfers between devices, local(): gate_piece = lax.all_gather(gate_block, 'col', axis=0, tiled=True)  50.5 us
    all_gather x1, waiting for transfers between devices, local(): up_piece = lax.all_gather(up_block, 'col', axis=0, tiled=True)  39.5 us
    all_to_all x1, blocking collectives, row_gather(): got = lax.all_to_all(copies, 'row', split_axis=0, concat_axis=0, tiled=True)  23.2 us
    all_gather x1, waiting for transfers between devices, local(): hidden_piece = lax.all_gather(hidden_block, 'col', axis=0, tiled=True)  21.8 us
    all_to_all x1, waiting for transfers between devices, local(): got = lax.all_to_all(sent, 'row', split_axis=0, concat_axis=0, tiled=True)  16.9 us
    all_to_all x1, blocking collectives, local(): lax.all_to_all(normed, 'col', split_axis=1, concat_axis=0, tiled=True)  13.7 us
    all_to_all x1, blocking collectives, local(): lax.all_to_all(grad_out, 'col', split_axis=1, concat_axis=0, tiled=True)  13.4 us
  transfers between devices with their start and end apart: 7, of which 5 were waited for; matrix products, arithmetic and copies ran while one was open for 14% of the time, Pallas kernels for 0%

profile of v2, /device:TPU:1, one launch (start us, length us, event | category | flops | bytes accessed | tf_op | source)
XLA Modules:
  0.0 359.0 jit_solution(729511443567385319)
XLA Ops:
  7.2 0.0 reduce-scatter.2.cloned.1.call-start
  7.2 13.4 %all_to_all.52 = bf16[8,16,512]{2,0,1:T(8,128)(2,1)S(1)} all-to-all(bf16[8,16,512]{2,0,1:T(8,128)(2,1)} %bitcast.44), channel_id=1, replica_groups=mesh['row'=8,'col'=16] {'col'}, dimensions={1} | all-to-all | bytes 262144 | tf_op jit(solution)/shard_map/all_to_all | solution.py:38
  20.6 0.1 broadcast_in_dim.13
  20.7 23.2 %all_to_all.53 = bf16[8,128,512]{2,1,0:T(8,128)(2,1)S(1)} all-to-all(bf16[8,128,512]{2,1,0:T(8,128)(2,1)S(1)} %broadcast_in_dim.13), channel_id=1, replica_groups=mesh['row'=8,'col'=16] {'row'}, dimensions={0} | all-to-all | bytes 2097152 | tf_op jit(solution)/shard_map/all_to_all | solution.py:25
  43.8 0.0 copy-start.1
  43.8 1.0 copy-done.1
  44.8 9.4 %fusion.11 = f32[1024,3584]{1,0:T(8,128)} fusion(bf16[1024,512]{1,0:T(8,128)(2,1)S(1)} %bitcast.40, bf16[3584,512]{1,0:T(8,128)(2,1)} %param.17), kind=kOutput, calls=%fused_computation.33 | convolution fusion | flops 3758096384 | bytes 19398656 | tf_op jit(solution)/shard_map/td,fd->tf/dot_general | solution.py:40
  54.2 0.0 copy-start.3
  54.2 0.0 reduce-scatter.2.cloned.1.call-update
  54.2 0.0 copy-start
  54.3 0.0 all-gather.4.cloned.1.call-start
  54.3 83.0 %reduce-scatter.2.cloned.1.call-done = f32[64,3584]{1,0:T(8,128)} async-done(((f32[1024,3584]{1,0:T(8,128)}), f32[64,3584]{1,0:T(8,128)}) %reduce-scatter.2.cloned.1.call-update) | async-done | bytes 917520 | tf_op jit(solution)/shard_map/reduce_scatter | solution.py:43
  137.3 0.0 copy-done.3
  137.3 0.0 copy-done.4
  137.3 2.7 multiply_convert_fusion
  140.0 0.0 all-gather.4.cloned.1.call-update
  140.1 0.0 all-gather.6.cloned.1.call-start
  140.1 0.7 all-gather.6.cloned.1.call-update
  140.8 0.0 all-gather.8.cloned.1.call-start
  140.8 0.5 all-gather.8.cloned.1.call-update
  141.4 0.0 copy-done
  141.4 0.2 fusion.10
  141.6 0.1 convert_multiply_fusion.4
  141.7 13.7 %all_to_all.54 = f32[8,16,512]{2,0,1:T(8,128)S(1)} all-to-all(f32[8,16,512]{2,0,1:T(8,128)S(1)} %bitcast.42), channel_id=1, replica_groups=mesh['row'=8,'col'=16] {'col'}, dimensions={1} | all-to-all | bytes 524288 | tf_op jit(solution)/shard_map/all_to_all | solution.py:37
  155.3 1.6 broadcast_in_dim.15
  156.9 6.1 %all-to-all-start.3 = ((f32[8,128,512]{2,1,0:T(8,128)}), f32[8,128,512]{2,1,0:T(8,128)S(1)}, u32[]{:S(2)}, u32[]{:S(2)}) async-start(f32[8,128,512]{2,1,0:T(8,128)} %broadcast_in_dim.15), calls=%async_computation.4 | async-start | bytes 4194304 | tf_op jit(solution)/shard_map/all_to_all | solution.py:25
  163.0 0.0 copy-done.5
  163.0 0.1 dynamic_slice.3
  163.1 50.5 %all-gather.4.cloned.1.call-done = bf16[1024,3584]{1,0:T(8,128)(2,1)} async-done(((bf16[64,3584]{1,0:T(8,128)(2,1)}), bf16[1024,3584]{1,0:T(8,128)(2,1)}) %all-gather.4.cloned.1.call-update) | async-done | bytes 7340048 | tf_op jit(solution)/shard_map/all_gather | solution.py:45
  213.5 9.4 %fusion.12 = f32[1024,512]{1,0:T(8,128)} fusion(bf16[1024,3584]{1,0:T(8,128)(2,1)} %all-gather.4.cloned.1.call-done, bf16[512,3584]{1,0:T(8,128)(2,1)} %param.15), kind=kOutput, calls=%fused_computation.34 | convolution fusion | flops 3758096384 | bytes 13107200 | tf_op jit(solution)/shard_map/tf,df->td/dot_general | solution.py:50
  223.0 0.0 all-to-all-done.3
  223.0 39.5 %all-gather.6.cloned.1.call-done = bf16[1024,3584]{1,0:T(8,128)(2,1)} async-done(((bf16[64,3584]{1,0:T(8,128)(2,1)}), bf16[1024,3584]{1,0:T(8,128)(2,1)}) %all-gather.6.cloned.1.call-update) | async-done | bytes 7340048 | tf_op jit(solution)/shard_map/all_gather | solution.py:46
  262.5 8.9 %fusion.1 = (bf16[1024,512]{1,0:T(8,128)(2,1)S(1)}, f32[512]{0:T(512)S(1)}, f32[1024,512]{1,0:T(8,128)S(1)}) fusion(f32[8,128,512]{2,1,0:T(8,128)S(1)} %all-to-all-done.3, f32[512]{0:T(512)S(1)} %dynamic_slice.3, f32[1024,512]{1,0:T(8,128)} %fusion.12, bf16[1024,3584]{1,0:T(8,128)(2,1)} %all-gather.6.cloned.1.call-done, bf16[512,3584]{1,0:T(8,128)(2,1)} %param.16), kind=kOutput, calls=%fused_computation.8 | convolution fusion | flops 3760717312 | bytes 18354176 | tf_op jit(solution)/shard_map/tf,df->td/dot_general | solution.py:51
  271.4 1.6 select_maximum_fusion
  273.0 6.4 %all-to-all-start.4 = ((f32[8,136,512]{2,1,0:T(8,128)}), f32[8,136,512]{2,1,0:T(8,128)S(1)}, u32[]{:S(2)}, u32[]{:S(2)}) async-start(f32[8,136,512]{2,1,0:T(8,128)} %select_maximum_fusion), calls=%async_computation.5 | async-start | bytes 4456448 | tf_op jit(solution)/shard_map/all_to_all | solution.py:59
  279.4 8.7 %convolution_convert_fusion.2 = bf16[512,3584]{1,0:T(8,128)(2,1)} fusion(bf16[1024,512]{1,0:T(8,128)(2,1)S(1)} %get-tuple-element.17, bf16[1024,3584]{1,0:T(8,128)(2,1)} %all-gather.4.cloned.1.call-done), kind=kOutput, calls=%fused_computation.2 | convolution fusion | flops 3759931392 | bytes 12058624 | tf_op jit(solution)/shard_map/td,tf->df/dot_general | solution.py:71
  288.1 8.5 %convolution_convert_fusion.1 = bf16[512,3584]{1,0:T(8,128)(2,1)} fusion(bf16[1024,512]{1,0:T(8,128)(2,1)S(1)} %get-tuple-element.17, bf16[1024,3584]{1,0:T(8,128)(2,1)} %all-gather.6.cloned.1.call-done), kind=kOutput, calls=%fused_computation.1 | convolution fusion | flops 3759931392 | bytes 12058624 | tf_op jit(solution)/shard_map/td,tf->df/dot_general | solution.py:72
  296.6 16.9 %all-to-all-done.4 = f32[8,136,512]{2,1,0:T(8,128)S(1)} async-done(((f32[8,136,512]{2,1,0:T(8,128)}), f32[8,136,512]{2,1,0:T(8,128)S(1)}, u32[]{:S(2)}, u32[]{:S(2)}) %all-to-all-start.4) | async-done | bytes 2228256 | tf_op jit(solution)/shard_map/all_to_all | solution.py:59
  313.5 0.2 reduce_sum.38
  313.8 0.9 pad_maximum_fusion
  314.6 5.1 %all-to-all-start.5 = ((f32[16,9,512]{2,1,0:T(8,128)}), f32[16,9,512]{2,1,0:T(8,128)S(1)}, u32[]{:S(2)}, u32[]{:S(2)}) async-start(f32[16,9,512]{2,1,0:T(8,128)} %pad_maximum_fusion), calls=%async_computation.6 | async-start | bytes 1048576 | tf_op jit(solution)/shard_map/all_to_all | solution.py:68
  319.7 21.8 %all-gather.8.cloned.1.call-done = bf16[1024,3584]{1,0:T(8,128)(2,1)} async-done(((bf16[64,3584]{1,0:T(8,128)(2,1)}), bf16[1024,3584]{1,0:T(8,128)(2,1)}) %all-gather.8.cloned.1.call-update) | async-done | bytes 7340048 | tf_op jit(solution)/shard_map/all_gather | solution.py:47
  341.6 9.2 %convolution_convert_fusion = bf16[3584,512]{1,0:T(8,128)(2,1)} fusion(bf16[1024,3584]{1,0:T(8,128)(2,1)} %all-gather.8.cloned.1.call-done, bf16[1024,512]{1,0:T(8,128)(2,1)} %bitcast.41), kind=kOutput, calls=%fused_computation | convolution fusion | flops 3759931392 | bytes 12058624 | tf_op jit(solution)/shard_map/tf,td->fd/dot_general | solution.py:73
  350.7 0.0 all-to-all-done.5
  350.7 0.3 multiply_reduce_fusion
  351.0 0.0 copy-done.2
  351.0 0.8 add_convert_fusion
  351.8 0.6 slice.38
  (10 shorter events, 0.1 us)
Async XLA Ops:
  7.2 130.2 %reduce-scatter.2.cloned.1.call-start = ((), (), s32[]{:S(2)}) async-start(), calls=%async_computation.7 | async-start | bytes 15597568 | tf_op jit(solution)/shard_map/reduce_scatter | solution.py:43
  43.8 1.0 copy-start.1
  54.2 83.1 %copy-start.3 = (bf16[64,3584]{1,0:T(8,128)(2,1)S(1)}, bf16[64,3584]{1,0:T(8,128)(2,1)}, u32[]{:S(2)}) copy-start(bf16[64,3584]{1,0:T(8,128)(2,1)} %param.13) | copy-start | bytes 1376260
  54.2 83.1 %copy-start.4 = (bf16[64,3584]{1,0:T(8,128)(2,1)S(1)}, bf16[64,3584]{1,0:T(8,128)(2,1)}, u32[]{:S(2)}) copy-start(bf16[64,3584]{1,0:T(8,128)(2,1)} %param.14) | copy-start | bytes 1376260
  54.2 87.1 %copy-start = (bf16[8,8192]{1,0:T(8,128)(2,1)S(1)}, bf16[8,8192]{1,0:T(8,128)(2,1)}, u32[]{:S(2)}) copy-start(bf16[8,8192]{1,0:T(8,128)(2,1)} %param.10) | copy-start | bytes 393220
  54.3 159.3 %all-gather.4.cloned.1.call-start = ((), (), s32[]{:S(2)}) async-start(), calls=%async_computation.8 | async-start | bytes 7798784 | tf_op jit(solution)/shard_map/all_gather | solution.py:45
  140.1 122.4 %all-gather.6.cloned.1.call-start = ((), (), s32[]{:S(2)}) async-start(), calls=%async_computation.9 | async-start | bytes 7798784 | tf_op jit(solution)/shard_map/all_gather | solution.py:46
  140.8 200.8 %all-gather.8.cloned.1.call-start = ((), (), s32[]{:S(2)}) async-start(), calls=%async_computation.10 | async-start | bytes 7798784 | tf_op jit(solution)/shard_map/all_gather | solution.py:47
  141.6 21.4 %copy-start.5 = (f32[8192]{0:T(1024)S(1)}, f32[8192]{0:T(1024)}, u32[]{:S(2)}) copy-start(f32[8192]{0:T(1024)} %param.11) | copy-start | bytes 98308
  156.9 66.0 %all-to-all-start.3 = ((f32[8,128,512]{2,1,0:T(8,128)}), f32[8,128,512]{2,1,0:T(8,128)S(1)}, u32[]{:S(2)}, u32[]{:S(2)}) async-start(f32[8,128,512]{2,1,0:T(8,128)} %broadcast_in_dim.15), calls=%async_computation.4 | async-start | bytes 4194304 | tf_op jit(solution)/shard_map/all_to_all | solution.py:25
  273.0 40.5 %all-to-all-start.4 = ((f32[8,136,512]{2,1,0:T(8,128)}), f32[8,136,512]{2,1,0:T(8,128)S(1)}, u32[]{:S(2)}, u32[]{:S(2)}) async-start(f32[8,136,512]{2,1,0:T(8,128)} %select_maximum_fusion), calls=%async_computation.5 | async-start | bytes 4456448 | tf_op jit(solution)/shard_map/all_to_all | solution.py:59
  314.6 36.1 %all-to-all-start.5 = ((f32[16,9,512]{2,1,0:T(8,128)}), f32[16,9,512]{2,1,0:T(8,128)S(1)}, u32[]{:S(2)}, u32[]{:S(2)}) async-start(f32[16,9,512]{2,1,0:T(8,128)} %pad_maximum_fusion), calls=%async_computation.6 | async-start | bytes 1048576 | tf_op jit(solution)/shard_map/all_to_all | solution.py:68
  319.7 31.3 %copy-start.2 = (bf16[8,8192]{1,0:T(8,128)(2,1)S(1)}, bf16[8,8192]{1,0:T(8,128)(2,1)}, u32[]{:S(2)}) copy-start(bf16[8,8192]{1,0:T(8,128)(2,1)} %param.12) | copy-start | bytes 393220
Sparse Core Ops, SparseCore 0:
  54.4 82.9 reduce-scatter.1
  140.2 73.3 all-gather.3
  215.8 46.6 all-gather.5
  264.0 77.4 all-gather.7

commit v3 on v2

--- a/solution.py
+++ b/solution.py
@@ -40,7 +40,9 @@
     partial_grad = jnp.einsum(
         "td,fd->tf", all_grad, down_weight, preferred_element_type=jnp.float32
     )
-    block_grad = lax.psum_scatter(partial_grad, "col", scatter_dimension=0, tiled=True)
+    terms = partial_grad.astype(jnp.bfloat16).reshape(cols, -1, partial_grad.shape[1])
+    terms = lax.all_to_all(terms, "col", split_axis=0, concat_axis=0, tiled=True)
+    block_grad = jnp.sum(terms.astype(jnp.float32), axis=0)
     hidden_block, gate_block, up_block = swiglu_grads(block_grad, pre_gate, pre_up)
     gate_piece = lax.all_gather(gate_block, "col", axis=0, tiled=True)
     up_piece = lax.all_gather(up_block, "col", axis=0, tiled=True)

time: 360 us -> 354 us (0.983)
  blocking collectives: 50.2 us -> 137 us
  waiting for transfers between devices: 213 us -> 127 us
    all_to_all x0 -> x1, blocking collectives: none -> 87 us  [local(): lax.all_to_all(terms, 'col', split_axis=0, concat_axis=0, tiled=True)]
    reduce_scatter x1 -> x0, waiting for transfers between devices: 83 us -> none  [local(): lax.psum_scatter(partial_grad, 'col', scatter_dimension=0, tiled=True)]
  transfers between devices with their start and end apart: 7 -> 6, of which waited for: 5 -> 4; matrix products, arithmetic and copies ran while one was open for 14% -> 14% of each run, Pallas kernels for 0% -> 0%
where the time goes in v3:
time: 354 us; the launch traced here: 353 us
  blocking collectives  137 us (39%)
  waiting for transfers between devices  127 us (36%)
  matrix products  51.5 us (15%)
  starting transfers between devices  15.2 us (4%)
  between operations  13.9 us (4%)
  other arithmetic  6.54 us (2%)
    all_to_all x1, blocking collectives, local(): lax.all_to_all(terms, 'col', split_axis=0, concat_axis=0, tiled=True)  87 us
    all_gather x1, waiting for transfers between devices, local(): gate_piece = lax.all_gather(gate_block, 'col', axis=0, tiled=True)  48.1 us
    all_gather x1, waiting for transfers between devices, local(): up_piece = lax.all_gather(up_block, 'col', axis=0, tiled=True)  38.3 us
    all_to_all x1, blocking collectives, row_gather(): got = lax.all_to_all(copies, 'row', split_axis=0, concat_axis=0, tiled=True)  23.2 us
    all_gather x1, waiting for transfers between devices, local(): hidden_piece = lax.all_gather(hidden_block, 'col', axis=0, tiled=True)  22 us
    all_to_all x1, waiting for transfers between devices, local(): got = lax.all_to_all(sent, 'row', split_axis=0, concat_axis=0, tiled=True)  16.9 us
    all_to_all x1, blocking collectives, local(): lax.all_to_all(grad_out, 'col', split_axis=1, concat_axis=0, tiled=True)  13.4 us
    all_to_all x1, blocking collectives, local(): lax.all_to_all(normed, 'col', split_axis=1, concat_axis=0, tiled=True)  13.3 us
  transfers between devices with their start and end apart: 6, of which 4 were waited for; matrix products, arithmetic and copies ran while one was open for 14% of the time, Pallas kernels for 0%

profile of v3, /device:TPU:1, one launch (start us, length us, event | category | flops | bytes accessed | tf_op | source)
XLA Modules:
  0.0 353.3 jit_solution(6410531516429825157)
XLA Ops:
  7.2 0.0 all-gather.4.cloned.1.call-start
  7.2 13.4 %all_to_all.57 = bf16[8,16,512]{2,0,1:T(8,128)(2,1)S(1)} all-to-all(bf16[8,16,512]{2,0,1:T(8,128)(2,1)} %bitcast.46), channel_id=1, replica_groups=mesh['row'=8,'col'=16] {'col'}, dimensions={1} | all-to-all | bytes 262144 | tf_op jit(solution)/shard_map/all_to_all | solution.py:38
  20.6 0.1 broadcast_in_dim.13
  20.7 23.2 %all_to_all.58 = bf16[8,128,512]{2,1,0:T(8,128)(2,1)S(1)} all-to-all(bf16[8,128,512]{2,1,0:T(8,128)(2,1)S(1)} %broadcast_in_dim.13), channel_id=1, replica_groups=mesh['row'=8,'col'=16] {'row'}, dimensions={0} | all-to-all | bytes 2097152 | tf_op jit(solution)/shard_map/all_to_all | solution.py:25
  43.8 0.0 copy-start.1
  43.8 6.8 %convolution_convert_fusion = bf16[1024,3584]{1,0:T(8,128)(2,1)S(1)} fusion(bf16[1024,512]{1,0:T(8,128)(2,1)S(1)} %bitcast.42, bf16[3584,512]{1,0:T(8,128)(2,1)} %param.17), kind=kOutput, calls=%fused_computation.1 | convolution fusion | flops 3761766400 | bytes 12058624 | tf_op jit(solution)/shard_map/td,fd->tf/dot_general | solution.py:40
  50.7 0.0 copy-done.1
  50.7 87.0 %all_to_all.59 = bf16[16,64,3584]{2,1,0:T(8,128)(2,1)S(1)} all-to-all(bf16[16,64,3584]{2,1,0:T(8,128)(2,1)S(1)} %bitcast.37), channel_id=1, replica_groups=mesh['row'=8,'col'=16] {'col'}, dimensions={0} | all-to-all | bytes 14680064 | tf_op jit(solution)/shard_map/all_to_all | solution.py:44
  137.7 0.0 copy-start.3
  137.7 0.0 copy-start.4
  137.7 1.0 convert_reduce_fusion
  138.7 0.0 copy-done.3
  138.7 0.1 copy-done.4
  138.8 0.0 copy-start
  138.8 1.5 multiply_convert_fusion
  140.3 0.0 all-gather.4.cloned.1.call-update
  140.4 0.0 all-gather.6.cloned.1.call-start
  140.4 0.7 all-gather.6.cloned.1.call-update
  141.1 0.0 all-gather.8.cloned.1.call-start
  141.2 0.7 all-gather.8.cloned.1.call-update
  141.9 0.0 copy-done
  141.9 0.2 fusion.10
  142.1 0.1 convert_multiply_fusion.4
  142.2 13.3 %all_to_all.60 = f32[8,16,512]{2,0,1:T(8,128)S(1)} all-to-all(f32[8,16,512]{2,0,1:T(8,128)S(1)} %bitcast.44), channel_id=1, replica_groups=mesh['row'=8,'col'=16] {'col'}, dimensions={1} | all-to-all | bytes 524288 | tf_op jit(solution)/shard_map/all_to_all | solution.py:37
  155.5 1.6 broadcast_in_dim.15
  157.1 3.6 %all-to-all-start.4 = ((f32[8,128,512]{2,1,0:T(8,128)}), f32[8,128,512]{2,1,0:T(8,128)S(1)}, u32[]{:S(2)}, u32[]{:S(2)}) async-start(f32[8,128,512]{2,1,0:T(8,128)} %broadcast_in_dim.15), calls=%async_computation.4 | async-start | bytes 4194304 | tf_op jit(solution)/shard_map/all_to_all | solution.py:25
  160.7 0.0 copy-done.5
  160.7 0.1 dynamic_slice.3
  160.8 48.1 %all-gather.4.cloned.1.call-done = bf16[1024,3584]{1,0:T(8,128)(2,1)} async-done(((bf16[64,3584]{1,0:T(8,128)(2,1)}), bf16[1024,3584]{1,0:T(8,128)(2,1)}) %all-gather.4.cloned.1.call-update) | async-done | bytes 7340048 | tf_op jit(solution)/shard_map/all_gather | solution.py:47
  208.9 9.4 %fusion.11 = f32[1024,512]{1,0:T(8,128)} fusion(bf16[1024,3584]{1,0:T(8,128)(2,1)} %all-gather.4.cloned.1.call-done, bf16[512,3584]{1,0:T(8,128)(2,1)} %param.15), kind=kOutput, calls=%fused_computation.35 | convolution fusion | flops 3758096384 | bytes 13107200 | tf_op jit(solution)/shard_map/tf,df->td/dot_general | solution.py:52
  218.3 0.0 all-to-all-done.4
  218.3 38.3 %all-gather.6.cloned.1.call-done = bf16[1024,3584]{1,0:T(8,128)(2,1)} async-done(((bf16[64,3584]{1,0:T(8,128)(2,1)}), bf16[1024,3584]{1,0:T(8,128)(2,1)}) %all-gather.6.cloned.1.call-update) | async-done | bytes 7340048 | tf_op jit(solution)/shard_map/all_gather | solution.py:48
  256.6 8.9 %fusion.1 = (bf16[1024,512]{1,0:T(8,128)(2,1)S(1)}, f32[512]{0:T(512)S(1)}, f32[1024,512]{1,0:T(8,128)S(1)}) fusion(f32[8,128,512]{2,1,0:T(8,128)S(1)} %all-to-all-done.4, f32[512]{0:T(512)S(1)} %dynamic_slice.3, f32[1024,512]{1,0:T(8,128)} %fusion.11, bf16[1024,3584]{1,0:T(8,128)(2,1)} %all-gather.6.cloned.1.call-done, bf16[512,3584]{1,0:T(8,128)(2,1)} %param.16), kind=kOutput, calls=%fused_computation.10 | convolution fusion | flops 3760717312 | bytes 18354176 | tf_op jit(solution)/shard_map/tf,df->td/dot_general | solution.py:53
  265.5 1.6 select_maximum_fusion
  267.1 6.4 %all-to-all-start.5 = ((f32[8,136,512]{2,1,0:T(8,128)}), f32[8,136,512]{2,1,0:T(8,128)S(1)}, u32[]{:S(2)}, u32[]{:S(2)}) async-start(f32[8,136,512]{2,1,0:T(8,128)} %select_maximum_fusion), calls=%async_computation.5 | async-start | bytes 4456448 | tf_op jit(solution)/shard_map/all_to_all | solution.py:61
  273.6 8.7 %convolution_convert_fusion.3 = bf16[512,3584]{1,0:T(8,128)(2,1)} fusion(bf16[1024,512]{1,0:T(8,128)(2,1)S(1)} %get-tuple-element.17, bf16[1024,3584]{1,0:T(8,128)(2,1)} %all-gather.4.cloned.1.call-done), kind=kOutput, calls=%fused_computation.4 | convolution fusion | flops 3759931392 | bytes 12058624 | tf_op jit(solution)/shard_map/td,tf->df/dot_general | solution.py:73
  282.3 8.5 %convolution_convert_fusion.2 = bf16[512,3584]{1,0:T(8,128)(2,1)} fusion(bf16[1024,512]{1,0:T(8,128)(2,1)S(1)} %get-tuple-element.17, bf16[1024,3584]{1,0:T(8,128)(2,1)} %all-gather.6.cloned.1.call-done), kind=kOutput, calls=%fused_computation.3 | convolution fusion | flops 3759931392 | bytes 12058624 | tf_op jit(solution)/shard_map/td,tf->df/dot_general | solution.py:74
  290.8 16.9 %all-to-all-done.5 = f32[8,136,512]{2,1,0:T(8,128)S(1)} async-done(((f32[8,136,512]{2,1,0:T(8,128)}), f32[8,136,512]{2,1,0:T(8,128)S(1)}, u32[]{:S(2)}, u32[]{:S(2)}) %all-to-all-start.5) | async-done | bytes 2228256 | tf_op jit(solution)/shard_map/all_to_all | solution.py:61
  307.7 0.2 reduce_sum.48
  308.0 0.8 pad_maximum_fusion
  308.8 5.1 %all-to-all-start.6 = ((f32[16,9,512]{2,1,0:T(8,128)}), f32[16,9,512]{2,1,0:T(8,128)S(1)}, u32[]{:S(2)}, u32[]{:S(2)}) async-start(f32[16,9,512]{2,1,0:T(8,128)} %pad_maximum_fusion), calls=%async_computation.6 | async-start | bytes 1048576 | tf_op jit(solution)/shard_map/all_to_all | solution.py:70
  313.9 22.0 %all-gather.8.cloned.1.call-done = bf16[1024,3584]{1,0:T(8,128)(2,1)} async-done(((bf16[64,3584]{1,0:T(8,128)(2,1)}), bf16[1024,3584]{1,0:T(8,128)(2,1)}) %all-gather.8.cloned.1.call-update) | async-done | bytes 7340048 | tf_op jit(solution)/shard_map/all_gather | solution.py:49
  335.9 9.2 %convolution_convert_fusion.1 = bf16[3584,512]{1,0:T(8,128)(2,1)} fusion(bf16[1024,3584]{1,0:T(8,128)(2,1)} %all-gather.8.cloned.1.call-done, bf16[1024,512]{1,0:T(8,128)(2,1)} %bitcast.43), kind=kOutput, calls=%fused_computation.2 | convolution fusion | flops 3759931392 | bytes 12058624 | tf_op jit(solution)/shard_map/tf,td->fd/dot_general | solution.py:75
  345.0 0.0 all-to-all-done.6
  345.1 0.3 multiply_reduce_fusion
  345.3 0.0 copy-done.2
  345.3 0.8 add_convert_fusion
  346.1 0.6 slice.38
  (9 shorter events, 0.1 us)
Async XLA Ops:
  7.2 201.7 %all-gather.4.cloned.1.call-start = ((), (), s32[]{:S(2)}) async-start(), calls=%async_computation.7 | async-start | bytes 7798784 | tf_op jit(solution)/shard_map/all_gather | solution.py:47
  43.8 6.9 %copy-start.1 = (bf16[8,128,512]{2,1,0:T(8,128)(2,1)}, bf16[8,128,512]{2,1,0:T(8,128)(2,1)S(1)}, u32[]{:S(2)}) copy-start(bf16[8,128,512]{2,1,0:T(8,128)(2,1)S(1)} %all_to_all.58) | copy-start | bytes 3145732
  137.7 1.0 copy-start.3
  137.7 1.2 copy-start.4
  138.8 3.0 copy-start
  140.4 116.3 %all-gather.6.cloned.1.call-start = ((), (), s32[]{:S(2)}) async-start(), calls=%async_computation.8 | async-start | bytes 7798784 | tf_op jit(solution)/shard_map/all_gather | solution.py:48
  141.1 194.8 %all-gather.8.cloned.1.call-start = ((), (), s32[]{:S(2)}) async-start(), calls=%async_computation.9 | async-start | bytes 7798784 | tf_op jit(solution)/shard_map/all_gather | solution.py:49
  142.1 18.6 %copy-start.5 = (f32[8192]{0:T(1024)S(1)}, f32[8192]{0:T(1024)}, u32[]{:S(2)}) copy-start(f32[8192]{0:T(1024)} %param.11) | copy-start | bytes 98308
  157.1 61.3 %all-to-all-start.4 = ((f32[8,128,512]{2,1,0:T(8,128)}), f32[8,128,512]{2,1,0:T(8,128)S(1)}, u32[]{:S(2)}, u32[]{:S(2)}) async-start(f32[8,128,512]{2,1,0:T(8,128)} %broadcast_in_dim.15), calls=%async_computation.4 | async-start | bytes 4194304 | tf_op jit(solution)/shard_map/all_to_all | solution.py:25
  267.1 40.5 %all-to-all-start.5 = ((f32[8,136,512]{2,1,0:T(8,128)}), f32[8,136,512]{2,1,0:T(8,128)S(1)}, u32[]{:S(2)}, u32[]{:S(2)}) async-start(f32[8,136,512]{2,1,0:T(8,128)} %select_maximum_fusion), calls=%async_computation.5 | async-start | bytes 4456448 | tf_op jit(solution)/shard_map/all_to_all | solution.py:61
  308.8 36.2 %all-to-all-start.6 = ((f32[16,9,512]{2,1,0:T(8,128)}), f32[16,9,512]{2,1,0:T(8,128)S(1)}, u32[]{:S(2)}, u32[]{:S(2)}) async-start(f32[16,9,512]{2,1,0:T(8,128)} %pad_maximum_fusion), calls=%async_computation.6 | async-start | bytes 1048576 | tf_op jit(solution)/shard_map/all_to_all | solution.py:70
  313.9 31.4 %copy-start.2 = (bf16[8,8192]{1,0:T(8,128)(2,1)S(1)}, bf16[8,8192]{1,0:T(8,128)(2,1)}, u32[]{:S(2)}) copy-start(bf16[8,8192]{1,0:T(8,128)(2,1)} %param.12) | copy-start | bytes 393220
Sparse Core Ops, SparseCore 0:
  140.5 68.3 all-gather.3
  211.2 45.4 all-gather.5
  258.4 77.4 all-gather.7

commit v4 on v2

--- a/solution.py
+++ b/solution.py
@@ -34,8 +34,21 @@
     normed = tokens_wide * inverse_rms
     tile = gate_weight.shape[0]
     gain_tile = lax.dynamic_slice_in_dim(gain, lax.axis_index("col") * tile, tile)
-    grid_normed = lax.all_to_all(normed, "col", split_axis=1, concat_axis=0, tiled=True)
-    grid_grad = lax.all_to_all(grad_out, "col", split_axis=1, concat_axis=0, tiled=True)
+    mine_rows = tokens.shape[0]
+    lanes = 128
+    packed = jnp.concatenate(
+        [
+            grad_out.astype(jnp.float32).reshape(mine_rows, cols, tile),
+            tokens_wide.reshape(mine_rows, cols, tile),
+            jnp.broadcast_to(inverse_rms[:, :, None], (mine_rows, cols, lanes)),
+        ],
+        axis=2,
+    )
+    grid = lax.all_to_all(packed, "col", split_axis=1, concat_axis=0, tiled=True)
+    grid = grid.reshape(cols * mine_rows, 2 * tile + lanes)
+    grid_grad = grid[:, :tile].astype(jnp.bfloat16)
+    grid_tokens = grid[:, tile : 2 * tile].astype(jnp.bfloat16)
+    grid_scale = grid[:, 2 * tile : 2 * tile + 1].reshape(1, cols * mine_rows)
     all_grad = row_gather(grid_grad)
     partial_grad = jnp.einsum(
         "td,fd->tf", all_grad, down_weight, preferred_element_type=jnp.float32
@@ -45,7 +58,9 @@
     gate_piece = lax.all_gather(gate_block, "col", axis=0, tiled=True)
     up_piece = lax.all_gather(up_block, "col", axis=0, tiled=True)
     hidden_piece = lax.all_gather(hidden_block, "col", axis=0, tiled=True)
-    all_normed = row_gather(grid_normed)
+    all_tokens = row_gather(grid_tokens).astype(jnp.float32)
+    all_scale = row_gather(grid_scale).reshape(-1, 1)
+    all_normed = all_tokens * all_scale
     all_input = (all_normed * gain_tile).astype(jnp.bfloat16)
     new_rows = jnp.einsum("tf,df->td", gate_piece, gate_weight, preferred_element_type=jnp.float32)
     new_rows = new_rows + jnp.einsum(

time: 360 us -> 353 us (0.981)
  blocking collectives: 50.2 us -> 41.8 us
  waiting for transfers between devices: 213 us -> 208 us
  starting transfers between devices: 17.7 us -> 21.8 us
    all_gather x1, waiting for transfers between devices: 50.5 us -> 41.1 us  [local(): gate_piece = lax.all_gather(gate_block, 'col', axis=0, tiled=True)]
    all_to_all x2 -> x1, blocking collectives: 27 us -> 18.3 us  [local(): lax.all_to_all(packed, 'col', split_axis=1, concat_axis=0, tiled=True)]
    all_to_all x1 -> x2, waiting for transfers between devices: 0.01 us -> 5.71 us  [row_gather(): got = lax.all_to_all(copies, 'row', split_axis=0, concat_axis=0, tiled=True)]
    all_to_all x1 -> x2, starting transfers between devices: 6.07 us -> 10.1 us  [row_gather(): got = lax.all_to_all(copies, 'row', split_axis=0, concat_axis=0, tiled=True)]
  transfers between devices with their start and end apart: 7 -> 8, of which waited for: 5 -> 6; matrix products, arithmetic and copies ran while one was open for 14% -> 15% of each run, Pallas kernels for 0% -> 0%
where the time goes in v4:
time: 353 us; the launch traced here: 352 us
  waiting for transfers between devices  208 us (59%)
  matrix products  53.2 us (15%)
  blocking collectives  41.8 us (12%)
  starting transfers between devices  21.8 us (6%)
  between operations  13.9 us (4%)
  other arithmetic  9.63 us (3%)
    reduce_scatter x1, waiting for transfers between devices, local(): lax.psum_scatter(partial_grad, 'col', scatter_dimension=0, tiled=True)  82.7 us
    all_gather x1, waiting for transfers between devices, local(): gate_piece = lax.all_gather(gate_block, 'col', axis=0, tiled=True)  41.1 us
    all_gather x1, waiting for transfers between devices, local(): up_piece = lax.all_gather(up_block, 'col', axis=0, tiled=True)  40.7 us
    all_to_all x1, blocking collectives, row_gather(): got = lax.all_to_all(copies, 'row', split_axis=0, concat_axis=0, tiled=True)  23.4 us
    all_gather x1, waiting for transfers between devices, local(): hidden_piece = lax.all_gather(hidden_block, 'col', axis=0, tiled=True)  20.8 us
    all_to_all x1, blocking collectives, local(): lax.all_to_all(packed, 'col', split_axis=1, concat_axis=0, tiled=True)  18.3 us
    all_to_all x1, waiting for transfers between devices, local(): got = lax.all_to_all(sent, 'row', split_axis=0, concat_axis=0, tiled=True)  16.1 us
    all_to_all x2, starting transfers between devices, row_gather(): got = lax.all_to_all(copies, 'row', split_axis=0, concat_axis=0, tiled=True)  10.1 us
  transfers between devices with their start and end apart: 8, of which 6 were waited for; matrix products, arithmetic and copies ran while one was open for 15% of the time, Pallas kernels for 0%

profile of v4, /device:TPU:1, one launch (start us, length us, event | category | flops | bytes accessed | tf_op | source)
XLA Modules:
  0.0 352.0 jit_solution(12043899856569020936)
XLA Ops:
  7.2 0.0 reduce-scatter.2.cloned.1.call-start
  7.2 1.1 multiply_reduce_fusion.1
  8.3 0.9 convert.17
  9.2 0.0 copy-start.7
  9.3 1.1 convert.18
  10.3 0.1 broadcast_in_dim.14
  10.5 18.3 %all_to_all.40 = f32[8,16,1152]{2,0,1:T(8,128)S(1)} all-to-all(f32[8,16,1152]{2,0,1:T(8,128)S(1)} %pad_maximum_fusion), channel_id=1, replica_groups=mesh['row'=8,'col'=16] {'col'}, dimensions={1} | all-to-all | bytes 1179648 | tf_op jit(solution)/shard_map/all_to_all | solution.py:47
  28.9 0.1 broadcast_in_dim.15
  29.0 23.4 %all_to_all.41 = bf16[8,128,512]{2,1,0:T(8,128)(2,1)S(1)} all-to-all(bf16[8,128,512]{2,1,0:T(8,128)(2,1)S(1)} %broadcast_in_dim.15), channel_id=1, replica_groups=mesh['row'=8,'col'=16] {'row'}, dimensions={0} | all-to-all | bytes 2097152 | tf_op jit(solution)/shard_map/all_to_all | solution.py:25
  52.4 7.3 %fusion.13 = f32[1024,3584]{1,0:T(8,128)} fusion(bf16[1024,512]{1,0:T(8,128)(2,1)S(1)} %bitcast.41, bf16[3584,512]{1,0:T(8,128)(2,1)S(1)} %copy-done.7), kind=kOutput, calls=%fused_computation.36 | convolution fusion | flops 3758096384 | bytes 19398656 | tf_op jit(solution)/shard_map/td,fd->tf/dot_general | solution.py:53
  59.7 0.0 reduce-scatter.2.cloned.1.call-update
  59.7 0.0 all-gather.4.cloned.1.call-start
  59.8 82.7 %reduce-scatter.2.cloned.1.call-done = f32[64,3584]{1,0:T(8,128)} async-done(((f32[1024,3584]{1,0:T(8,128)}), f32[64,3584]{1,0:T(8,128)}) %reduce-scatter.2.cloned.1.call-update) | async-done | bytes 917520 | tf_op jit(solution)/shard_map/reduce_scatter | solution.py:56
  142.5 2.7 multiply_convert_fusion
  145.2 0.0 all-gather.4.cloned.1.call-update
  145.2 0.0 all-gather.6.cloned.1.call-start
  145.3 0.7 all-gather.6.cloned.1.call-update
  145.9 0.0 all-gather.8.cloned.1.call-start
  146.0 0.5 all-gather.8.cloned.1.call-update
  146.5 0.1 slice_reduce_fusion
  146.6 0.6 broadcast_in_dim.18
  147.2 6.6 %all-to-all-start.3 = ((f32[8,1,128]{2,1,0:T(1,128)}), f32[8,1,128]{2,1,0:T(1,128)S(1)}, u32[]{:S(2)}, u32[]{:S(2)}) async-start(f32[8,1,128]{2,1,0:T(1,128)} %broadcast_in_dim.18), calls=%async_computation.4 | async-start | bytes 8192 | tf_op jit(solution)/shard_map/all_to_all | solution.py:25
  153.8 0.8 dynamic_slice.3
  154.6 5.7 %all-to-all-done.3 = f32[8,1,128]{2,1,0:T(1,128)S(1)} async-done(((f32[8,1,128]{2,1,0:T(1,128)}), f32[8,1,128]{2,1,0:T(1,128)S(1)}, u32[]{:S(2)}, u32[]{:S(2)}) %all-to-all-start.3) | async-done | bytes 4128 | tf_op jit(solution)/shard_map/all_to_all | solution.py:25
  160.3 1.1 broadcast_in_dim.16
  161.3 3.6 %all-to-all-start.2 = ((bf16[8,128,512]{2,1,0:T(8,128)(2,1)}), bf16[8,128,512]{2,1,0:T(8,128)(2,1)S(1)}, u32[]{:S(2)}, u32[]{:S(2)}) async-start(bf16[8,128,512]{2,1,0:T(8,128)(2,1)} %broadcast_in_dim.16), calls=%async_computation.3 | async-start | bytes 2097152 | tf_op jit(solution)/shard_map/all_to_all | solution.py:25
  164.9 41.1 %all-gather.4.cloned.1.call-done = bf16[1024,3584]{1,0:T(8,128)(2,1)} async-done(((bf16[64,3584]{1,0:T(8,128)(2,1)}), bf16[1024,3584]{1,0:T(8,128)(2,1)}) %all-gather.4.cloned.1.call-update) | async-done | bytes 7340048 | tf_op jit(solution)/shard_map/all_gather | solution.py:58
  206.0 9.4 %fusion.14 = f32[1024,512]{1,0:T(8,128)} fusion(bf16[1024,3584]{1,0:T(8,128)(2,1)} %all-gather.4.cloned.1.call-done, bf16[512,3584]{1,0:T(8,128)(2,1)} %param.15), kind=kOutput, calls=%fused_computation.37 | convolution fusion | flops 3758096384 | bytes 13107200 | tf_op jit(solution)/shard_map/tf,df->td/dot_general | solution.py:65
  215.4 0.0 all-to-all-done.2
  215.4 40.7 %all-gather.6.cloned.1.call-done = bf16[1024,3584]{1,0:T(8,128)(2,1)} async-done(((bf16[64,3584]{1,0:T(8,128)(2,1)}), bf16[1024,3584]{1,0:T(8,128)(2,1)}) %all-gather.6.cloned.1.call-update) | async-done | bytes 7340048 | tf_op jit(solution)/shard_map/all_gather | solution.py:59
  256.1 9.9 %fusion.3 = (bf16[1024,512]{1,0:T(8,128)(2,1)}, f32[512]{0:T(512)S(1)}, f32[1024,512]{1,0:T(8,128)S(1)}) fusion(bf16[8,128,512]{2,1,0:T(8,128)(2,1)S(1)} %all-to-all-done.2, f32[512]{0:T(512)S(1)} %dynamic_slice.3, f32[1024]{0:T(1024)S(1)} %bitcast.46, f32[1024,512]{1,0:T(8,128)} %fusion.14, bf16[1024,3584]{1,0:T(8,128)(2,1)} %all-gather.6.cloned.1.call-done, ...), kind=kOutput, calls=%fused_computation.9 | convolution fusion | flops 3761765888 | bytes 17309696 | tf_op jit(solution)/shard_map/tf,df->td/dot_general | solution.py:66
  266.0 1.6 select_maximum_fusion
  267.6 6.4 %all-to-all-start.4 = ((f32[8,136,512]{2,1,0:T(8,128)}), f32[8,136,512]{2,1,0:T(8,128)S(1)}, u32[]{:S(2)}, u32[]{:S(2)}) async-start(f32[8,136,512]{2,1,0:T(8,128)} %select_maximum_fusion), calls=%async_computation.5 | async-start | bytes 4456448 | tf_op jit(solution)/shard_map/all_to_all | solution.py:74
  274.0 9.5 %convolution_convert_fusion.1 = bf16[512,3584]{1,0:T(8,128)(2,1)} fusion(bf16[1024,512]{1,0:T(8,128)(2,1)} %get-tuple-element.19, bf16[1024,3584]{1,0:T(8,128)(2,1)} %all-gather.6.cloned.1.call-done), kind=kOutput, calls=%fused_computation.1 | convolution fusion | flops 3759931392 | bytes 12058624 | tf_op jit(solution)/shard_map/td,tf->df/dot_general | solution.py:87
  283.5 8.5 %convolution_convert_fusion.2 = bf16[512,3584]{1,0:T(8,128)(2,1)} fusion(bf16[1024,512]{1,0:T(8,128)(2,1)S(1)} %copy-done.8, bf16[1024,3584]{1,0:T(8,128)(2,1)} %all-gather.4.cloned.1.call-done), kind=kOutput, calls=%fused_computation.2 | convolution fusion | flops 3759931392 | bytes 12058624 | tf_op jit(solution)/shard_map/td,tf->df/dot_general | solution.py:86
  292.0 16.1 %all-to-all-done.4 = f32[8,136,512]{2,1,0:T(8,128)S(1)} async-done(((f32[8,136,512]{2,1,0:T(8,128)}), f32[8,136,512]{2,1,0:T(8,128)S(1)}, u32[]{:S(2)}, u32[]{:S(2)}) %all-to-all-start.4) | async-done | bytes 2228256 | tf_op jit(solution)/shard_map/all_to_all | solution.py:74
  308.1 0.2 reduce_sum.38
  308.4 0.9 pad_maximum_fusion.1
  309.3 5.1 %all-to-all-start.5 = ((f32[16,9,512]{2,1,0:T(8,128)}), f32[16,9,512]{2,1,0:T(8,128)S(1)}, u32[]{:S(2)}, u32[]{:S(2)}) async-start(f32[16,9,512]{2,1,0:T(8,128)} %pad_maximum_fusion.1), calls=%async_computation.6 | async-start | bytes 1048576 | tf_op jit(solution)/shard_map/all_to_all | solution.py:83
  314.4 0.0 copy-start.4
  314.4 0.0 copy-start.6
  314.4 0.0 copy-start.1
  314.4 20.8 %all-gather.8.cloned.1.call-done = bf16[1024,3584]{1,0:T(8,128)(2,1)} async-done(((bf16[64,3584]{1,0:T(8,128)(2,1)}), bf16[1024,3584]{1,0:T(8,128)(2,1)}) %all-gather.8.cloned.1.call-update) | async-done | bytes 7340048 | tf_op jit(solution)/shard_map/all_gather | solution.py:60
  335.2 8.6 %convolution_convert_fusion = bf16[3584,512]{1,0:T(8,128)(2,1)} fusion(bf16[1024,3584]{1,0:T(8,128)(2,1)} %all-gather.8.cloned.1.call-done, bf16[1024,512]{1,0:T(8,128)(2,1)S(1)} %bitcast.42), kind=kOutput, calls=%fused_computation | convolution fusion | flops 3759931392 | bytes 12058624 | tf_op jit(solution)/shard_map/tf,td->fd/dot_general | solution.py:88
  343.8 0.0 all-to-all-done.5
  343.8 0.3 multiply_reduce_fusion
  344.1 0.8 add_convert_fusion
  344.9 0.6 slice.55
  (24 shorter events, 0.2 us)
Async XLA Ops:
  7.2 135.3 %reduce-scatter.2.cloned.1.call-start = ((), (), s32[]{:S(2)}) async-start(), calls=%async_computation.7 | async-start | bytes 15597568 | tf_op jit(solution)/shard_map/reduce_scatter | solution.py:56
  8.3 20.6 %copy-start.5 = (f32[8]{0:T(128)}, f32[8]{0:T(128)S(1)}, u32[]{:S(2)}) copy-start(f32[8]{0:T(128)S(1)} %add_rsqrt_fusion) | copy-start | bytes 100
  9.2 43.1 %copy-start.7 = (bf16[3584,512]{1,0:T(8,128)(2,1)S(1)}, bf16[3584,512]{1,0:T(8,128)(2,1)}, u32[]{:S(2)}) copy-start(bf16[3584,512]{1,0:T(8,128)(2,1)} %param.17) | copy-start | bytes 11010052
  59.7 82.7 %copy-start.2 = (bf16[64,3584]{1,0:T(8,128)(2,1)S(1)}, bf16[64,3584]{1,0:T(8,128)(2,1)}, u32[]{:S(2)}) copy-start(bf16[64,3584]{1,0:T(8,128)(2,1)} %param.13) | copy-start | bytes 1376260
  59.7 82.7 %copy-start.3 = (bf16[64,3584]{1,0:T(8,128)(2,1)S(1)}, bf16[64,3584]{1,0:T(8,128)(2,1)}, u32[]{:S(2)}) copy-start(bf16[64,3584]{1,0:T(8,128)(2,1)} %param.14) | copy-start | bytes 1376260
  59.7 146.2 %all-gather.4.cloned.1.call-start = ((), (), s32[]{:S(2)}) async-start(), calls=%async_computation.8 | async-start | bytes 7798784 | tf_op jit(solution)/shard_map/all_gather | solution.py:58
  145.2 110.9 %all-gather.6.cloned.1.call-start = ((), (), s32[]{:S(2)}) async-start(), calls=%async_computation.9 | async-start | bytes 7798784 | tf_op jit(solution)/shard_map/all_gather | solution.py:59
  145.9 189.2 %all-gather.8.cloned.1.call-start = ((), (), s32[]{:S(2)}) async-start(), calls=%async_computation.10 | async-start | bytes 7798784 | tf_op jit(solution)/shard_map/all_gather | solution.py:60
  147.2 13.0 %all-to-all-start.3 = ((f32[8,1,128]{2,1,0:T(1,128)}), f32[8,1,128]{2,1,0:T(1,128)S(1)}, u32[]{:S(2)}, u32[]{:S(2)}) async-start(f32[8,1,128]{2,1,0:T(1,128)} %broadcast_in_dim.18), calls=%async_computation.4 | async-start | bytes 8192 | tf_op jit(solution)/shard_map/all_to_all | solution.py:25
  161.3 54.1 %all-to-all-start.2 = ((bf16[8,128,512]{2,1,0:T(8,128)(2,1)}), bf16[8,128,512]{2,1,0:T(8,128)(2,1)S(1)}, u32[]{:S(2)}, u32[]{:S(2)}) async-start(bf16[8,128,512]{2,1,0:T(8,128)(2,1)} %broadcast_in_dim.16), calls=%async_computation.3 | async-start | bytes 2097152 | tf_op jit(solution)/shard_map/all_to_all | solution.py:25
  267.6 40.5 %all-to-all-start.4 = ((f32[8,136,512]{2,1,0:T(8,128)}), f32[8,136,512]{2,1,0:T(8,128)S(1)}, u32[]{:S(2)}, u32[]{:S(2)}) async-start(f32[8,136,512]{2,1,0:T(8,128)} %select_maximum_fusion), calls=%async_computation.5 | async-start | bytes 4456448 | tf_op jit(solution)/shard_map/all_to_all | solution.py:74
  274.0 9.5 %copy-start.8 = (bf16[1024,512]{1,0:T(8,128)(2,1)S(1)}, bf16[1024,512]{1,0:T(8,128)(2,1)}, u32[]{:S(2)}) copy-start(bf16[1024,512]{1,0:T(8,128)(2,1)} %get-tuple-element.19) | copy-start | bytes 3145732
  309.3 34.5 %all-to-all-start.5 = ((f32[16,9,512]{2,1,0:T(8,128)}), f32[16,9,512]{2,1,0:T(8,128)S(1)}, u32[]{:S(2)}, u32[]{:S(2)}) async-start(f32[16,9,512]{2,1,0:T(8,128)} %pad_maximum_fusion.1), calls=%async_computation.6 | async-start | bytes 1048576 | tf_op jit(solution)/shard_map/all_to_all | solution.py:83
  314.4 29.4 %copy-start = (bf16[8,8192]{1,0:T(8,128)(2,1)S(1)}, bf16[8,8192]{1,0:T(8,128)(2,1)}, u32[]{:S(2)}) copy-start(bf16[8,8192]{1,0:T(8,128)(2,1)} %param.10) | copy-start | bytes 393220
  314.4 29.4 %copy-start.4 = (f32[8192]{0:T(1024)S(1)}, f32[8192]{0:T(1024)}, u32[]{:S(2)}) copy-start(f32[8192]{0:T(1024)} %param.11) | copy-start | bytes 98308
  314.4 29.4 %copy-start.6 = (f32[8]{0:T(128)S(1)}, f32[8]{0:T(128)}, u32[]{:S(2)}) copy-start(f32[8]{0:T(128)} %copy-done.5) | copy-start | bytes 100
  314.4 29.7 %copy-start.1 = (bf16[8,8192]{1,0:T(8,128)(2,1)S(1)}, bf16[8,8192]{1,0:T(8,128)(2,1)}, u32[]{:S(2)}) copy-start(bf16[8,8192]{1,0:T(8,128)(2,1)} %param.12) | copy-start | bytes 393220
Sparse Core Ops, SparseCore 0:
  59.9 82.5 reduce-scatter.1
  145.3 60.6 all-gather.3
  208.3 47.8 all-gather.5
  257.7 77.4 all-gather.7

commit v5 on v4

--- a/solution.py
+++ b/solution.py
@@ -36,19 +36,18 @@
     gain_tile = lax.dynamic_slice_in_dim(gain, lax.axis_index("col") * tile, tile)
     mine_rows = tokens.shape[0]
     lanes = 128
+    grid_grad = lax.all_to_all(grad_out, "col", split_axis=1, concat_axis=0, tiled=True)
     packed = jnp.concatenate(
         [
-            grad_out.astype(jnp.float32).reshape(mine_rows, cols, tile),
             tokens_wide.reshape(mine_rows, cols, tile),
             jnp.broadcast_to(inverse_rms[:, :, None], (mine_rows, cols, lanes)),
         ],
         axis=2,
     )
     grid = lax.all_to_all(packed, "col", split_axis=1, concat_axis=0, tiled=True)
-    grid = grid.reshape(cols * mine_rows, 2 * tile + lanes)
-    grid_grad = grid[:, :tile].astype(jnp.bfloat16)
-    grid_tokens = grid[:, tile : 2 * tile].astype(jnp.bfloat16)
-    grid_scale = grid[:, 2 * tile : 2 * tile + 1].reshape(1, cols * mine_rows)
+    grid = grid.reshape(cols * mine_rows, tile + lanes)
+    grid_tokens = grid[:, :tile].astype(jnp.bfloat16)
+    grid_scale = grid[:, tile : tile + 1].reshape(1, cols * mine_rows)
     all_grad = row_gather(grid_grad)
     partial_grad = jnp.einsum(
         "td,fd->tf", all_grad, down_weight, preferred_element_type=jnp.float32
@@ -68,13 +67,16 @@
     )
     gain_part = jnp.sum(new_rows * all_normed, axis=0)
     tokens_all = new_rows.shape[0]
-    blocks = new_rows.reshape(rows, tokens_all // rows, tile)
-    extra = jnp.zeros((rows, 8, tile), jnp.float32).at[:, 0, :].set(gain_part)
+    blocks = new_rows.astype(jnp.bfloat16).reshape(rows, tokens_all // rows, tile)
+    gain_high = gain_part.astype(jnp.bfloat16)
+    gain_low = (gain_part - gain_high.astype(jnp.float32)).astype(jnp.bfloat16)
+    extra = jnp.zeros((rows, 8, tile), jnp.bfloat16)
+    extra = extra.at[:, 0, :].set(gain_high).at[:, 1, :].set(gain_low)
     sent = jnp.concatenate([blocks, extra], axis=1)
     got = lax.all_to_all(sent, "row", split_axis=0, concat_axis=0, tiled=True)
-    summed = jnp.sum(got, axis=0)
+    summed = jnp.sum(got.astype(jnp.float32), axis=0)
     grid_back = summed[: tokens_all // rows]
-    gain_tile_grad = summed[tokens_all // rows]
+    gain_tile_grad = summed[tokens_all // rows] + summed[tokens_all // rows + 1]
     per_col = grid_back.reshape(cols, -1, tile)
     mine = per_col.shape[1]
     sent2 = jnp.concatenate(

time: 353 us -> 335 us (0.949)
  waiting for transfers between devices: 208 us -> 184 us
  blocking collectives: 41.8 us -> 51.5 us
    all_to_all x1, waiting for transfers between devices: 16.1 us -> 1.16 us  [local(): got = lax.all_to_all(sent, 'row', split_axis=0, concat_axis=0, tiled=True)]
    all_to_all x0 -> x1, blocking collectives: none -> 13.4 us  [local(): lax.all_to_all(grad_out, 'col', split_axis=1, concat_axis=0, tiled=True)]
    all_gather x1, waiting for transfers between devices: 41.1 us -> 28.7 us  [local(): gate_piece = lax.all_gather(gate_block, 'col', axis=0, tiled=True)]
where the time goes in v5:
time: 335 us
  waiting for transfers between devices  184 us (55%)
  matrix products  55.2 us (16%)
  blocking collectives  51.5 us (15%)
  starting transfers between devices  21 us (6%)
  between operations  13.9 us (4%)
  other arithmetic  6.11 us (2%)
    reduce_scatter x1, waiting for transfers between devices, local(): lax.psum_scatter(partial_grad, 'col', scatter_dimension=0, tiled=True)  83 us
    all_gather x1, waiting for transfers between devices, local(): up_piece = lax.all_gather(up_block, 'col', axis=0, tiled=True)  39.4 us
    all_gather x1, waiting for transfers between devices, local(): gate_piece = lax.all_gather(gate_block, 'col', axis=0, tiled=True)  28.7 us
    all_gather x1, waiting for transfers between devices, local(): hidden_piece = lax.all_gather(hidden_block, 'col', axis=0, tiled=True)  24.2 us
    all_to_all x1, blocking collectives, row_gather(): got = lax.all_to_all(copies, 'row', split_axis=0, concat_axis=0, tiled=True)  23.2 us
    all_to_all x1, blocking collectives, local(): lax.all_to_all(packed, 'col', split_axis=1, concat_axis=0, tiled=True)  14.9 us
    all_to_all x1, blocking collectives, local(): lax.all_to_all(grad_out, 'col', split_axis=1, concat_axis=0, tiled=True)  13.4 us
    dot_general x1, matrix products, local(): jnp.einsum('tf,df->td', up_piece, up_weight, preferred_element_type=jnp.f...  9.91 us
  transfers between devices with their start and end apart: 8, of which 6 were waited for; matrix products, arithmetic and copies ran while one was open for 15% of the time, Pallas kernels for 0%

profile of v5, /device:TPU:1, one launch (start us, length us, event | category | flops | bytes accessed | tf_op | source)
XLA Modules:
  0.0 334.7 jit_solution(11893688080982382999)
XLA Ops:
  7.2 0.0 reduce-scatter.2.cloned.1.call-start
  7.2 13.4 %all_to_all.56 = bf16[8,16,512]{2,0,1:T(8,128)(2,1)S(1)} all-to-all(bf16[8,16,512]{2,0,1:T(8,128)(2,1)} %bitcast.46), channel_id=1, replica_groups=mesh['row'=8,'col'=16] {'col'}, dimensions={1} | all-to-all | bytes 262144 | tf_op jit(solution)/shard_map/all_to_all | solution.py:39
  20.6 0.1 broadcast_in_dim.15
  20.7 23.2 %all_to_all.57 = bf16[8,128,512]{2,1,0:T(8,128)(2,1)S(1)} all-to-all(bf16[8,128,512]{2,1,0:T(8,128)(2,1)S(1)} %broadcast_in_dim.15), channel_id=1, replica_groups=mesh['row'=8,'col'=16] {'row'}, dimensions={0} | all-to-all | bytes 2097152 | tf_op jit(solution)/shard_map/all_to_all | solution.py:25
  43.8 9.3 %fusion.13 = f32[1024,3584]{1,0:T(8,128)} fusion(bf16[1024,512]{1,0:T(8,128)(2,1)S(1)} %bitcast.40, bf16[3584,512]{1,0:T(8,128)(2,1)} %param.19), kind=kOutput, calls=%fused_computation.38 | convolution fusion | flops 3758096384 | bytes 19398656 | tf_op jit(solution)/shard_map/td,fd->tf/dot_general | solution.py:52
  53.2 0.0 reduce-scatter.2.cloned.1.call-update
  53.2 0.0 copy-start
  53.2 0.0 copy-start.4
  53.2 0.0 all-gather.4.cloned.1.call-start
  53.3 83.0 %reduce-scatter.2.cloned.1.call-done = f32[64,3584]{1,0:T(8,128)} async-done(((f32[1024,3584]{1,0:T(8,128)}), f32[64,3584]{1,0:T(8,128)}) %reduce-scatter.2.cloned.1.call-update) | async-done | bytes 917520 | tf_op jit(solution)/shard_map/reduce_scatter | solution.py:55
  136.3 2.7 multiply_convert_fusion
  139.0 0.0 all-gather.4.cloned.1.call-update
  139.0 0.0 all-gather.6.cloned.1.call-start
  139.1 0.7 all-gather.6.cloned.1.call-update
  139.7 0.0 all-gather.8.cloned.1.call-start
  139.8 0.5 all-gather.8.cloned.1.call-update
  140.4 0.2 multiply_reduce_fusion.1
  140.5 0.1 broadcast_in_dim.16
  140.7 14.9 %all_to_all.58 = f32[8,16,640]{2,0,1:T(8,128)S(1)} all-to-all(f32[8,16,640]{2,0,1:T(8,128)S(1)} %pad_maximum_fusion.2), channel_id=1, replica_groups=mesh['row'=8,'col'=16] {'col'}, dimensions={1} | all-to-all | bytes 655360 | tf_op jit(solution)/shard_map/all_to_all | solution.py:47
  155.6 0.1 slice_reduce_fusion
  155.7 0.6 broadcast_in_dim.19
  156.3 5.8 %all-to-all-start.4 = ((f32[8,1,128]{2,1,0:T(1,128)}), f32[8,1,128]{2,1,0:T(1,128)S(1)}, u32[]{:S(2)}, u32[]{:S(2)}) async-start(f32[8,1,128]{2,1,0:T(1,128)} %broadcast_in_dim.19), calls=%async_computation.5 | async-start | bytes 8192 | tf_op jit(solution)/shard_map/all_to_all | solution.py:25
  162.1 0.0 copy-done.4
  162.1 0.1 dynamic_slice.3
  162.2 6.4 %all-to-all-done.4 = f32[8,1,128]{2,1,0:T(1,128)S(1)} async-done(((f32[8,1,128]{2,1,0:T(1,128)}), f32[8,1,128]{2,1,0:T(1,128)S(1)}, u32[]{:S(2)}, u32[]{:S(2)}) %all-to-all-start.4) | async-done | bytes 4128 | tf_op jit(solution)/shard_map/all_to_all | solution.py:25
  168.6 1.1 broadcast_in_dim.17
  169.6 3.6 %all-to-all-start.3 = ((bf16[8,128,512]{2,1,0:T(8,128)(2,1)}), bf16[8,128,512]{2,1,0:T(8,128)(2,1)S(1)}, u32[]{:S(2)}, u32[]{:S(2)}) async-start(bf16[8,128,512]{2,1,0:T(8,128)(2,1)} %broadcast_in_dim.17), calls=%async_computation.4 | async-start | bytes 2097152 | tf_op jit(solution)/shard_map/all_to_all | solution.py:25
  173.2 28.7 %all-gather.4.cloned.1.call-done = bf16[1024,3584]{1,0:T(8,128)(2,1)} async-done(((bf16[64,3584]{1,0:T(8,128)(2,1)}), bf16[1024,3584]{1,0:T(8,128)(2,1)}) %all-gather.4.cloned.1.call-update) | async-done | bytes 7340048 | tf_op jit(solution)/shard_map/all_gather | solution.py:57
  201.9 9.4 %fusion.14 = f32[1024,512]{1,0:T(8,128)} fusion(bf16[1024,3584]{1,0:T(8,128)(2,1)} %all-gather.4.cloned.1.call-done, bf16[512,3584]{1,0:T(8,128)(2,1)} %param.17), kind=kOutput, calls=%fused_computation.39 | convolution fusion | flops 3758096384 | bytes 13107200 | tf_op jit(solution)/shard_map/tf,df->td/dot_general | solution.py:64
  211.3 0.0 all-to-all-done.3
  211.3 39.4 %all-gather.6.cloned.1.call-done = bf16[1024,3584]{1,0:T(8,128)(2,1)} async-done(((bf16[64,3584]{1,0:T(8,128)(2,1)}), bf16[1024,3584]{1,0:T(8,128)(2,1)}) %all-gather.6.cloned.1.call-update) | async-done | bytes 7340048 | tf_op jit(solution)/shard_map/all_gather | solution.py:58
  250.7 9.9 %fusion.12 = (bf16[1024,512]{1,0:T(8,128)(2,1)S(1)}, f32[512]{0:T(512)S(1)}, bf16[1024,512]{1,0:T(8,128)(2,1)}) fusion(f32[1024]{0:T(1024)S(1)} %bitcast.49, bf16[8,128,512]{2,1,0:T(8,128)(2,1)S(1)} %all-to-all-done.3, f32[512]{0:T(512)S(1)} %dynamic_slice.3, f32[1024,512]{1,0:T(8,128)} %fusion.14, bf16[1024,3584]{1,0:T(8,128)(2,1)} %all-gather.6.cloned.1.call-done, ...), kind=kOutput, calls=%fused_computation.37 | convolution fusion | flops 3762290176 | bytes 16261120 | tf_op jit(solution)/shard_map/tf,df->td/dot_general | solution.py:65
  260.7 0.1 scatter.9
  260.8 1.1 pad_maximum_fusion
  261.9 6.4 %all-to-all-start.5 = ((bf16[8,136,512]{2,1,0:T(8,128)(2,1)}), bf16[8,136,512]{2,1,0:T(8,128)(2,1)S(1)}, u32[]{:S(2)}, u32[]{:S(2)}) async-start(bf16[8,136,512]{2,1,0:T(8,128)(2,1)} %pad_maximum_fusion), calls=%async_computation.6 | async-start | bytes 2228224 | tf_op jit(solution)/shard_map/all_to_all | solution.py:76
  268.3 9.5 %convolution_convert_fusion.1 = bf16[512,3584]{1,0:T(8,128)(2,1)} fusion(bf16[1024,512]{1,0:T(8,128)(2,1)} %get-tuple-element.35, bf16[1024,3584]{1,0:T(8,128)(2,1)} %all-gather.6.cloned.1.call-done), kind=kOutput, calls=%fused_computation.1 | convolution fusion | flops 3759931392 | bytes 12058624 | tf_op jit(solution)/shard_map/td,tf->df/dot_general | solution.py:89
  277.8 8.5 %convolution_convert_fusion.2 = bf16[512,3584]{1,0:T(8,128)(2,1)} fusion(bf16[1024,512]{1,0:T(8,128)(2,1)S(1)} %copy-done.5, bf16[1024,3584]{1,0:T(8,128)(2,1)} %all-gather.4.cloned.1.call-done), kind=kOutput, calls=%fused_computation.2 | convolution fusion | flops 3759931392 | bytes 12058624 | tf_op jit(solution)/shard_map/td,tf->df/dot_general | solution.py:88
  286.3 1.2 all-to-all-done.5
  287.5 0.2 convert_reduce_fusion
  287.7 0.9 pad_maximum_fusion.1
  288.6 5.1 %all-to-all-start.6 = ((f32[16,9,512]{2,1,0:T(8,128)}), f32[16,9,512]{2,1,0:T(8,128)S(1)}, u32[]{:S(2)}, u32[]{:S(2)}) async-start(f32[16,9,512]{2,1,0:T(8,128)} %pad_maximum_fusion.1), calls=%async_computation.7 | async-start | bytes 1048576 | tf_op jit(solution)/shard_map/all_to_all | solution.py:85
  293.7 24.2 %all-gather.8.cloned.1.call-done = bf16[1024,3584]{1,0:T(8,128)(2,1)} async-done(((bf16[64,3584]{1,0:T(8,128)(2,1)}), bf16[1024,3584]{1,0:T(8,128)(2,1)}) %all-gather.8.cloned.1.call-update) | async-done | bytes 7340048 | tf_op jit(solution)/shard_map/all_gather | solution.py:59
  317.9 8.6 %convolution_convert_fusion = bf16[3584,512]{1,0:T(8,128)(2,1)} fusion(bf16[1024,3584]{1,0:T(8,128)(2,1)} %all-gather.8.cloned.1.call-done, bf16[1024,512]{1,0:T(8,128)(2,1)S(1)} %bitcast.41), kind=kOutput, calls=%fused_computation | convolution fusion | flops 3759931392 | bytes 12058624 | tf_op jit(solution)/shard_map/tf,td->fd/dot_general | solution.py:90
  326.4 0.0 all-to-all-done.6
  326.5 0.3 multiply_reduce_fusion
  326.7 0.0 copy-done.1
  326.7 0.8 add_convert_fusion
  327.5 0.6 slice.74
  (21 shorter events, 0.2 us)
Async XLA Ops:
  7.2 129.1 %reduce-scatter.2.cloned.1.call-start = ((), (), s32[]{:S(2)}) async-start(), calls=%async_computation.8 | async-start | bytes 15597568 | tf_op jit(solution)/shard_map/reduce_scatter | solution.py:55
  53.2 83.1 %copy-start.2 = (bf16[64,3584]{1,0:T(8,128)(2,1)S(1)}, bf16[64,3584]{1,0:T(8,128)(2,1)}, u32[]{:S(2)}) copy-start(bf16[64,3584]{1,0:T(8,128)(2,1)} %param.15) | copy-start | bytes 1376260
  53.2 83.1 %copy-start.3 = (bf16[64,3584]{1,0:T(8,128)(2,1)S(1)}, bf16[64,3584]{1,0:T(8,128)(2,1)}, u32[]{:S(2)}) copy-start(bf16[64,3584]{1,0:T(8,128)(2,1)} %param.16) | copy-start | bytes 1376260
  53.2 87.1 %copy-start = (bf16[8,8192]{1,0:T(8,128)(2,1)S(1)}, bf16[8,8192]{1,0:T(8,128)(2,1)}, u32[]{:S(2)}) copy-start(bf16[8,8192]{1,0:T(8,128)(2,1)} %param.12) | copy-start | bytes 393220
  53.2 108.9 %copy-start.4 = (f32[8192]{0:T(1024)S(1)}, f32[8192]{0:T(1024)}, u32[]{:S(2)}) copy-start(f32[8192]{0:T(1024)} %param.13) | copy-start | bytes 98308
  53.2 148.7 %all-gather.4.cloned.1.call-start = ((), (), s32[]{:S(2)}) async-start(), calls=%async_computation.9 | async-start | bytes 7798784 | tf_op jit(solution)/shard_map/all_gather | solution.py:57
  139.0 111.7 %all-gather.6.cloned.1.call-start = ((), (), s32[]{:S(2)}) async-start(), calls=%async_computation.10 | async-start | bytes 7798784 | tf_op jit(solution)/shard_map/all_gather | solution.py:58
  139.7 178.1 %all-gather.8.cloned.1.call-start = ((), (), s32[]{:S(2)}) async-start(), calls=%async_computation.11 | async-start | bytes 7798784 | tf_op jit(solution)/shard_map/all_gather | solution.py:59
  156.3 12.3 %all-to-all-start.4 = ((f32[8,1,128]{2,1,0:T(1,128)}), f32[8,1,128]{2,1,0:T(1,128)S(1)}, u32[]{:S(2)}, u32[]{:S(2)}) async-start(f32[8,1,128]{2,1,0:T(1,128)} %broadcast_in_dim.19), calls=%async_computation.5 | async-start | bytes 8192 | tf_op jit(solution)/shard_map/all_to_all | solution.py:25
  169.6 41.7 %all-to-all-start.3 = ((bf16[8,128,512]{2,1,0:T(8,128)(2,1)}), bf16[8,128,512]{2,1,0:T(8,128)(2,1)S(1)}, u32[]{:S(2)}, u32[]{:S(2)}) async-start(bf16[8,128,512]{2,1,0:T(8,128)(2,1)} %broadcast_in_dim.17), calls=%async_computation.4 | async-start | bytes 2097152 | tf_op jit(solution)/shard_map/all_to_all | solution.py:25
  261.9 25.6 %all-to-all-start.5 = ((bf16[8,136,512]{2,1,0:T(8,128)(2,1)}), bf16[8,136,512]{2,1,0:T(8,128)(2,1)S(1)}, u32[]{:S(2)}, u32[]{:S(2)}) async-start(bf16[8,136,512]{2,1,0:T(8,128)(2,1)} %pad_maximum_fusion), calls=%async_computation.6 | async-start | bytes 2228224 | tf_op jit(solution)/shard_map/all_to_all | solution.py:76
  268.3 9.5 %copy-start.5 = (bf16[1024,512]{1,0:T(8,128)(2,1)S(1)}, bf16[1024,512]{1,0:T(8,128)(2,1)}, u32[]{:S(2)}) copy-start(bf16[1024,512]{1,0:T(8,128)(2,1)} %get-tuple-element.35) | copy-start | bytes 3145732
  288.6 37.9 %all-to-all-start.6 = ((f32[16,9,512]{2,1,0:T(8,128)}), f32[16,9,512]{2,1,0:T(8,128)S(1)}, u32[]{:S(2)}, u32[]{:S(2)}) async-start(f32[16,9,512]{2,1,0:T(8,128)} %pad_maximum_fusion.1), calls=%async_computation.7 | async-start | bytes 1048576 | tf_op jit(solution)/shard_map/all_to_all | solution.py:85
  293.7 33.1 %copy-start.1 = (bf16[8,8192]{1,0:T(8,128)(2,1)S(1)}, bf16[8,8192]{1,0:T(8,128)(2,1)}, u32[]{:S(2)}) copy-start(bf16[8,8192]{1,0:T(8,128)(2,1)} %param.14) | copy-start | bytes 393220
Sparse Core Ops, SparseCore 0:
  53.3 82.9 reduce-scatter.1
  139.1 62.7 all-gather.3
  204.2 46.4 all-gather.5
  252.3 65.5 all-gather.7

commit v6 on v5

--- a/solution.py
+++ b/solution.py
@@ -49,14 +49,16 @@
     grid_tokens = grid[:, :tile].astype(jnp.bfloat16)
     grid_scale = grid[:, tile : tile + 1].reshape(1, cols * mine_rows)
     all_grad = row_gather(grid_grad)
+    hidden_block = swiglu_grads(jnp.zeros(pre_gate.shape, jnp.float32), pre_gate, pre_up)[0]
+    hidden_piece = lax.all_gather(hidden_block, "col", axis=0, tiled=True)
     partial_grad = jnp.einsum(
         "td,fd->tf", all_grad, down_weight, preferred_element_type=jnp.float32
     )
+    hidden_piece, partial_grad = lax.optimization_barrier((hidden_piece, partial_grad))
     block_grad = lax.psum_scatter(partial_grad, "col", scatter_dimension=0, tiled=True)
-    hidden_block, gate_block, up_block = swiglu_grads(block_grad, pre_gate, pre_up)
+    _, gate_block, up_block = swiglu_grads(block_grad, pre_gate, pre_up)
     gate_piece = lax.all_gather(gate_block, "col", axis=0, tiled=True)
     up_piece = lax.all_gather(up_block, "col", axis=0, tiled=True)
-    hidden_piece = lax.all_gather(hidden_block, "col", axis=0, tiled=True)
     all_tokens = row_gather(grid_tokens).astype(jnp.float32)
     all_scale = row_gather(grid_scale).reshape(-1, 1)
     all_normed = all_tokens * all_scale

time: 335 us -> 335 us (level)
  waiting for transfers between devices: 184 us -> 180 us
    all_gather x1, waiting for transfers between devices: 24.2 us -> 14.7 us  [local(): hidden_piece = lax.all_gather(hidden_block, 'col', axis=0, tiled=True)]
    reduce_scatter x1, waiting for transfers between devices: 83 us -> 88.9 us  [local(): lax.psum_scatter(partial_grad, 'col', scatter_dimension=0, tiled=True)]
  transfers between devices with their start and end apart: 8 -> 8, of which waited for: 6 -> 7; matrix products, arithmetic and copies ran while one was open for 15% -> 14% of each run, Pallas kernels for 0% -> 0%
where the time goes in v6:
time: 335 us; the launch traced here: 334 us
  waiting for transfers between devices  180 us (54%)
  matrix products  55.4 us (17%)
  blocking collectives  53.3 us (16%)
  starting transfers between devices  20.6 us (6%)
  between operations  13.9 us (4%)
  other arithmetic  8.17 us (2%)
    reduce_scatter x1, waiting for transfers between devices, local(): lax.psum_scatter(partial_grad, 'col', scatter_dimension=0, tiled=True)  88.9 us
    all_gather x1, waiting for transfers between devices, local(): up_piece = lax.all_gather(up_block, 'col', axis=0, tiled=True)  39.3 us
    all_gather x1, waiting for transfers between devices, local(): gate_piece = lax.all_gather(gate_block, 'col', axis=0, tiled=True)  29.3 us
    all_to_all x1, blocking collectives, row_gather(): got = lax.all_to_all(copies, 'row', split_axis=0, concat_axis=0, tiled=True)  25 us
    all_to_all x1, blocking collectives, local(): lax.all_to_all(packed, 'col', split_axis=1, concat_axis=0, tiled=True)  14.8 us
    all_gather x1, waiting for transfers between devices, local(): hidden_piece = lax.all_gather(hidden_block, 'col', axis=0, tiled=True)  14.7 us
    all_to_all x1, blocking collectives, local(): lax.all_to_all(grad_out, 'col', split_axis=1, concat_axis=0, tiled=True)  13.4 us
    dot_general x1, matrix products, local(): jnp.einsum('tf,df->td', up_piece, up_weight, preferred_element_type=jnp.f...  9.94 us
  transfers between devices with their start and end apart: 8, of which 7 were waited for; matrix products, arithmetic and copies ran while one was open for 14% of the time, Pallas kernels for 0%

profile of v6, /device:TPU:1, one launch (start us, length us, event | category | flops | bytes accessed | tf_op | source)
XLA Modules:
  0.0 334.4 jit_solution(18331446118995921205)
XLA Ops:
  7.2 0.0 all-gather.4.cloned.1.call-start
  7.2 2.2 fusion.4
  9.4 0.0 all-gather.4.cloned.1.call-update
  9.4 0.0 reduce-scatter.2.cloned.1.call-start
  9.5 13.4 %all_to_all.56 = bf16[8,16,512]{2,0,1:T(8,128)(2,1)S(1)} all-to-all(bf16[8,16,512]{2,0,1:T(8,128)(2,1)} %bitcast.46), channel_id=1, replica_groups=mesh['row'=8,'col'=16] {'col'}, dimensions={1} | all-to-all | bytes 262144 | tf_op jit(solution)/shard_map/all_to_all | solution.py:39
  22.9 0.1 broadcast_in_dim.15
  23.0 25.0 %all_to_all.57 = bf16[8,128,512]{2,1,0:T(8,128)(2,1)S(1)} all-to-all(bf16[8,128,512]{2,1,0:T(8,128)(2,1)S(1)} %broadcast_in_dim.15), channel_id=1, replica_groups=mesh['row'=8,'col'=16] {'row'}, dimensions={0} | all-to-all | bytes 2097152 | tf_op jit(solution)/shard_map/all_to_all | solution.py:25
  48.0 9.6 %fusion.13 = f32[1024,3584]{1,0:T(8,128)} fusion(bf16[1024,512]{1,0:T(8,128)(2,1)S(1)} %bitcast.40, bf16[3584,512]{1,0:T(8,128)(2,1)} %param.19), kind=kOutput, calls=%fused_computation.38 | convolution fusion | flops 3758096384 | bytes 19398656 | tf_op jit(solution)/shard_map/td,fd->tf/dot_general | solution.py:54
  57.6 14.7 %all-gather.4.cloned.1.call-done = bf16[1024,3584]{1,0:T(8,128)(2,1)} async-done(((bf16[64,3584]{1,0:T(8,128)(2,1)}), bf16[1024,3584]{1,0:T(8,128)(2,1)}) %all-gather.4.cloned.1.call-update) | async-done | bytes 7340048 | tf_op jit(solution)/shard_map/all_gather | solution.py:53
  72.3 0.0 reduce-scatter.2.cloned.1.call-update
  72.3 0.0 copy-start
  72.3 0.0 copy-start.4
  72.3 0.0 all-gather.6.cloned.1.call-start
  72.4 88.9 %reduce-scatter.2.cloned.1.call-done = f32[64,3584]{1,0:T(8,128)} async-done(((f32[1024,3584]{1,0:T(8,128)}), f32[64,3584]{1,0:T(8,128)}) %reduce-scatter.2.cloned.1.call-update) | async-done | bytes 917520 | tf_op jit(solution)/shard_map/reduce_scatter | solution.py:58
  161.3 0.0 copy-done.1
  161.3 2.5 multiply_convert_fusion
  163.8 0.0 all-gather.6.cloned.1.call-update
  163.8 0.0 all-gather.8.cloned.1.call-start
  163.9 0.5 all-gather.8.cloned.1.call-update
  164.4 0.2 multiply_reduce_fusion.1
  164.6 0.1 broadcast_in_dim.16
  164.8 14.8 %all_to_all.58 = f32[8,16,640]{2,0,1:T(8,128)S(1)} all-to-all(f32[8,16,640]{2,0,1:T(8,128)S(1)} %pad_maximum_fusion.2), channel_id=1, replica_groups=mesh['row'=8,'col'=16] {'col'}, dimensions={1} | all-to-all | bytes 655360 | tf_op jit(solution)/shard_map/all_to_all | solution.py:47
  179.6 0.1 slice_reduce_fusion
  179.7 0.6 broadcast_in_dim.19
  180.3 5.5 %all-to-all-start.4 = ((f32[8,1,128]{2,1,0:T(1,128)}), f32[8,1,128]{2,1,0:T(1,128)S(1)}, u32[]{:S(2)}, u32[]{:S(2)}) async-start(f32[8,1,128]{2,1,0:T(1,128)} %broadcast_in_dim.19), calls=%async_computation.5 | async-start | bytes 8192 | tf_op jit(solution)/shard_map/all_to_all | solution.py:25
  185.8 0.1 dynamic_slice.3
  185.9 6.4 %all-to-all-done.4 = f32[8,1,128]{2,1,0:T(1,128)S(1)} async-done(((f32[8,1,128]{2,1,0:T(1,128)}), f32[8,1,128]{2,1,0:T(1,128)S(1)}, u32[]{:S(2)}, u32[]{:S(2)}) %all-to-all-start.4) | async-done | bytes 4128 | tf_op jit(solution)/shard_map/all_to_all | solution.py:25
  192.2 1.1 broadcast_in_dim.17
  193.3 3.6 %all-to-all-start.3 = ((bf16[8,128,512]{2,1,0:T(8,128)(2,1)}), bf16[8,128,512]{2,1,0:T(8,128)(2,1)S(1)}, u32[]{:S(2)}, u32[]{:S(2)}) async-start(bf16[8,128,512]{2,1,0:T(8,128)(2,1)} %broadcast_in_dim.17), calls=%async_computation.4 | async-start | bytes 2097152 | tf_op jit(solution)/shard_map/all_to_all | solution.py:25
  196.9 29.3 %all-gather.6.cloned.1.call-done = bf16[1024,3584]{1,0:T(8,128)(2,1)} async-done(((bf16[64,3584]{1,0:T(8,128)(2,1)}), bf16[1024,3584]{1,0:T(8,128)(2,1)}) %all-gather.6.cloned.1.call-update) | async-done | bytes 7340048 | tf_op jit(solution)/shard_map/all_gather | solution.py:60
  226.2 9.4 %fusion.14 = f32[1024,512]{1,0:T(8,128)} fusion(bf16[1024,3584]{1,0:T(8,128)(2,1)} %all-gather.6.cloned.1.call-done, bf16[512,3584]{1,0:T(8,128)(2,1)} %param.17), kind=kOutput, calls=%fused_computation.39 | convolution fusion | flops 3758096384 | bytes 13107200 | tf_op jit(solution)/shard_map/tf,df->td/dot_general | solution.py:66
  235.6 0.0 all-to-all-done.3
  235.6 39.3 %all-gather.8.cloned.1.call-done = bf16[1024,3584]{1,0:T(8,128)(2,1)} async-done(((bf16[64,3584]{1,0:T(8,128)(2,1)}), bf16[1024,3584]{1,0:T(8,128)(2,1)}) %all-gather.8.cloned.1.call-update) | async-done | bytes 7340048 | tf_op jit(solution)/shard_map/all_gather | solution.py:61
  274.9 9.9 %fusion.12 = (bf16[1024,512]{1,0:T(8,128)(2,1)S(1)}, f32[512]{0:T(512)S(1)}, bf16[1024,512]{1,0:T(8,128)(2,1)}) fusion(f32[1024]{0:T(1024)S(1)} %bitcast.49, bf16[8,128,512]{2,1,0:T(8,128)(2,1)S(1)} %all-to-all-done.3, f32[512]{0:T(512)S(1)} %dynamic_slice.3, f32[1024,512]{1,0:T(8,128)} %fusion.14, bf16[1024,3584]{1,0:T(8,128)(2,1)} %all-gather.8.cloned.1.call-done, ...), kind=kOutput, calls=%fused_computation.37 | convolution fusion | flops 3762290176 | bytes 16261120 | tf_op jit(solution)/shard_map/tf,df->td/dot_general | solution.py:67
  284.9 0.1 scatter.9
  285.0 1.1 pad_maximum_fusion
  286.1 6.4 %all-to-all-start.5 = ((bf16[8,136,512]{2,1,0:T(8,128)(2,1)}), bf16[8,136,512]{2,1,0:T(8,128)(2,1)S(1)}, u32[]{:S(2)}, u32[]{:S(2)}) async-start(bf16[8,136,512]{2,1,0:T(8,128)(2,1)} %pad_maximum_fusion), calls=%async_computation.6 | async-start | bytes 2228224 | tf_op jit(solution)/shard_map/all_to_all | solution.py:78
  292.6 8.7 %convolution_convert_fusion = bf16[3584,512]{1,0:T(8,128)(2,1)} fusion(bf16[1024,3584]{1,0:T(8,128)(2,1)} %all-gather.4.cloned.1.call-done, bf16[1024,512]{1,0:T(8,128)(2,1)S(1)} %bitcast.41), kind=kOutput, calls=%fused_computation | convolution fusion | flops 3759931392 | bytes 12058624 | tf_op jit(solution)/shard_map/tf,td->fd/dot_general | solution.py:92
  301.2 8.5 %convolution_convert_fusion.1 = bf16[512,3584]{1,0:T(8,128)(2,1)} fusion(bf16[1024,512]{1,0:T(8,128)(2,1)S(1)} %copy-done.5, bf16[1024,3584]{1,0:T(8,128)(2,1)} %all-gather.8.cloned.1.call-done), kind=kOutput, calls=%fused_computation.1 | convolution fusion | flops 3759931392 | bytes 12058624 | tf_op jit(solution)/shard_map/td,tf->df/dot_general | solution.py:91
  309.8 0.9 all-to-all-done.5
  310.6 0.2 convert_reduce_fusion
  310.8 0.9 pad_maximum_fusion.1
  311.7 5.0 %all-to-all-start.6 = ((f32[16,9,512]{2,1,0:T(8,128)}), f32[16,9,512]{2,1,0:T(8,128)S(1)}, u32[]{:S(2)}, u32[]{:S(2)}) async-start(f32[16,9,512]{2,1,0:T(8,128)} %pad_maximum_fusion.1), calls=%async_computation.7 | async-start | bytes 1048576 | tf_op jit(solution)/shard_map/all_to_all | solution.py:87
  316.7 9.3 %convolution_convert_fusion.2 = bf16[512,3584]{1,0:T(8,128)(2,1)} fusion(bf16[1024,512]{1,0:T(8,128)(2,1)} %get-tuple-element.39, bf16[1024,3584]{1,0:T(8,128)(2,1)} %all-gather.6.cloned.1.call-done), kind=kOutput, calls=%fused_computation.2 | convolution fusion | flops 3759931392 | bytes 12058624 | tf_op jit(solution)/shard_map/td,tf->df/dot_general | solution.py:90
  326.0 0.2 all-to-all-done.6
  326.2 0.3 multiply_reduce_fusion
  326.5 0.8 add_convert_fusion
  327.2 0.6 slice.74
  (22 shorter events, 0.2 us)
Async XLA Ops:
  7.2 65.1 %all-gather.4.cloned.1.call-start = ((), (), s32[]{:S(2)}) async-start(), calls=%async_computation.8 | async-start | bytes 7798784 | tf_op jit(solution)/shard_map/all_gather | solution.py:53
  9.4 151.8 %reduce-scatter.2.cloned.1.call-start = ((), (), s32[]{:S(2)}) async-start(), calls=%async_computation.9 | async-start | bytes 15597568 | tf_op jit(solution)/shard_map/reduce_scatter | solution.py:58
  57.6 103.7 %copy-start.1 = (bf16[64,3584]{1,0:T(8,128)(2,1)S(1)}, bf16[64,3584]{1,0:T(8,128)(2,1)}, u32[]{:S(2)}) copy-start(bf16[64,3584]{1,0:T(8,128)(2,1)} %param.16) | copy-start | bytes 1376260
  57.6 103.7 %copy-start.2 = (bf16[64,3584]{1,0:T(8,128)(2,1)S(1)}, bf16[64,3584]{1,0:T(8,128)(2,1)}, u32[]{:S(2)}) copy-start(bf16[64,3584]{1,0:T(8,128)(2,1)} %param.15) | copy-start | bytes 1376260
  72.3 92.1 %copy-start = (bf16[8,8192]{1,0:T(8,128)(2,1)S(1)}, bf16[8,8192]{1,0:T(8,128)(2,1)}, u32[]{:S(2)}) copy-start(bf16[8,8192]{1,0:T(8,128)(2,1)} %param.12) | copy-start | bytes 393220
  72.3 113.5 %copy-start.4 = (f32[8192]{0:T(1024)S(1)}, f32[8192]{0:T(1024)}, u32[]{:S(2)}) copy-start(f32[8192]{0:T(1024)} %param.13) | copy-start | bytes 98308
  72.3 153.8 %all-gather.6.cloned.1.call-start = ((), (), s32[]{:S(2)}) async-start(), calls=%async_computation.10 | async-start | bytes 7798784 | tf_op jit(solution)/shard_map/all_gather | solution.py:60
  163.8 111.1 %all-gather.8.cloned.1.call-start = ((), (), s32[]{:S(2)}) async-start(), calls=%async_computation.11 | async-start | bytes 7798784 | tf_op jit(solution)/shard_map/all_gather | solution.py:61
  180.3 11.9 %all-to-all-start.4 = ((f32[8,1,128]{2,1,0:T(1,128)}), f32[8,1,128]{2,1,0:T(1,128)S(1)}, u32[]{:S(2)}, u32[]{:S(2)}) async-start(f32[8,1,128]{2,1,0:T(1,128)} %broadcast_in_dim.19), calls=%async_computation.5 | async-start | bytes 8192 | tf_op jit(solution)/shard_map/all_to_all | solution.py:25
  193.3 42.3 %all-to-all-start.3 = ((bf16[8,128,512]{2,1,0:T(8,128)(2,1)}), bf16[8,128,512]{2,1,0:T(8,128)(2,1)S(1)}, u32[]{:S(2)}, u32[]{:S(2)}) async-start(bf16[8,128,512]{2,1,0:T(8,128)(2,1)} %broadcast_in_dim.17), calls=%async_computation.4 | async-start | bytes 2097152 | tf_op jit(solution)/shard_map/all_to_all | solution.py:25
  286.1 24.5 %all-to-all-start.5 = ((bf16[8,136,512]{2,1,0:T(8,128)(2,1)}), bf16[8,136,512]{2,1,0:T(8,128)(2,1)S(1)}, u32[]{:S(2)}, u32[]{:S(2)}) async-start(bf16[8,136,512]{2,1,0:T(8,128)(2,1)} %pad_maximum_fusion), calls=%async_computation.6 | async-start | bytes 2228224 | tf_op jit(solution)/shard_map/all_to_all | solution.py:78
  292.5 8.7 %copy-start.5 = (bf16[1024,512]{1,0:T(8,128)(2,1)S(1)}, bf16[1024,512]{1,0:T(8,128)(2,1)}, u32[]{:S(2)}) copy-start(bf16[1024,512]{1,0:T(8,128)(2,1)} %get-tuple-element.39) | copy-start | bytes 3145732
  311.7 14.5 %all-to-all-start.6 = ((f32[16,9,512]{2,1,0:T(8,128)}), f32[16,9,512]{2,1,0:T(8,128)S(1)}, u32[]{:S(2)}, u32[]{:S(2)}) async-start(f32[16,9,512]{2,1,0:T(8,128)} %pad_maximum_fusion.1), calls=%async_computation.7 | async-start | bytes 1048576 | tf_op jit(solution)/shard_map/all_to_all | solution.py:87
  316.7 9.8 %copy-start.3 = (bf16[8,8192]{1,0:T(8,128)(2,1)S(1)}, bf16[8,8192]{1,0:T(8,128)(2,1)}, u32[]{:S(2)}) copy-start(bf16[8,8192]{1,0:T(8,128)(2,1)} %param.14) | copy-start | bytes 393220
Sparse Core Ops, SparseCore 0:
  10.2 61.9 all-gather.3
  74.7 86.5 reduce-scatter.1
  164.0 62.1 all-gather.5
  228.3 46.5 all-gather.7

commit v7 on v6

--- a/solution.py
+++ b/solution.py
@@ -56,13 +56,17 @@
     )
     hidden_piece, partial_grad = lax.optimization_barrier((hidden_piece, partial_grad))
     block_grad = lax.psum_scatter(partial_grad, "col", scatter_dimension=0, tiled=True)
+    down_total = jnp.einsum("tf,td->fd", hidden_piece, all_grad, preferred_element_type=jnp.float32)
+    down_total, block_grad = lax.optimization_barrier((down_total, block_grad))
     _, gate_block, up_block = swiglu_grads(block_grad, pre_gate, pre_up)
-    gate_piece = lax.all_gather(gate_block, "col", axis=0, tiled=True)
-    up_piece = lax.all_gather(up_block, "col", axis=0, tiled=True)
     all_tokens = row_gather(grid_tokens).astype(jnp.float32)
     all_scale = row_gather(grid_scale).reshape(-1, 1)
     all_normed = all_tokens * all_scale
     all_input = (all_normed * gain_tile).astype(jnp.bfloat16)
+    gate_piece = lax.all_gather(gate_block, "col", axis=0, tiled=True)
+    up_piece = lax.all_gather(up_block, "col", axis=0, tiled=True)
+    gate_total = jnp.einsum("td,tf->df", all_input, gate_piece, preferred_element_type=jnp.float32)
+    gate_total, up_piece = lax.optimization_barrier((gate_total, up_piece))
     new_rows = jnp.einsum("tf,df->td", gate_piece, gate_weight, preferred_element_type=jnp.float32)
     new_rows = new_rows + jnp.einsum(
         "tf,df->td", up_piece, up_weight, preferred_element_type=jnp.float32
@@ -87,9 +91,7 @@
     got2 = lax.all_to_all(sent2, "col", split_axis=0, concat_axis=0, tiled=True)
     normed_grad = got2[:, :mine, :].transpose(1, 0, 2).reshape(mine, cols * tile)
     grad_gain = got2[:, mine, :].reshape(cols * tile)
-    gate_total = jnp.einsum("td,tf->df", all_input, gate_piece, preferred_element_type=jnp.float32)
     up_total = jnp.einsum("td,tf->df", all_input, up_piece, preferred_element_type=jnp.float32)
-    down_total = jnp.einsum("tf,td->fd", hidden_piece, all_grad, preferred_element_type=jnp.float32)
     scaled_grad = normed_grad * gain
     inner = jnp.mean(scaled_grad * normed, axis=1, keepdims=True)
     grad_tokens = (

time: 335 us -> 335 us (level)
  blocking collectives: 53.3 us -> 77.5 us
  waiting for transfers between devices: 180 us -> 171 us
  matrix products: 55.4 us -> 46.9 us
  starting transfers between devices: 20.6 us -> 14.5 us
    all_to_all x0 -> x1, blocking collectives: none -> 24.3 us  [local(): got = lax.all_to_all(sent, 'row', split_axis=0, concat_axis=0, tiled=True)]
    all_gather x1, waiting for transfers between devices: 29.3 us -> 11.2 us  [local(): gate_piece = lax.all_gather(gate_block, 'col', axis=0, tiled=True)]
    all_to_all x2, waiting for transfers between devices: 6.36 us -> 24.1 us  [row_gather(): got = lax.all_to_all(copies, 'row', split_axis=0, concat_axis=0, tiled=True)]
    reduce_scatter x1, waiting for transfers between devices: 88.9 us -> 80.2 us  [local(): lax.psum_scatter(partial_grad, 'col', scatter_dimension=0, tiled=True)]
    all_to_all x1 -> x0, starting transfers between devices: 6.42 us -> none  [local(): got = lax.all_to_all(sent, 'row', split_axis=0, concat_axis=0, tiled=True)]
    dot_general x1, matrix products: 9.94 us -> 4.13 us  [local(): jnp.einsum('tf,df->td', up_piece, up_weight, preferred_element_type=jnp.f...]
  transfers between devices with their start and end apart: 8 -> 7, of which waited for: 7 -> 7; matrix products, arithmetic and copies ran while one was open for 14% -> 11% of each run, Pallas kernels for 0% -> 0%
where the time goes in v7:
time: 335 us
  waiting for transfers between devices  171 us (51%)
  blocking collectives  77.5 us (23%)
  matrix products  46.9 us (14%)
  starting transfers between devices  14.5 us (4%)
  between operations  14 us (4%)
  other arithmetic  7.45 us (2%)
    reduce_scatter x1, waiting for transfers between devices, local(): lax.psum_scatter(partial_grad, 'col', scatter_dimension=0, tiled=True)  80.2 us
    all_gather x1, waiting for transfers between devices, local(): up_piece = lax.all_gather(up_block, 'col', axis=0, tiled=True)  39.7 us
    all_to_all x1, blocking collectives, row_gather(): got = lax.all_to_all(copies, 'row', split_axis=0, concat_axis=0, tiled=True)  25 us
    all_to_all x1, blocking collectives, local(): got = lax.all_to_all(sent, 'row', split_axis=0, concat_axis=0, tiled=True)  24.3 us
    all_to_all x2, waiting for transfers between devices, row_gather(): got = lax.all_to_all(copies, 'row', split_axis=0, concat_axis=0, tiled=True)  24.1 us
    all_to_all x1, blocking collectives, local(): lax.all_to_all(packed, 'col', split_axis=1, concat_axis=0, tiled=True)  14.8 us
    all_gather x1, waiting for transfers between devices, local(): hidden_piece = lax.all_gather(hidden_block, 'col', axis=0, tiled=True)  14.7 us
    all_to_all x1, blocking collectives, local(): lax.all_to_all(grad_out, 'col', split_axis=1, concat_axis=0, tiled=True)  13.4 us
  transfers between devices with their start and end apart: 7, of which 7 were waited for; matrix products, arithmetic and copies ran while one was open for 11% of the time, Pallas kernels for 0%

profile of v7, /device:TPU:1, one launch (start us, length us, event | category | flops | bytes accessed | tf_op | source)
XLA Modules:
  0.0 334.6 jit_solution(16336424300861437451)
XLA Ops:
  7.2 0.0 all-gather.4.cloned.1.call-start
  7.2 2.2 fusion.4
  9.4 0.0 all-gather.4.cloned.1.call-update
  9.4 0.0 reduce-scatter.2.cloned.1.call-start
  9.5 13.4 %all_to_all.56 = bf16[8,16,512]{2,0,1:T(8,128)(2,1)S(1)} all-to-all(bf16[8,16,512]{2,0,1:T(8,128)(2,1)} %bitcast.46), channel_id=1, replica_groups=mesh['row'=8,'col'=16] {'col'}, dimensions={1} | all-to-all | bytes 262144 | tf_op jit(solution)/shard_map/all_to_all | solution.py:39
  22.9 0.1 broadcast_in_dim.15
  23.0 25.0 %all_to_all.57 = bf16[8,128,512]{2,1,0:T(8,128)(2,1)S(1)} all-to-all(bf16[8,128,512]{2,1,0:T(8,128)(2,1)S(1)} %broadcast_in_dim.15), channel_id=1, replica_groups=mesh['row'=8,'col'=16] {'row'}, dimensions={0} | all-to-all | bytes 2097152 | tf_op jit(solution)/shard_map/all_to_all | solution.py:25
  48.0 9.6 %fusion.13 = f32[1024,3584]{1,0:T(8,128)} fusion(bf16[1024,512]{1,0:T(8,128)(2,1)S(1)} %bitcast.41, bf16[3584,512]{1,0:T(8,128)(2,1)} %param.19), kind=kOutput, calls=%fused_computation.36 | convolution fusion | flops 3758096384 | bytes 19398656 | tf_op jit(solution)/shard_map/td,fd->tf/dot_general | solution.py:54
  57.6 14.7 %all-gather.4.cloned.1.call-done = bf16[1024,3584]{1,0:T(8,128)(2,1)} async-done(((bf16[64,3584]{1,0:T(8,128)(2,1)}), bf16[1024,3584]{1,0:T(8,128)(2,1)}) %all-gather.4.cloned.1.call-update) | async-done | bytes 7340048 | tf_op jit(solution)/shard_map/all_gather | solution.py:53
  72.3 0.0 reduce-scatter.2.cloned.1.call-update
  72.3 0.0 copy-start.1
  72.3 0.0 copy-start.2
  72.3 0.0 all-gather.6.cloned.1.call-start
  72.4 8.7 %fusion.14 = bf16[3584,512]{1,0:T(8,128)(2,1)} fusion(bf16[1024,3584]{1,0:T(8,128)(2,1)} %all-gather.4.cloned.1.call-done, bf16[1024,512]{1,0:T(8,128)(2,1)S(1)} %bitcast.42), kind=kOutput, calls=%fused_computation.37 | convolution fusion | flops 3758096384 | bytes 12058624 | tf_op jit(solution)/shard_map/tf,td->fd/dot_general | solution.py:59
  81.0 80.2 %reduce-scatter.2.cloned.1.call-done = f32[64,3584]{1,0:T(8,128)} async-done(((f32[1024,3584]{1,0:T(8,128)}), f32[64,3584]{1,0:T(8,128)}) %reduce-scatter.2.cloned.1.call-update) | async-done | bytes 917520 | tf_op jit(solution)/shard_map/reduce_scatter | solution.py:58
  161.3 0.0 copy-done.2
  161.3 2.5 multiply_convert_fusion
  163.8 0.0 all-gather.6.cloned.1.call-update
  163.8 0.0 all-gather.8.cloned.1.call-start
  163.9 0.5 all-gather.8.cloned.1.call-update
  164.5 0.2 multiply_reduce_fusion.1
  164.6 0.1 broadcast_in_dim.16
  164.8 14.8 %all_to_all.58 = f32[8,16,640]{2,0,1:T(8,128)S(1)} all-to-all(f32[8,16,640]{2,0,1:T(8,128)S(1)} %pad_maximum_fusion.2), channel_id=1, replica_groups=mesh['row'=8,'col'=16] {'col'}, dimensions={1} | all-to-all | bytes 655360 | tf_op jit(solution)/shard_map/all_to_all | solution.py:47
  179.6 0.1 slice_reduce_fusion
  179.7 0.6 broadcast_in_dim.19
  180.3 5.5 %all-to-all-start.4 = ((f32[8,1,128]{2,1,0:T(1,128)}), f32[8,1,128]{2,1,0:T(1,128)S(1)}, u32[]{:S(2)}, u32[]{:S(2)}) async-start(f32[8,1,128]{2,1,0:T(1,128)} %broadcast_in_dim.19), calls=%async_computation.5 | async-start | bytes 8192 | tf_op jit(solution)/shard_map/all_to_all | solution.py:25
  185.8 6.4 %all-to-all-done.4 = f32[8,1,128]{2,1,0:T(1,128)S(1)} async-done(((f32[8,1,128]{2,1,0:T(1,128)}), f32[8,1,128]{2,1,0:T(1,128)S(1)}, u32[]{:S(2)}, u32[]{:S(2)}) %all-to-all-start.4) | async-done | bytes 4128 | tf_op jit(solution)/shard_map/all_to_all | solution.py:25
  192.2 1.1 broadcast_in_dim.17
  193.3 3.6 %all-to-all-start.3 = ((bf16[8,128,512]{2,1,0:T(8,128)(2,1)}), bf16[8,128,512]{2,1,0:T(8,128)(2,1)S(1)}, u32[]{:S(2)}, u32[]{:S(2)}) async-start(bf16[8,128,512]{2,1,0:T(8,128)(2,1)} %broadcast_in_dim.17), calls=%async_computation.4 | async-start | bytes 2097152 | tf_op jit(solution)/shard_map/all_to_all | solution.py:25
  196.9 0.1 dynamic_slice.3
  197.0 17.7 %all-to-all-done.3 = bf16[8,128,512]{2,1,0:T(8,128)(2,1)S(1)} async-done(((bf16[8,128,512]{2,1,0:T(8,128)(2,1)}), bf16[8,128,512]{2,1,0:T(8,128)(2,1)S(1)}, u32[]{:S(2)}, u32[]{:S(2)}) %all-to-all-start.3) | async-done | bytes 1048608 | tf_op jit(solution)/shard_map/all_to_all | solution.py:25
  214.6 0.3 fusion.2
  214.9 11.2 %all-gather.6.cloned.1.call-done = bf16[1024,3584]{1,0:T(8,128)(2,1)} async-done(((bf16[64,3584]{1,0:T(8,128)(2,1)}), bf16[1024,3584]{1,0:T(8,128)(2,1)}) %all-gather.6.cloned.1.call-update) | async-done | bytes 7340048 | tf_op jit(solution)/shard_map/all_gather | solution.py:66
  226.2 8.5 %fusion.16 = bf16[512,3584]{1,0:T(8,128)(2,1)} fusion(bf16[1024,512]{1,0:T(8,128)(2,1)S(1)} %fusion.2, bf16[1024,3584]{1,0:T(8,128)(2,1)} %all-gather.6.cloned.1.call-done), kind=kOutput, calls=%fused_computation.39 | convolution fusion | flops 3758096384 | bytes 12058624 | tf_op jit(solution)/shard_map/td,tf->df/dot_general | solution.py:68
  234.7 39.7 %all-gather.8.cloned.1.call-done = bf16[1024,3584]{1,0:T(8,128)(2,1)} async-done(((bf16[64,3584]{1,0:T(8,128)(2,1)}), bf16[1024,3584]{1,0:T(8,128)(2,1)}) %all-gather.8.cloned.1.call-update) | async-done | bytes 7340048 | tf_op jit(solution)/shard_map/all_gather | solution.py:67
  274.4 7.5 %fusion.15 = f32[1024,512]{1,0:T(8,128)S(1)} fusion(bf16[1024,3584]{1,0:T(8,128)(2,1)} %all-gather.6.cloned.1.call-done, bf16[512,3584]{1,0:T(8,128)(2,1)} %param.17), kind=kOutput, calls=%fused_computation.38 | convolution fusion | flops 3758096384 | bytes 13107200 | tf_op jit(solution)/shard_map/tf,df->td/dot_general | solution.py:70
  281.9 4.1 %fusion.12 = (bf16[1024,512]{1,0:T(8,128)(2,1)S(1)}, f32[512]{0:T(512)S(1)}) fusion(f32[1024]{0:T(1024)S(1)} %bitcast.49, bf16[8,128,512]{2,1,0:T(8,128)(2,1)S(1)} %all-to-all-done.3, f32[1024,512]{1,0:T(8,128)S(1)} %fusion.15, bf16[1024,3584]{1,0:T(8,128)(2,1)S(1)} %copy-done.5, bf16[512,3584]{1,0:T(8,128)(2,1)S(1)} %copy-done.6), kind=kOutput, calls=%fused_computation.35 | convolution fusion | flops 3761241600 | bytes 15210496 | tf_op jit(solution)/shard_map/tf,df->td/dot_general | solution.py:71
  286.1 0.1 scatter.9
  286.2 0.1 pad_maximum_fusion
  286.3 24.3 %all_to_all.59 = bf16[8,136,512]{2,1,0:T(8,128)(2,1)S(1)} all-to-all(bf16[8,136,512]{2,1,0:T(8,128)(2,1)S(1)} %pad_maximum_fusion), channel_id=1, replica_groups=mesh['row'=8,'col'=16] {'row'}, dimensions={0} | all-to-all | bytes 2228224 | tf_op jit(solution)/shard_map/all_to_all | solution.py:82
  310.6 0.2 convert_reduce_fusion
  310.8 0.9 pad_maximum_fusion.1
  311.6 5.3 %all-to-all-start.6 = ((f32[16,9,512]{2,1,0:T(8,128)}), f32[16,9,512]{2,1,0:T(8,128)S(1)}, u32[]{:S(2)}, u32[]{:S(2)}) async-start(f32[16,9,512]{2,1,0:T(8,128)} %pad_maximum_fusion.1), calls=%async_computation.7 | async-start | bytes 1048576 | tf_op jit(solution)/shard_map/all_to_all | solution.py:91
  316.9 8.6 %convolution_convert_fusion = bf16[512,3584]{1,0:T(8,128)(2,1)} fusion(bf16[1024,512]{1,0:T(8,128)(2,1)S(1)} %fusion.2, bf16[1024,3584]{1,0:T(8,128)(2,1)} %all-gather.8.cloned.1.call-done), kind=kOutput, calls=%fused_computation | convolution fusion | flops 3759931392 | bytes 12058624 | tf_op jit(solution)/shard_map/td,tf->df/dot_general | solution.py:94
  325.5 0.9 all-to-all-done.6
  326.4 0.3 multiply_reduce_fusion
  326.7 0.8 add_convert_fusion
  327.5 0.6 slice.74
  (24 shorter events, 0.2 us)
Async XLA Ops:
  7.2 65.1 %all-gather.4.cloned.1.call-start = ((), (), s32[]{:S(2)}) async-start(), calls=%async_computation.8 | async-start | bytes 7798784 | tf_op jit(solution)/shard_map/all_gather | solution.py:53
  9.4 151.8 %reduce-scatter.2.cloned.1.call-start = ((), (), s32[]{:S(2)}) async-start(), calls=%async_computation.9 | async-start | bytes 15597568 | tf_op jit(solution)/shard_map/reduce_scatter | solution.py:58
  72.3 89.0 %copy-start.1 = (bf16[64,3584]{1,0:T(8,128)(2,1)S(1)}, bf16[64,3584]{1,0:T(8,128)(2,1)}, u32[]{:S(2)}) copy-start(bf16[64,3584]{1,0:T(8,128)(2,1)} %param.16) | copy-start | bytes 1376260
  72.3 89.0 %copy-start.2 = (bf16[64,3584]{1,0:T(8,128)(2,1)S(1)}, bf16[64,3584]{1,0:T(8,128)(2,1)}, u32[]{:S(2)}) copy-start(bf16[64,3584]{1,0:T(8,128)(2,1)} %param.15) | copy-start | bytes 1376260
  72.3 153.9 %all-gather.6.cloned.1.call-start = ((), (), s32[]{:S(2)}) async-start(), calls=%async_computation.10 | async-start | bytes 7798784 | tf_op jit(solution)/shard_map/all_gather | solution.py:66
  81.0 83.4 %copy-start = (bf16[8,8192]{1,0:T(8,128)(2,1)S(1)}, bf16[8,8192]{1,0:T(8,128)(2,1)}, u32[]{:S(2)}) copy-start(bf16[8,8192]{1,0:T(8,128)(2,1)} %param.12) | copy-start | bytes 393220
  163.8 33.1 %copy-start.4 = (f32[8192]{0:T(1024)S(1)}, f32[8192]{0:T(1024)}, u32[]{:S(2)}) copy-start(f32[8192]{0:T(1024)} %param.13) | copy-start | bytes 98308
  163.8 110.5 %all-gather.8.cloned.1.call-start = ((), (), s32[]{:S(2)}) async-start(), calls=%async_computation.11 | async-start | bytes 7798784 | tf_op jit(solution)/shard_map/all_gather | solution.py:67
  180.3 11.9 %all-to-all-start.4 = ((f32[8,1,128]{2,1,0:T(1,128)}), f32[8,1,128]{2,1,0:T(1,128)S(1)}, u32[]{:S(2)}, u32[]{:S(2)}) async-start(f32[8,1,128]{2,1,0:T(1,128)} %broadcast_in_dim.19), calls=%async_computation.5 | async-start | bytes 8192 | tf_op jit(solution)/shard_map/all_to_all | solution.py:25
  193.3 21.3 %all-to-all-start.3 = ((bf16[8,128,512]{2,1,0:T(8,128)(2,1)}), bf16[8,128,512]{2,1,0:T(8,128)(2,1)S(1)}, u32[]{:S(2)}, u32[]{:S(2)}) async-start(bf16[8,128,512]{2,1,0:T(8,128)(2,1)} %broadcast_in_dim.17), calls=%async_computation.4 | async-start | bytes 2097152 | tf_op jit(solution)/shard_map/all_to_all | solution.py:25
  274.4 7.5 %copy-start.5 = (bf16[1024,3584]{1,0:T(8,128)(2,1)S(1)}, bf16[1024,3584]{1,0:T(8,128)(2,1)}, u32[]{:S(2)}) copy-start(bf16[1024,3584]{1,0:T(8,128)(2,1)} %all-gather.8.cloned.1.call-done) | copy-start | bytes 22020100
  274.4 7.5 %copy-start.6 = (bf16[512,3584]{1,0:T(8,128)(2,1)S(1)}, bf16[512,3584]{1,0:T(8,128)(2,1)}, u32[]{:S(2)}) copy-start(bf16[512,3584]{1,0:T(8,128)(2,1)} %param.18) | copy-start | bytes 11010052
  311.6 14.7 %all-to-all-start.6 = ((f32[16,9,512]{2,1,0:T(8,128)}), f32[16,9,512]{2,1,0:T(8,128)S(1)}, u32[]{:S(2)}, u32[]{:S(2)}) async-start(f32[16,9,512]{2,1,0:T(8,128)} %pad_maximum_fusion.1), calls=%async_computation.7 | async-start | bytes 1048576 | tf_op jit(solution)/shard_map/all_to_all | solution.py:91
  316.9 9.8 %copy-start.3 = (bf16[8,8192]{1,0:T(8,128)(2,1)S(1)}, bf16[8,8192]{1,0:T(8,128)(2,1)}, u32[]{:S(2)}) copy-start(bf16[8,8192]{1,0:T(8,128)(2,1)} %param.14) | copy-start | bytes 393220
Sparse Core Ops, SparseCore 0:
  10.2 61.9 all-gather.3
  74.7 86.5 reduce-scatter.1
  164.0 62.1 all-gather.5
  227.7 46.5 all-gather.7

commit v8 on v7

--- a/solution.py
+++ b/solution.py
@@ -50,7 +50,8 @@
     grid_scale = grid[:, tile : tile + 1].reshape(1, cols * mine_rows)
     all_grad = row_gather(grid_grad)
     hidden_block = swiglu_grads(jnp.zeros(pre_gate.shape, jnp.float32), pre_gate, pre_up)[0]
-    hidden_piece = lax.all_gather(hidden_block, "col", axis=0, tiled=True)
+    split = (hidden_block.shape[1] // 256) * 128
+    hidden_piece = lax.all_gather(hidden_block[:, :split], "col", axis=0, tiled=True)
     partial_grad = jnp.einsum(
         "td,fd->tf", all_grad, down_weight, preferred_element_type=jnp.float32
     )
@@ -67,6 +68,8 @@
     up_piece = lax.all_gather(up_block, "col", axis=0, tiled=True)
     gate_total = jnp.einsum("td,tf->df", all_input, gate_piece, preferred_element_type=jnp.float32)
     gate_total, up_piece = lax.optimization_barrier((gate_total, up_piece))
+    late_block, up_piece = lax.optimization_barrier((hidden_block[:, split:], up_piece))
+    late_piece = lax.all_gather(late_block, "col", axis=0, tiled=True)
     new_rows = jnp.einsum("tf,df->td", gate_piece, gate_weight, preferred_element_type=jnp.float32)
     new_rows = new_rows + jnp.einsum(
         "tf,df->td", up_piece, up_weight, preferred_element_type=jnp.float32
@@ -92,6 +95,7 @@
     normed_grad = got2[:, :mine, :].transpose(1, 0, 2).reshape(mine, cols * tile)
     grad_gain = got2[:, mine, :].reshape(cols * tile)
     up_total = jnp.einsum("td,tf->df", all_input, up_piece, preferred_element_type=jnp.float32)
+    down_late = jnp.einsum("tf,td->fd", late_piece, all_grad, preferred_element_type=jnp.float32)
     scaled_grad = normed_grad * gain
     inner = jnp.mean(scaled_grad * normed, axis=1, keepdims=True)
     grad_tokens = (
@@ -102,7 +106,7 @@
         grad_gain,
         gate_total.astype(jnp.bfloat16),
         up_total.astype(jnp.bfloat16),
-        down_total.astype(jnp.bfloat16),
+        jnp.concatenate([down_total, down_late], axis=0).astype(jnp.bfloat16),
     )
 
 

time: 335 us -> 334 us (level)
  waiting for transfers between devices: 171 us -> 161 us
  other arithmetic: 7.45 us -> 12.7 us
    all_gather x1 -> x2, waiting for transfers between devices: 14.7 us -> 3.11 us  [the longest x1 3.11 us: local(): lax.all_gather(hidden_block[:, :split], 'col', axis=0, tiled=True)]
    dot_general x0 -> x1, matrix products: none -> 4.43 us  [local(): jnp.einsum('tf,td->fd', late_piece, all_grad, preferred_element_type=jnp....]
    dot_general x1, matrix products: 8.66 us -> 4.5 us  [local(): jnp.einsum('tf,td->fd', hidden_piece, all_grad, preferred_element_type=jn...]
    reduce_scatter x1, waiting for transfers between devices: 80.2 us -> 84.1 us  [local(): lax.psum_scatter(partial_grad, 'col', scatter_dimension=0, tiled=True)]
  transfers between devices with their start and end apart: 7 -> 8, of which waited for: 7 -> 7; matrix products, arithmetic and copies ran while one was open for 11% -> 16% of each run, Pallas kernels for 0% -> 0%
where the time goes in v8:
time: 334 us; the launch traced here: 333 us
  waiting for transfers between devices  161 us (48%)
  blocking collectives  76.2 us (23%)
  matrix products  48.8 us (15%)
  starting transfers between devices  15.1 us (5%)
  between operations  14 us (4%)
  other arithmetic  12.7 us (4%)
  local copies, waits for them, and re-layouts  5.33 us (2%)
    reduce_scatter x1, waiting for transfers between devices, local(): lax.psum_scatter(partial_grad, 'col', scatter_dimension=0, tiled=True)  84.1 us
    all_gather x1, waiting for transfers between devices, local(): up_piece = lax.all_gather(up_block, 'col', axis=0, tiled=True)  39 us
    all_to_all x1, blocking collectives, local(): got = lax.all_to_all(sent, 'row', split_axis=0, concat_axis=0, tiled=True)  24.8 us
    all_to_all x1, blocking collectives, row_gather(): got = lax.all_to_all(copies, 'row', split_axis=0, concat_axis=0, tiled=True)  23.6 us
    all_to_all x2, waiting for transfers between devices, row_gather(): got = lax.all_to_all(copies, 'row', split_axis=0, concat_axis=0, tiled=True)  23.2 us
    all_to_all x1, blocking collectives, local(): lax.all_to_all(packed, 'col', split_axis=1, concat_axis=0, tiled=True)  14.3 us
    all_to_all x1, blocking collectives, local(): lax.all_to_all(grad_out, 'col', split_axis=1, concat_axis=0, tiled=True)  13.4 us
    all_gather x1, waiting for transfers between devices, local(): gate_piece = lax.all_gather(gate_block, 'col', axis=0, tiled=True)  10.4 us
  transfers between devices with their start and end apart: 8, of which 7 were waited for; matrix products, arithmetic and copies ran while one was open for 16% of the time, Pallas kernels for 0%

profile of v8, /device:TPU:1, one launch (start us, length us, event | category | flops | bytes accessed | tf_op | source)
XLA Modules:
  0.0 333.4 jit_solution(18214211032560894156)
XLA Ops:
  7.2 0.0 all-gather.5.cloned.1.call-start
  7.2 1.4 fusion.4
  8.6 0.8 fusion.13
  9.4 0.0 all-gather.5.cloned.1.call-update
  9.5 0.0 reduce-scatter.2.cloned.1.call-start
  9.5 13.4 %all_to_all.56 = bf16[8,16,512]{2,0,1:T(8,128)(2,1)S(1)} all-to-all(bf16[8,16,512]{2,0,1:T(8,128)(2,1)} %bitcast.49), channel_id=1, replica_groups=mesh['row'=8,'col'=16] {'col'}, dimensions={1} | all-to-all | bytes 262144 | tf_op jit(solution)/shard_map/all_to_all | solution.py:39
  22.9 0.1 broadcast_in_dim.15
  23.0 23.6 %all_to_all.57 = bf16[8,128,512]{2,1,0:T(8,128)(2,1)S(1)} all-to-all(bf16[8,128,512]{2,1,0:T(8,128)(2,1)S(1)} %broadcast_in_dim.15), channel_id=1, replica_groups=mesh['row'=8,'col'=16] {'row'}, dimensions={0} | all-to-all | bytes 2097152 | tf_op jit(solution)/shard_map/all_to_all | solution.py:25
  46.6 1.0 copy-done.4
  47.6 9.5 %fusion.14 = f32[1024,3584]{1,0:T(8,128)} fusion(bf16[1024,512]{1,0:T(8,128)(2,1)S(1)} %bitcast.42, bf16[3584,512]{1,0:T(8,128)(2,1)} %param.19), kind=kOutput, calls=%fused_computation.39 | convolution fusion | flops 3758096384 | bytes 19398656 | tf_op jit(solution)/shard_map/td,fd->tf/dot_general | solution.py:55
  57.1 3.1 all-gather.5.cloned.1.call-done
  60.2 0.0 all-gather.7.cloned.1.call-start
  60.3 4.5 %fusion.15 = bf16[1792,512]{1,0:T(8,128)(2,1)S(1)} fusion(bf16[1024,1792]{1,0:T(8,128)(2,1)} %all-gather.5.cloned.1.call-done, bf16[1024,512]{1,0:T(8,128)(2,1)} %bitcast.43), kind=kOutput, calls=%fused_computation.40 | convolution fusion | flops 1879048192 | bytes 6553600 | tf_op jit(solution)/shard_map/tf,td->fd/dot_general | solution.py:60
  64.8 84.1 %reduce-scatter.2.cloned.1.call-done = f32[64,3584]{1,0:T(8,128)} async-done(((f32[1024,3584]{1,0:T(8,128)}), f32[64,3584]{1,0:T(8,128)}) %reduce-scatter.2.cloned.1.call-update) | async-done | bytes 917520 | tf_op jit(solution)/shard_map/reduce_scatter | solution.py:59
  149.0 2.5 multiply_convert_fusion
  151.5 0.0 all-gather.9.cloned.1.call-start
  151.6 0.5 all-gather.9.cloned.1.call-update
  152.1 0.2 multiply_reduce_fusion.1
  152.3 0.1 broadcast_in_dim.16
  152.4 14.3 %all_to_all.58 = f32[8,16,640]{2,0,1:T(8,128)S(1)} all-to-all(f32[8,16,640]{2,0,1:T(8,128)S(1)} %pad_maximum_fusion.3), channel_id=1, replica_groups=mesh['row'=8,'col'=16] {'col'}, dimensions={1} | all-to-all | bytes 655360 | tf_op jit(solution)/shard_map/all_to_all | solution.py:47
  166.8 0.1 slice_reduce_fusion
  166.9 0.6 broadcast_in_dim.19
  167.5 6.1 %all-to-all-start.4 = ((f32[8,1,128]{2,1,0:T(1,128)}), f32[8,1,128]{2,1,0:T(1,128)S(1)}, u32[]{:S(2)}, u32[]{:S(2)}) async-start(f32[8,1,128]{2,1,0:T(1,128)} %broadcast_in_dim.19), calls=%async_computation.5 | async-start | bytes 8192 | tf_op jit(solution)/shard_map/all_to_all | solution.py:25
  173.6 6.4 %all-to-all-done.4 = f32[8,1,128]{2,1,0:T(1,128)S(1)} async-done(((f32[8,1,128]{2,1,0:T(1,128)}), f32[8,1,128]{2,1,0:T(1,128)S(1)}, u32[]{:S(2)}, u32[]{:S(2)}) %all-to-all-start.4) | async-done | bytes 4128 | tf_op jit(solution)/shard_map/all_to_all | solution.py:25
  180.0 1.1 broadcast_in_dim.17
  181.1 3.6 %all-to-all-start.3 = ((bf16[8,128,512]{2,1,0:T(8,128)(2,1)}), bf16[8,128,512]{2,1,0:T(8,128)(2,1)S(1)}, u32[]{:S(2)}, u32[]{:S(2)}) async-start(bf16[8,128,512]{2,1,0:T(8,128)(2,1)} %broadcast_in_dim.17), calls=%async_computation.4 | async-start | bytes 2097152 | tf_op jit(solution)/shard_map/all_to_all | solution.py:25
  184.6 0.2 all-gather.11.cloned.1.call-start
  184.9 0.8 dynamic_slice.3
  185.6 16.7 %all-to-all-done.3 = bf16[8,128,512]{2,1,0:T(8,128)(2,1)S(1)} async-done(((bf16[8,128,512]{2,1,0:T(8,128)(2,1)}), bf16[8,128,512]{2,1,0:T(8,128)(2,1)S(1)}, u32[]{:S(2)}, u32[]{:S(2)}) %all-to-all-start.3) | async-done | bytes 1048608 | tf_op jit(solution)/shard_map/all_to_all | solution.py:25
  202.4 1.3 fusion.2
  203.7 10.4 %all-gather.7.cloned.1.call-done = bf16[1024,3584]{1,0:T(8,128)(2,1)} async-done(((bf16[64,3584]{1,0:T(8,128)(2,1)}), bf16[1024,3584]{1,0:T(8,128)(2,1)}) %all-gather.7.cloned.1.call-update) | async-done | bytes 7340048 | tf_op jit(solution)/shard_map/all_gather | solution.py:67
  214.1 9.3 %fusion.17 = bf16[512,3584]{1,0:T(8,128)(2,1)} fusion(bf16[1024,512]{1,0:T(8,128)(2,1)} %fusion.2, bf16[1024,3584]{1,0:T(8,128)(2,1)} %all-gather.7.cloned.1.call-done), kind=kOutput, calls=%fused_computation.42 | convolution fusion | flops 3758096384 | bytes 12058624 | tf_op jit(solution)/shard_map/td,tf->df/dot_general | solution.py:69
  223.3 39.0 %all-gather.9.cloned.1.call-done = bf16[1024,3584]{1,0:T(8,128)(2,1)} async-done(((bf16[64,3584]{1,0:T(8,128)(2,1)}), bf16[1024,3584]{1,0:T(8,128)(2,1)}) %all-gather.9.cloned.1.call-update) | async-done | bytes 7340048 | tf_op jit(solution)/shard_map/all_gather | solution.py:68
  262.3 7.5 %fusion.16 = f32[1024,512]{1,0:T(8,128)S(1)} fusion(bf16[1024,3584]{1,0:T(8,128)(2,1)} %all-gather.7.cloned.1.call-done, bf16[512,3584]{1,0:T(8,128)(2,1)} %param.17), kind=kOutput, calls=%fused_computation.41 | convolution fusion | flops 3758096384 | bytes 13107200 | tf_op jit(solution)/shard_map/tf,df->td/dot_general | solution.py:73
  269.9 5.1 %fusion.12 = (bf16[1024,512]{1,0:T(8,128)(2,1)}, f32[512]{0:T(512)S(1)}) fusion(f32[1024]{0:T(1024)S(1)} %bitcast.52, bf16[8,128,512]{2,1,0:T(8,128)(2,1)S(1)} %all-to-all-done.3, f32[1024,512]{1,0:T(8,128)S(1)} %fusion.16, bf16[1024,3584]{1,0:T(8,128)(2,1)S(1)} %copy-done.5, bf16[512,3584]{1,0:T(8,128)(2,1)S(1)} %copy-done.6), kind=kOutput, calls=%fused_computation.37 | convolution fusion | flops 3761241600 | bytes 15210496 | tf_op jit(solution)/shard_map/tf,df->td/dot_general | solution.py:74
  275.0 0.1 scatter.9
  275.1 1.4 pad_maximum_fusion.1
  276.5 24.8 %all_to_all.59 = bf16[8,136,512]{2,1,0:T(8,128)(2,1)S(1)} all-to-all(bf16[8,136,512]{2,1,0:T(8,128)(2,1)S(1)} %pad_maximum_fusion.1), channel_id=1, replica_groups=mesh['row'=8,'col'=16] {'row'}, dimensions={0} | all-to-all | bytes 2228224 | tf_op jit(solution)/shard_map/all_to_all | solution.py:85
  301.3 0.2 convert_reduce_fusion
  301.5 0.9 pad_maximum_fusion.2
  302.4 5.1 %all-to-all-start.6 = ((f32[16,9,512]{2,1,0:T(8,128)}), f32[16,9,512]{2,1,0:T(8,128)S(1)}, u32[]{:S(2)}, u32[]{:S(2)}) async-start(f32[16,9,512]{2,1,0:T(8,128)} %pad_maximum_fusion.2), calls=%async_computation.7 | async-start | bytes 1048576 | tf_op jit(solution)/shard_map/all_to_all | solution.py:94
  307.5 8.5 %convolution_convert_fusion = bf16[512,3584]{1,0:T(8,128)(2,1)} fusion(bf16[1024,512]{1,0:T(8,128)(2,1)S(1)} %copy-done.3, bf16[1024,3584]{1,0:T(8,128)(2,1)} %all-gather.9.cloned.1.call-done), kind=kOutput, calls=%fused_computation | convolution fusion | flops 3759931392 | bytes 12058624 | tf_op jit(solution)/shard_map/td,tf->df/dot_general | solution.py:97
  316.0 0.9 all-to-all-done.6
  317.0 0.6 slice.84
  317.6 1.0 multiply_reduce_fusion
  318.6 1.7 add_convert_fusion
  320.3 4.4 %convolution_convert_fusion.1 = bf16[1792,512]{1,0:T(8,128)(2,1)S(1)} fusion(bf16[1024,1792]{1,0:T(8,128)(2,1)} %all-gather.11.cloned.1.call-done, bf16[1024,512]{1,0:T(8,128)(2,1)} %bitcast.44), kind=kOutput, calls=%fused_computation.2 | convolution fusion | flops 1879965696 | bytes 6553600 | tf_op jit(solution)/shard_map/tf,td->fd/dot_general | solution.py:98
  324.8 2.1 pad_maximum_fusion
  (30 shorter events, 0.3 us)
Async XLA Ops:
  7.2 53.0 %all-gather.5.cloned.1.call-start = ((), (), s32[]{:S(2)}) async-start(), calls=%async_computation.8 | async-start | bytes 3899392 | tf_op jit(solution)/shard_map/all_gather | solution.py:54
  9.5 139.5 %reduce-scatter.2.cloned.1.call-start = ((), (), s32[]{:S(2)}) async-start(), calls=%async_computation.9 | async-start | bytes 15597568 | tf_op jit(solution)/shard_map/reduce_scatter | solution.py:59
  46.6 1.0 copy-start.4
  60.2 88.7 %copy-start.1 = (bf16[64,3584]{1,0:T(8,128)(2,1)S(1)}, bf16[64,3584]{1,0:T(8,128)(2,1)}, u32[]{:S(2)}) copy-start(bf16[64,3584]{1,0:T(8,128)(2,1)} %param.16) | copy-start | bytes 1376260
  60.2 88.7 %copy-start.2 = (bf16[64,3584]{1,0:T(8,128)(2,1)S(1)}, bf16[64,3584]{1,0:T(8,128)(2,1)}, u32[]{:S(2)}) copy-start(bf16[64,3584]{1,0:T(8,128)(2,1)} %param.15) | copy-start | bytes 1376260
  60.2 153.8 %all-gather.7.cloned.1.call-start = ((), (), s32[]{:S(2)}) async-start(), calls=%async_computation.10 | async-start | bytes 7798784 | tf_op jit(solution)/shard_map/all_gather | solution.py:67
  64.8 87.3 %copy-start = (bf16[8,8192]{1,0:T(8,128)(2,1)S(1)}, bf16[8,8192]{1,0:T(8,128)(2,1)}, u32[]{:S(2)}) copy-start(bf16[8,8192]{1,0:T(8,128)(2,1)} %param.12) | copy-start | bytes 393220
  151.5 110.8 %all-gather.9.cloned.1.call-start = ((), (), s32[]{:S(2)}) async-start(), calls=%async_computation.11 | async-start | bytes 7798784 | tf_op jit(solution)/shard_map/all_gather | solution.py:68
  167.5 12.5 %all-to-all-start.4 = ((f32[8,1,128]{2,1,0:T(1,128)}), f32[8,1,128]{2,1,0:T(1,128)S(1)}, u32[]{:S(2)}, u32[]{:S(2)}) async-start(f32[8,1,128]{2,1,0:T(1,128)} %broadcast_in_dim.19), calls=%async_computation.5 | async-start | bytes 8192 | tf_op jit(solution)/shard_map/all_to_all | solution.py:25
  181.1 21.3 %all-to-all-start.3 = ((bf16[8,128,512]{2,1,0:T(8,128)(2,1)}), bf16[8,128,512]{2,1,0:T(8,128)(2,1)S(1)}, u32[]{:S(2)}, u32[]{:S(2)}) async-start(bf16[8,128,512]{2,1,0:T(8,128)(2,1)} %broadcast_in_dim.17), calls=%async_computation.4 | async-start | bytes 2097152 | tf_op jit(solution)/shard_map/all_to_all | solution.py:25
  184.6 135.7 %all-gather.11.cloned.1.call-start = ((), (), s32[]{:S(2)}) async-start(), calls=%async_computation.12 | async-start | bytes 3899392 | tf_op jit(solution)/shard_map/all_gather | solution.py:72
  262.3 7.5 %copy-start.5 = (bf16[1024,3584]{1,0:T(8,128)(2,1)S(1)}, bf16[1024,3584]{1,0:T(8,128)(2,1)}, u32[]{:S(2)}) copy-start(bf16[1024,3584]{1,0:T(8,128)(2,1)} %all-gather.9.cloned.1.call-done) | copy-start | bytes 22020100
  262.3 7.5 %copy-start.6 = (bf16[512,3584]{1,0:T(8,128)(2,1)S(1)}, bf16[512,3584]{1,0:T(8,128)(2,1)}, u32[]{:S(2)}) copy-start(bf16[512,3584]{1,0:T(8,128)(2,1)} %param.18) | copy-start | bytes 11010052
  275.1 32.4 %copy-start.3 = (bf16[1024,512]{1,0:T(8,128)(2,1)S(1)}, bf16[1024,512]{1,0:T(8,128)(2,1)}, u32[]{:S(2)}) copy-start(bf16[1024,512]{1,0:T(8,128)(2,1)} %fusion.2) | copy-start | bytes 3145732
  302.4 14.6 %all-to-all-start.6 = ((f32[16,9,512]{2,1,0:T(8,128)}), f32[16,9,512]{2,1,0:T(8,128)S(1)}, u32[]{:S(2)}, u32[]{:S(2)}) async-start(f32[16,9,512]{2,1,0:T(8,128)} %pad_maximum_fusion.2), calls=%async_computation.7 | async-start | bytes 1048576 | tf_op jit(solution)/shard_map/all_to_all | solution.py:94
Sparse Core Ops, SparseCore 0:
  10.2 49.8 all-gather.4
  62.6 86.3 reduce-scatter.1
  151.6 62.3 all-gather.6
  215.6 46.6 all-gather.8
  263.8 49.1 all-gather.10

commit v9 on v8

--- a/solution.py
+++ b/solution.py
@@ -82,7 +82,13 @@
     extra = jnp.zeros((rows, 8, tile), jnp.bfloat16)
     extra = extra.at[:, 0, :].set(gain_high).at[:, 1, :].set(gain_low)
     sent = jnp.concatenate([blocks, extra], axis=1)
-    got = lax.all_to_all(sent, "row", split_axis=0, concat_axis=0, tiled=True)
+    me = lax.axis_index("row")
+    arrived = [lax.dynamic_index_in_dim(sent, me, 0, keepdims=False)]
+    for k in range(1, rows):
+        piece = lax.dynamic_index_in_dim(sent, (me + k) % rows, 0, keepdims=False)
+        arrived.append(lax.ppermute(piece, "row", [(i, (i + k) % rows) for i in range(rows)]))
+    ahead = jnp.stack([arrived[(-j) % rows] for j in range(rows)])
+    got = jnp.roll(ahead, me, axis=0)
     summed = jnp.sum(got.astype(jnp.float32), axis=0)
     grid_back = summed[: tokens_all // rows]
     gain_tile_grad = summed[tokens_all // rows] + summed[tokens_all // rows + 1]

time: 334 us -> 342 us (1.024)
  blocking collectives: 76.2 us -> 51.5 us
  starting transfers between devices: 15.1 us -> 29.7 us
  waiting for transfers between devices: 161 us -> 172 us
  local copies, waits for them, and re-layouts: 5.33 us -> 13 us
    all_to_all x1 -> x0, blocking collectives: 24.8 us -> none  [local(): got = lax.all_to_all(sent, 'row', split_axis=0, concat_axis=0, tiled=True)]
    ppermute x0 -> x7, starting transfers between devices: none -> 14 us  [local(): lax.ppermute(piece, 'row', [(i, (i + k) % rows) for i in range(rows)])]
    unnamed x14 -> x33, local copies, waits for them, and re-layouts: 1.01 us -> 8.73 us
    ppermute x0 -> x7, waiting for transfers between devices: none -> 4.7 us  [local(): lax.ppermute(piece, 'row', [(i, (i + k) % rows) for i in range(rows)])]
  transfers between devices with their start and end apart: 8 -> 15, of which waited for: 7 -> 10; matrix products, arithmetic and copies ran while one was open for 16% -> 15% of each run, Pallas kernels for 0% -> 0%
where the time goes in v9:
time: 342 us; the launch traced here: 341 us
  waiting for transfers between devices  172 us (50%)
  blocking collectives  51.5 us (15%)
  matrix products  48.3 us (14%)
  starting transfers between devices  29.7 us (9%)
  between operations  14.1 us (4%)
  local copies, waits for them, and re-layouts  13 us (4%)
  other arithmetic  12.2 us (4%)
    reduce_scatter x1, waiting for transfers between devices, local(): lax.psum_scatter(partial_grad, 'col', scatter_dimension=0, tiled=True)  83 us
    all_gather x1, waiting for transfers between devices, local(): up_piece = lax.all_gather(up_block, 'col', axis=0, tiled=True)  40.3 us
    all_to_all x1, blocking collectives, row_gather(): got = lax.all_to_all(copies, 'row', split_axis=0, concat_axis=0, tiled=True)  24 us
    all_to_all x2, waiting for transfers between devices, row_gather(): got = lax.all_to_all(copies, 'row', split_axis=0, concat_axis=0, tiled=True)  24 us
    all_to_all x1, blocking collectives, local(): lax.all_to_all(packed, 'col', split_axis=1, concat_axis=0, tiled=True)  14.2 us
    ppermute x7, starting transfers between devices, local(): lax.ppermute(piece, 'row', [(i, (i + k) % rows) for i in range(rows)])  14 us
    all_to_all x1, blocking collectives, local(): lax.all_to_all(grad_out, 'col', split_axis=1, concat_axis=0, tiled=True)  13.2 us
    all_gather x1, waiting for transfers between devices, local(): gate_piece = lax.all_gather(gate_block, 'col', axis=0, tiled=True)  11.2 us
  transfers between devices with their start and end apart: 15, of which 10 were waited for; matrix products, arithmetic and copies ran while one was open for 15% of the time, Pallas kernels for 0%

profile of v9, /device:TPU:1, one launch (start us, length us, event | category | flops | bytes accessed | tf_op | source)
XLA Modules:
  0.0 341.3 jit_solution(1857959050181184331)
XLA Ops:
  7.2 1.5 fusion.4
  8.7 0.8 fusion.28
  9.6 13.2 %all_to_all.51 = bf16[8,16,512]{2,0,1:T(8,128)(2,1)S(1)} all-to-all(bf16[8,16,512]{2,0,1:T(8,128)(2,1)S(1)} %bitcast.86), channel_id=1, replica_groups=mesh['row'=8,'col'=16] {'col'}, dimensions={1} | all-to-all | bytes 262144 | tf_op jit(solution)/shard_map/all_to_all | solution.py:39
  22.8 24.0 %all_to_all.52 = bf16[8,128,512]{2,1,0:T(8,128)(2,1)S(1)} all-to-all(bf16[8,128,512]{2,1,0:T(8,128)(2,1)S(1)} %broadcast_in_dim.15), channel_id=1, replica_groups=mesh['row'=8,'col'=16] {'row'}, dimensions={0} | all-to-all | bytes 2097152 | tf_op jit(solution)/shard_map/all_to_all | solution.py:25
  46.9 9.9 %fusion.29 = f32[1024,3584]{1,0:T(8,128)} fusion(bf16[1024,512]{1,0:T(8,128)(2,1)S(1)} %bitcast.80, bf16[3584,512]{1,0:T(8,128)(2,1)} %param.19), kind=kOutput, calls=%fused_computation.85 | convolution fusion | flops 3758096384 | bytes 19398656 | tf_op jit(solution)/shard_map/td,fd->tf/dot_general | solution.py:55
  56.8 3.4 %all-gather.5.cloned.1.call-done = bf16[1024,1792]{1,0:T(8,128)(2,1)} async-done(((bf16[64,1792]{1,0:T(8,128)(2,1)}), bf16[1024,1792]{1,0:T(8,128)(2,1)}) %all-gather.5.cloned.1.call-update) | async-done | bytes 3670032 | tf_op jit(solution)/shard_map/all_gather | solution.py:54
  60.3 5.5 %fusion.30 = bf16[1792,512]{1,0:T(8,128)(2,1)} fusion(bf16[1024,1792]{1,0:T(8,128)(2,1)} %all-gather.5.cloned.1.call-done, bf16[1024,512]{1,0:T(8,128)(2,1)S(1)} %bitcast.81), kind=kOutput, calls=%fused_computation.86 | convolution fusion | flops 1879048192 | bytes 6553600 | tf_op jit(solution)/shard_map/tf,td->fd/dot_general | solution.py:60
  65.8 83.0 %reduce-scatter.2.cloned.1.call-done = f32[64,3584]{1,0:T(8,128)} async-done(((f32[1024,3584]{1,0:T(8,128)}), f32[64,3584]{1,0:T(8,128)}) %reduce-scatter.2.cloned.1.call-update) | async-done | bytes 917520 | tf_op jit(solution)/shard_map/reduce_scatter | solution.py:59
  148.7 2.5 multiply_convert_fusion
  152.2 14.2 %all_to_all.53 = f32[8,16,640]{2,0,1:T(8,128)S(1)} all-to-all(f32[8,16,640]{2,0,1:T(8,128)S(1)} %pad_maximum_fusion.2), channel_id=1, replica_groups=mesh['row'=8,'col'=16] {'col'}, dimensions={1} | all-to-all | bytes 655360 | tf_op jit(solution)/shard_map/all_to_all | solution.py:47
  167.2 6.2 %all-to-all-start.4 = ((f32[8,1,128]{2,1,0:T(1,128)}), f32[8,1,128]{2,1,0:T(1,128)S(1)}, u32[]{:S(2)}, u32[]{:S(2)}) async-start(f32[8,1,128]{2,1,0:T(1,128)} %broadcast_in_dim.19), calls=%async_computation.5 | async-start | bytes 8192 | tf_op jit(solution)/shard_map/all_to_all | solution.py:25
  173.4 6.4 %all-to-all-done.4 = f32[8,1,128]{2,1,0:T(1,128)S(1)} async-done(((f32[8,1,128]{2,1,0:T(1,128)}), f32[8,1,128]{2,1,0:T(1,128)S(1)}, u32[]{:S(2)}, u32[]{:S(2)}) %all-to-all-start.4) | async-done | bytes 4128 | tf_op jit(solution)/shard_map/all_to_all | solution.py:25
  179.8 1.1 broadcast_in_dim.17
  180.9 3.6 %all-to-all-start.3 = ((bf16[8,128,512]{2,1,0:T(8,128)(2,1)}), bf16[8,128,512]{2,1,0:T(8,128)(2,1)S(1)}, u32[]{:S(2)}, u32[]{:S(2)}) async-start(bf16[8,128,512]{2,1,0:T(8,128)(2,1)} %broadcast_in_dim.17), calls=%async_computation.4 | async-start | bytes 2097152 | tf_op jit(solution)/shard_map/all_to_all | solution.py:25
  184.7 17.5 %all-to-all-done.3 = bf16[8,128,512]{2,1,0:T(8,128)(2,1)S(1)} async-done(((bf16[8,128,512]{2,1,0:T(8,128)(2,1)}), bf16[8,128,512]{2,1,0:T(8,128)(2,1)S(1)}, u32[]{:S(2)}, u32[]{:S(2)}) %all-to-all-start.3) | async-done | bytes 1048608 | tf_op jit(solution)/shard_map/all_to_all | solution.py:25
  202.5 11.2 %all-gather.7.cloned.1.call-done = bf16[1024,3584]{1,0:T(8,128)(2,1)} async-done(((bf16[64,3584]{1,0:T(8,128)(2,1)}), bf16[1024,3584]{1,0:T(8,128)(2,1)}) %all-gather.7.cloned.1.call-update) | async-done | bytes 7340048 | tf_op jit(solution)/shard_map/all_gather | solution.py:67
  213.7 8.5 %fusion.32 = bf16[512,3584]{1,0:T(8,128)(2,1)} fusion(bf16[1024,512]{1,0:T(8,128)(2,1)S(1)} %fusion.2, bf16[1024,3584]{1,0:T(8,128)(2,1)} %all-gather.7.cloned.1.call-done), kind=kOutput, calls=%fused_computation.88 | convolution fusion | flops 3758096384 | bytes 12058624 | tf_op jit(solution)/shard_map/td,tf->df/dot_general | solution.py:69
  222.3 40.3 %all-gather.9.cloned.1.call-done = bf16[1024,3584]{1,0:T(8,128)(2,1)} async-done(((bf16[64,3584]{1,0:T(8,128)(2,1)}), bf16[1024,3584]{1,0:T(8,128)(2,1)}) %all-gather.9.cloned.1.call-update) | async-done | bytes 7340048 | tf_op jit(solution)/shard_map/all_gather | solution.py:68
  262.5 7.5 %fusion.31 = f32[1024,512]{1,0:T(8,128)S(1)} fusion(bf16[1024,3584]{1,0:T(8,128)(2,1)} %all-gather.7.cloned.1.call-done, bf16[512,3584]{1,0:T(8,128)(2,1)} %param.17), kind=kOutput, calls=%fused_computation.87 | convolution fusion | flops 3758096384 | bytes 13107200 | tf_op jit(solution)/shard_map/tf,df->td/dot_general | solution.py:73
  270.0 4.1 %fusion.27 = (bf16[1024,512]{1,0:T(8,128)(2,1)S(1)}, f32[512]{0:T(512)S(1)}) fusion(f32[1024]{0:T(1024)S(1)} %bitcast.89, bf16[8,128,512]{2,1,0:T(8,128)(2,1)S(1)} %all-to-all-done.3, f32[1024,512]{1,0:T(8,128)S(1)} %fusion.31, bf16[1024,3584]{1,0:T(8,128)(2,1)S(1)} %copy-done.8, bf16[512,3584]{1,0:T(8,128)(2,1)S(1)} %copy-done.9), kind=kOutput, calls=%fused_computation.83 | convolution fusion | flops 3761241600 | bytes 15210496 | tf_op jit(solution)/shard_map/tf,df->td/dot_general | solution.py:74
  274.4 0.8 fusion.26
  275.2 4.8 %collective-permute-start = (bf16[136,512]{1,0:T(8,128)(2,1)S(1)}, bf16[136,512]{1,0:T(8,128)(2,1)S(1)}, u32[]{:S(2)}, u32[]{:S(2)}) collective-permute-start(bf16[136,512]{1,0:T(8,128)(2,1)S(1)} %get-tuple-element.53), channel_id=1, source_target_pairs={{0,112},{16,0},{32,16},{48,32},{64,48},{80,64},{96,80},{112,96},{1... | collective-permute-start | bytes 417800 | tf_op jit(solution)/shard_map/ppermute | solution.py:89
  281.2 2.7 collective-permute-start.3
  283.9 0.7 fusion.20
  284.6 1.1 collective-permute-done
  285.8 2.2 collective-permute-start.5
  288.0 0.7 bitcast_dynamic-update-slice_fusion.12
  288.6 3.1 collective-permute-start.6
  291.8 0.7 bitcast_dynamic-update-slice_fusion.10
  292.5 0.7 bitcast_dynamic-update-slice_fusion.8
  293.1 0.7 bitcast_dynamic-update-slice_fusion.6
  293.8 0.7 bitcast_dynamic-update-slice_fusion.4
  294.5 0.7 bitcast_dynamic-update-slice_fusion.2
  295.2 3.6 %collective-permute-done.6 = bf16[136,512]{1,0:T(8,128)(2,1)S(1)} collective-permute-done((bf16[136,512]{1,0:T(8,128)(2,1)}, bf16[136,512]{1,0:T(8,128)(2,1)S(1)}, u32[]{:S(2)}, u32[]{:S(2)}) %collective-permute-start.6) | collective-permute-done | bytes 139296 | tf_op jit(solution)/shard_map/ppermute | solution.py:89
  298.7 0.7 bitcast_dynamic-update-slice_fusion
  299.4 0.7 constant_dynamic-update-slice_fusion
  300.1 0.7 bitcast_dynamic-update-slice_fusion.13
  300.7 0.7 bitcast_dynamic-update-slice_fusion.11
  302.1 0.7 bitcast_dynamic-update-slice_fusion.7
  304.7 1.4 convert_reduce_fusion
  306.2 0.9 pad_maximum_fusion.1
  307.1 5.7 %all-to-all-start.5 = ((f32[16,9,512]{2,1,0:T(8,128)}), f32[16,9,512]{2,1,0:T(8,128)S(1)}, u32[]{:S(2)}, u32[]{:S(2)}) async-start(f32[16,9,512]{2,1,0:T(8,128)} %pad_maximum_fusion.1), calls=%async_computation.6 | async-start | bytes 1048576 | tf_op jit(solution)/shard_map/all_to_all | solution.py:100
  312.8 8.7 %convolution_convert_fusion = bf16[512,3584]{1,0:T(8,128)(2,1)} fusion(bf16[1024,512]{1,0:T(8,128)(2,1)S(1)} %fusion.2, bf16[1024,3584]{1,0:T(8,128)(2,1)} %all-gather.9.cloned.1.call-done), kind=kOutput, calls=%fused_computation | convolution fusion | flops 3759931392 | bytes 12058624 | tf_op jit(solution)/shard_map/td,tf->df/dot_general | solution.py:103
  321.5 4.3 %all-to-all-done.5 = f32[16,9,512]{2,1,0:T(8,128)S(1)} async-done(((f32[16,9,512]{2,1,0:T(8,128)}), f32[16,9,512]{2,1,0:T(8,128)S(1)}, u32[]{:S(2)}, u32[]{:S(2)}) %all-to-all-start.5) | async-done | bytes 294944 | tf_op jit(solution)/shard_map/all_to_all | solution.py:100
  326.7 0.8 add_convert_fusion
  327.5 1.0 all-gather.11.cloned.1.call-done
  328.5 4.1 %convolution_convert_fusion.1 = bf16[1792,512]{1,0:T(8,128)(2,1)S(1)} fusion(bf16[1024,1792]{1,0:T(8,128)(2,1)} %all-gather.11.cloned.1.call-done, bf16[1024,512]{1,0:T(8,128)(2,1)S(1)} %bitcast.82), kind=kOutput, calls=%fused_computation.10 | convolution fusion | flops 1879965696 | bytes 6553600 | tf_op jit(solution)/shard_map/tf,td->fd/dot_general | solution.py:104
  332.7 2.1 pad_maximum_fusion
  (65 shorter events, 7.2 us)
Async XLA Ops:
  7.2 2.4 copy-start.6
  7.2 53.0 %all-gather.5.cloned.1.call-start = ((), (), s32[]{:S(2)}) async-start(), calls=%async_computation.7 | async-start | bytes 3899392 | tf_op jit(solution)/shard_map/all_gather | solution.py:54
  9.5 139.2 %reduce-scatter.2.cloned.1.call-start = ((), (), s32[]{:S(2)}) async-start(), calls=%async_computation.8 | async-start | bytes 15597568 | tf_op jit(solution)/shard_map/reduce_scatter | solution.py:59
  46.9 13.4 %copy-start.4 = (bf16[8,128,512]{2,1,0:T(8,128)(2,1)}, bf16[8,128,512]{2,1,0:T(8,128)(2,1)S(1)}, u32[]{:S(2)}) copy-start(bf16[8,128,512]{2,1,0:T(8,128)(2,1)S(1)} %all_to_all.52) | copy-start | bytes 3145732
  60.2 88.5 %copy-start.2 = (bf16[64,3584]{1,0:T(8,128)(2,1)S(1)}, bf16[64,3584]{1,0:T(8,128)(2,1)}, u32[]{:S(2)}) copy-start(bf16[64,3584]{1,0:T(8,128)(2,1)} %param.16) | copy-start | bytes 1376260
  60.2 88.5 %copy-start.3 = (bf16[64,3584]{1,0:T(8,128)(2,1)S(1)}, bf16[64,3584]{1,0:T(8,128)(2,1)}, u32[]{:S(2)}) copy-start(bf16[64,3584]{1,0:T(8,128)(2,1)} %param.15) | copy-start | bytes 1376260
  60.2 153.5 %all-gather.7.cloned.1.call-start = ((), (), s32[]{:S(2)}) async-start(), calls=%async_computation.9 | async-start | bytes 7798784 | tf_op jit(solution)/shard_map/all_gather | solution.py:67
  65.8 86.1 %copy-start = (bf16[8,8192]{1,0:T(8,128)(2,1)S(1)}, bf16[8,8192]{1,0:T(8,128)(2,1)}, u32[]{:S(2)}) copy-start(bf16[8,8192]{1,0:T(8,128)(2,1)} %param.12) | copy-start | bytes 393220
  151.3 111.2 %all-gather.9.cloned.1.call-start = ((), (), s32[]{:S(2)}) async-start(), calls=%async_computation.10 | async-start | bytes 7798784 | tf_op jit(solution)/shard_map/all_gather | solution.py:68
  152.2 32.4 %copy-start.7 = (f32[8192]{0:T(1024)S(1)}, f32[8192]{0:T(1024)}, u32[]{:S(2)}) copy-start(f32[8192]{0:T(1024)} %param.13) | copy-start | bytes 98308
  167.2 12.6 %all-to-all-start.4 = ((f32[8,1,128]{2,1,0:T(1,128)}), f32[8,1,128]{2,1,0:T(1,128)S(1)}, u32[]{:S(2)}, u32[]{:S(2)}) async-start(f32[8,1,128]{2,1,0:T(1,128)} %broadcast_in_dim.19), calls=%async_computation.5 | async-start | bytes 8192 | tf_op jit(solution)/shard_map/all_to_all | solution.py:25
  180.9 21.3 %all-to-all-start.3 = ((bf16[8,128,512]{2,1,0:T(8,128)(2,1)}), bf16[8,128,512]{2,1,0:T(8,128)(2,1)S(1)}, u32[]{:S(2)}, u32[]{:S(2)}) async-start(bf16[8,128,512]{2,1,0:T(8,128)(2,1)} %broadcast_in_dim.17), calls=%async_computation.4 | async-start | bytes 2097152 | tf_op jit(solution)/shard_map/all_to_all | solution.py:25
  184.5 144.1 %all-gather.11.cloned.1.call-start = ((), (), s32[]{:S(2)}) async-start(), calls=%async_computation.11 | async-start | bytes 3899392 | tf_op jit(solution)/shard_map/all_gather | solution.py:72
  262.5 7.5 %copy-start.8 = (bf16[1024,3584]{1,0:T(8,128)(2,1)S(1)}, bf16[1024,3584]{1,0:T(8,128)(2,1)}, u32[]{:S(2)}) copy-start(bf16[1024,3584]{1,0:T(8,128)(2,1)} %all-gather.9.cloned.1.call-done) | copy-start | bytes 22020100
  262.5 7.5 %copy-start.9 = (bf16[512,3584]{1,0:T(8,128)(2,1)S(1)}, bf16[512,3584]{1,0:T(8,128)(2,1)}, u32[]{:S(2)}) copy-start(bf16[512,3584]{1,0:T(8,128)(2,1)} %param.18) | copy-start | bytes 11010052
  275.2 10.6 %collective-permute-start = (bf16[136,512]{1,0:T(8,128)(2,1)S(1)}, bf16[136,512]{1,0:T(8,128)(2,1)S(1)}, u32[]{:S(2)}, u32[]{:S(2)}) collective-permute-start(bf16[136,512]{1,0:T(8,128)(2,1)S(1)} %get-tuple-element.53), channel_id=1, source_target_pairs={{0,112},{16,0},{32,16},{48,32},{64,48},{80,64},{96,80},{112,96},{1... | collective-permute-start | bytes 417800 | tf_op jit(solution)/shard_map/ppermute | solution.py:89
  280.0 8.6 %collective-permute-start.1 = (bf16[136,512]{1,0:T(8,128)(2,1)S(1)}, bf16[136,512]{1,0:T(8,128)(2,1)S(1)}, u32[]{:S(2)}, u32[]{:S(2)}) collective-permute-start(bf16[136,512]{1,0:T(8,128)(2,1)S(1)} %get-tuple-element.54), channel_id=1, source_target_pairs={{0,96},{16,112},{32,0},{48,16},{64,32},{80,48},{96,64},{112,80},{1... | collective-permute-start | bytes 417800 | tf_op jit(solution)/shard_map/ppermute | solution.py:89
  280.6 11.8 %collective-permute-start.2 = (bf16[136,512]{1,0:T(8,128)(2,1)}, bf16[136,512]{1,0:T(8,128)(2,1)S(1)}, u32[]{:S(2)}, u32[]{:S(2)}) collective-permute-start(bf16[136,512]{1,0:T(8,128)(2,1)} %get-tuple-element.55), channel_id=1, source_target_pairs={{0,80},{16,96},{32,112},{48,0},{64,16},{80,32},{96,48},{112,64},{1... | collective-permute-start | bytes 417800 | tf_op jit(solution)/shard_map/ppermute | solution.py:89
  281.2 12.0 %collective-permute-start.3 = (bf16[136,512]{1,0:T(8,128)(2,1)}, bf16[136,512]{1,0:T(8,128)(2,1)S(1)}, u32[]{:S(2)}, u32[]{:S(2)}) collective-permute-start(bf16[136,512]{1,0:T(8,128)(2,1)} %get-tuple-element.56), channel_id=1, source_target_pairs={{0,64},{16,80},{32,96},{48,112},{64,0},{80,16},{96,32},{112,48},{1... | collective-permute-start | bytes 417800 | tf_op jit(solution)/shard_map/ppermute | solution.py:89
  284.6 9.2 %collective-permute-start.4 = (bf16[136,512]{1,0:T(8,128)(2,1)}, bf16[136,512]{1,0:T(8,128)(2,1)S(1)}, u32[]{:S(2)}, u32[]{:S(2)}) collective-permute-start(bf16[136,512]{1,0:T(8,128)(2,1)} %get-tuple-element.58), channel_id=1, source_target_pairs={{0,48},{16,64},{32,80},{48,96},{64,112},{80,0},{96,16},{112,32},{1... | collective-permute-start | bytes 417800 | tf_op jit(solution)/shard_map/ppermute | solution.py:89
  285.8 8.7 %collective-permute-start.5 = (bf16[136,512]{1,0:T(8,128)(2,1)}, bf16[136,512]{1,0:T(8,128)(2,1)S(1)}, u32[]{:S(2)}, u32[]{:S(2)}) collective-permute-start(bf16[136,512]{1,0:T(8,128)(2,1)} %get-tuple-element.57), channel_id=1, source_target_pairs={{0,32},{16,48},{32,64},{48,80},{64,96},{80,112},{96,0},{112,16},{1... | collective-permute-start | bytes 417800 | tf_op jit(solution)/shard_map/ppermute | solution.py:89
  288.6 10.1 %collective-permute-start.6 = (bf16[136,512]{1,0:T(8,128)(2,1)}, bf16[136,512]{1,0:T(8,128)(2,1)S(1)}, u32[]{:S(2)}, u32[]{:S(2)}) collective-permute-start(bf16[136,512]{1,0:T(8,128)(2,1)} %get-tuple-element.51), channel_id=1, source_target_pairs={{0,16},{16,32},{32,48},{48,64},{64,80},{80,96},{96,112},{112,0},{1... | collective-permute-start | bytes 417800 | tf_op jit(solution)/shard_map/ppermute | solution.py:89
  307.1 18.7 %all-to-all-start.5 = ((f32[16,9,512]{2,1,0:T(8,128)}), f32[16,9,512]{2,1,0:T(8,128)S(1)}, u32[]{:S(2)}, u32[]{:S(2)}) async-start(f32[16,9,512]{2,1,0:T(8,128)} %pad_maximum_fusion.1), calls=%async_computation.6 | async-start | bytes 1048576 | tf_op jit(solution)/shard_map/all_to_all | solution.py:100
  312.8 15.7 %copy-start.5 = (bf16[8,128,512]{2,1,0:T(8,128)(2,1)S(1)}, bf16[8,128,512]{2,1,0:T(8,128)(2,1)}, u32[]{:S(2)}) copy-start(bf16[8,128,512]{2,1,0:T(8,128)(2,1)} %copy-done.4) | copy-start | bytes 3145732
  327.5 5.1 %copy-start.1 = (bf16[1792,512]{1,0:T(8,128)(2,1)S(1)}, bf16[1792,512]{1,0:T(8,128)(2,1)}, u32[]{:S(2)}) copy-start(bf16[1792,512]{1,0:T(8,128)(2,1)} %fusion.30) | copy-start | bytes 5505028
Sparse Core Ops, SparseCore 0:
  10.3 49.8 all-gather.4
  62.6 86.0 reduce-scatter.1
  151.4 62.2 all-gather.6
  215.9 46.6 all-gather.8
  284.8 43.7 all-gather.10

commit v10 on v8

--- a/solution.py
+++ b/solution.py
@@ -50,7 +50,7 @@
     grid_scale = grid[:, tile : tile + 1].reshape(1, cols * mine_rows)
     all_grad = row_gather(grid_grad)
     hidden_block = swiglu_grads(jnp.zeros(pre_gate.shape, jnp.float32), pre_gate, pre_up)[0]
-    split = (hidden_block.shape[1] // 256) * 128
+    split = (hidden_block.shape[1] // 448) * 128
     hidden_piece = lax.all_gather(hidden_block[:, :split], "col", axis=0, tiled=True)
     partial_grad = jnp.einsum(
         "td,fd->tf", all_grad, down_weight, preferred_element_type=jnp.float32

time: 334 us -> 331 us (level)
  transfers between devices with their start and end apart: 8 -> 8, of which waited for: 7 -> 6; matrix products, arithmetic and copies ran while one was open for 16% -> 16% of each run, Pallas kernels for 0% -> 0%
where the time goes in v10:
time: 331 us; the launch traced here: 330 us
  waiting for transfers between devices  159 us (48%)
  blocking collectives  76.2 us (23%)
  matrix products  48.8 us (15%)
  starting transfers between devices  15.6 us (5%)
  between operations  14 us (4%)
  other arithmetic  11 us (3%)
  local copies, waits for them, and re-layouts  5.29 us (2%)
    reduce_scatter x1, waiting for transfers between devices, local(): lax.psum_scatter(partial_grad, 'col', scatter_dimension=0, tiled=True)  84.9 us
    all_gather x1, waiting for transfers between devices, local(): up_piece = lax.all_gather(up_block, 'col', axis=0, tiled=True)  39.1 us
    all_to_all x1, blocking collectives, local(): got = lax.all_to_all(sent, 'row', split_axis=0, concat_axis=0, tiled=True)  25.1 us
    all_to_all x1, blocking collectives, row_gather(): got = lax.all_to_all(copies, 'row', split_axis=0, concat_axis=0, tiled=True)  23.5 us
    all_to_all x2, waiting for transfers between devices, row_gather(): got = lax.all_to_all(copies, 'row', split_axis=0, concat_axis=0, tiled=True)  23.1 us
    all_to_all x1, blocking collectives, local(): lax.all_to_all(packed, 'col', split_axis=1, concat_axis=0, tiled=True)  14.1 us
    all_to_all x1, blocking collectives, local(): lax.all_to_all(grad_out, 'col', split_axis=1, concat_axis=0, tiled=True)  13.4 us
    all_gather x1, waiting for transfers between devices, local(): gate_piece = lax.all_gather(gate_block, 'col', axis=0, tiled=True)  10.2 us
  transfers between devices with their start and end apart: 8, of which 6 were waited for; matrix products, arithmetic and copies ran while one was open for 16% of the time, Pallas kernels for 0%

profile of v10, /device:TPU:1, one launch (start us, length us, event | category | flops | bytes accessed | tf_op | source)
XLA Modules:
  0.0 330.3 jit_solution(11313620677822065228)
XLA Ops:
  7.2 0.0 all-gather.5.cloned.1.call-start
  7.2 1.4 fusion.4
  8.6 0.7 slice.76
  9.3 0.0 reduce-scatter.2.cloned.1.call-start
  9.4 13.4 %all_to_all.56 = bf16[8,16,512]{2,0,1:T(8,128)(2,1)S(1)} all-to-all(bf16[8,16,512]{2,0,1:T(8,128)(2,1)} %bitcast.49), channel_id=1, replica_groups=mesh['row'=8,'col'=16] {'col'}, dimensions={1} | all-to-all | bytes 262144 | tf_op jit(solution)/shard_map/all_to_all | solution.py:39
  22.8 0.1 broadcast_in_dim.15
  22.9 23.5 %all_to_all.57 = bf16[8,128,512]{2,1,0:T(8,128)(2,1)S(1)} all-to-all(bf16[8,128,512]{2,1,0:T(8,128)(2,1)S(1)} %broadcast_in_dim.15), channel_id=1, replica_groups=mesh['row'=8,'col'=16] {'row'}, dimensions={0} | all-to-all | bytes 2097152 | tf_op jit(solution)/shard_map/all_to_all | solution.py:25
  46.4 1.0 copy-done.4
  47.4 9.4 %fusion.13 = f32[1024,3584]{1,0:T(8,128)} fusion(bf16[1024,512]{1,0:T(8,128)(2,1)S(1)} %bitcast.42, bf16[3584,512]{1,0:T(8,128)(2,1)} %param.19), kind=kOutput, calls=%fused_computation.38 | convolution fusion | flops 3758096384 | bytes 19398656 | tf_op jit(solution)/shard_map/td,fd->tf/dot_general | solution.py:55
  56.8 0.0 reduce-scatter.2.cloned.1.call-update
  56.8 0.0 all-gather.7.cloned.1.call-start
  56.9 3.2 fusion.14
  60.1 84.9 %reduce-scatter.2.cloned.1.call-done = f32[64,3584]{1,0:T(8,128)} async-done(((f32[1024,3584]{1,0:T(8,128)}), f32[64,3584]{1,0:T(8,128)}) %reduce-scatter.2.cloned.1.call-update) | async-done | bytes 917520 | tf_op jit(solution)/shard_map/reduce_scatter | solution.py:59
  145.0 2.5 multiply_convert_fusion
  147.5 0.0 all-gather.9.cloned.1.call-start
  147.6 0.5 all-gather.9.cloned.1.call-update
  148.2 0.2 multiply_reduce_fusion.1
  148.3 0.1 broadcast_in_dim.16
  148.5 14.1 %all_to_all.58 = f32[8,16,640]{2,0,1:T(8,128)S(1)} all-to-all(f32[8,16,640]{2,0,1:T(8,128)S(1)} %pad_maximum_fusion.3), channel_id=1, replica_groups=mesh['row'=8,'col'=16] {'col'}, dimensions={1} | all-to-all | bytes 655360 | tf_op jit(solution)/shard_map/all_to_all | solution.py:47
  162.6 0.1 slice_reduce_fusion
  162.7 0.6 broadcast_in_dim.19
  163.3 6.3 %all-to-all-start.4 = ((f32[8,1,128]{2,1,0:T(1,128)}), f32[8,1,128]{2,1,0:T(1,128)S(1)}, u32[]{:S(2)}, u32[]{:S(2)}) async-start(f32[8,1,128]{2,1,0:T(1,128)} %broadcast_in_dim.19), calls=%async_computation.5 | async-start | bytes 8192 | tf_op jit(solution)/shard_map/all_to_all | solution.py:25
  169.6 6.4 %all-to-all-done.4 = f32[8,1,128]{2,1,0:T(1,128)S(1)} async-done(((f32[8,1,128]{2,1,0:T(1,128)}), f32[8,1,128]{2,1,0:T(1,128)S(1)}, u32[]{:S(2)}, u32[]{:S(2)}) %all-to-all-start.4) | async-done | bytes 4128 | tf_op jit(solution)/shard_map/all_to_all | solution.py:25
  176.1 1.1 broadcast_in_dim.17
  177.1 3.6 %all-to-all-start.3 = ((bf16[8,128,512]{2,1,0:T(8,128)(2,1)}), bf16[8,128,512]{2,1,0:T(8,128)(2,1)S(1)}, u32[]{:S(2)}, u32[]{:S(2)}) async-start(bf16[8,128,512]{2,1,0:T(8,128)(2,1)} %broadcast_in_dim.17), calls=%async_computation.4 | async-start | bytes 2097152 | tf_op jit(solution)/shard_map/all_to_all | solution.py:25
  180.7 0.2 all-gather.11.cloned.1.call-start
  180.9 0.7 slice.77
  181.7 0.1 dynamic_slice.3
  181.8 16.7 %all-to-all-done.3 = bf16[8,128,512]{2,1,0:T(8,128)(2,1)S(1)} async-done(((bf16[8,128,512]{2,1,0:T(8,128)(2,1)}), bf16[8,128,512]{2,1,0:T(8,128)(2,1)S(1)}, u32[]{:S(2)}, u32[]{:S(2)}) %all-to-all-start.3) | async-done | bytes 1048608 | tf_op jit(solution)/shard_map/all_to_all | solution.py:25
  198.5 1.3 fusion.2
  199.7 10.2 %all-gather.7.cloned.1.call-done = bf16[1024,3584]{1,0:T(8,128)(2,1)} async-done(((bf16[64,3584]{1,0:T(8,128)(2,1)}), bf16[1024,3584]{1,0:T(8,128)(2,1)}) %all-gather.7.cloned.1.call-update) | async-done | bytes 7340048 | tf_op jit(solution)/shard_map/all_gather | solution.py:67
  209.9 9.3 %fusion.16 = bf16[512,3584]{1,0:T(8,128)(2,1)} fusion(bf16[1024,512]{1,0:T(8,128)(2,1)} %fusion.2, bf16[1024,3584]{1,0:T(8,128)(2,1)} %all-gather.7.cloned.1.call-done), kind=kOutput, calls=%fused_computation.41 | convolution fusion | flops 3758096384 | bytes 12058624 | tf_op jit(solution)/shard_map/td,tf->df/dot_general | solution.py:69
  219.1 39.1 %all-gather.9.cloned.1.call-done = bf16[1024,3584]{1,0:T(8,128)(2,1)} async-done(((bf16[64,3584]{1,0:T(8,128)(2,1)}), bf16[1024,3584]{1,0:T(8,128)(2,1)}) %all-gather.9.cloned.1.call-update) | async-done | bytes 7340048 | tf_op jit(solution)/shard_map/all_gather | solution.py:68
  258.2 7.5 %fusion.15 = f32[1024,512]{1,0:T(8,128)S(1)} fusion(bf16[1024,3584]{1,0:T(8,128)(2,1)} %all-gather.7.cloned.1.call-done, bf16[512,3584]{1,0:T(8,128)(2,1)} %param.17), kind=kOutput, calls=%fused_computation.40 | convolution fusion | flops 3758096384 | bytes 13107200 | tf_op jit(solution)/shard_map/tf,df->td/dot_general | solution.py:73
  265.8 5.1 %fusion.12 = (bf16[1024,512]{1,0:T(8,128)(2,1)}, f32[512]{0:T(512)S(1)}) fusion(f32[1024]{0:T(1024)S(1)} %bitcast.52, bf16[8,128,512]{2,1,0:T(8,128)(2,1)S(1)} %all-to-all-done.3, f32[1024,512]{1,0:T(8,128)S(1)} %fusion.15, bf16[1024,3584]{1,0:T(8,128)(2,1)S(1)} %copy-done.7, bf16[512,3584]{1,0:T(8,128)(2,1)S(1)} %copy-done.8), kind=kOutput, calls=%fused_computation.37 | convolution fusion | flops 3761241600 | bytes 15210496 | tf_op jit(solution)/shard_map/tf,df->td/dot_general | solution.py:74
  270.9 0.1 scatter.9
  271.0 1.4 pad_maximum_fusion.1
  272.4 25.1 %all_to_all.59 = bf16[8,136,512]{2,1,0:T(8,128)(2,1)S(1)} all-to-all(bf16[8,136,512]{2,1,0:T(8,128)(2,1)S(1)} %pad_maximum_fusion.1), channel_id=1, replica_groups=mesh['row'=8,'col'=16] {'row'}, dimensions={0} | all-to-all | bytes 2228224 | tf_op jit(solution)/shard_map/all_to_all | solution.py:85
  297.5 0.2 convert_reduce_fusion
  297.8 0.9 pad_maximum_fusion.2
  298.6 5.4 %all-to-all-start.6 = ((f32[16,9,512]{2,1,0:T(8,128)}), f32[16,9,512]{2,1,0:T(8,128)S(1)}, u32[]{:S(2)}, u32[]{:S(2)}) async-start(f32[16,9,512]{2,1,0:T(8,128)} %pad_maximum_fusion.2), calls=%async_computation.7 | async-start | bytes 1048576 | tf_op jit(solution)/shard_map/all_to_all | solution.py:94
  304.0 8.7 %convolution_convert_fusion = bf16[512,3584]{1,0:T(8,128)(2,1)} fusion(bf16[1024,512]{1,0:T(8,128)(2,1)S(1)} %copy-done.3, bf16[1024,3584]{1,0:T(8,128)(2,1)} %all-gather.9.cloned.1.call-done), kind=kOutput, calls=%fused_computation | convolution fusion | flops 3759931392 | bytes 12058624 | tf_op jit(solution)/shard_map/td,tf->df/dot_general | solution.py:97
  312.7 1.6 all-to-all-done.6
  314.3 0.6 slice.84
  314.9 0.3 multiply_reduce_fusion
  315.2 0.8 add_convert_fusion
  316.0 5.7 %convolution_convert_fusion.1 = bf16[2560,512]{1,0:T(8,128)(2,1)S(1)} fusion(bf16[1024,2560]{1,0:T(8,128)(2,1)} %all-gather.11.cloned.1.call-done, bf16[1024,512]{1,0:T(8,128)(2,1)} %bitcast.44), kind=kOutput, calls=%fused_computation.1 | convolution fusion | flops 2685665280 | bytes 8912896 | tf_op jit(solution)/shard_map/tf,td->fd/dot_general | solution.py:98
  321.7 2.1 pad_maximum_fusion
  (35 shorter events, 0.3 us)
Async XLA Ops:
  7.2 49.6 %all-gather.5.cloned.1.call-start = ((), (), s32[]{:S(2)}) async-start(), calls=%async_computation.8 | async-start | bytes 2228224 | tf_op jit(solution)/shard_map/all_gather | solution.py:54
  9.3 135.6 %reduce-scatter.2.cloned.1.call-start = ((), (), s32[]{:S(2)}) async-start(), calls=%async_computation.9 | async-start | bytes 15597568 | tf_op jit(solution)/shard_map/reduce_scatter | solution.py:59
  46.4 1.0 copy-start.4
  56.8 88.2 %copy-start.1 = (bf16[64,3584]{1,0:T(8,128)(2,1)S(1)}, bf16[64,3584]{1,0:T(8,128)(2,1)}, u32[]{:S(2)}) copy-start(bf16[64,3584]{1,0:T(8,128)(2,1)} %param.16) | copy-start | bytes 1376260
  56.8 88.1 %copy-start.2 = (bf16[64,3584]{1,0:T(8,128)(2,1)S(1)}, bf16[64,3584]{1,0:T(8,128)(2,1)}, u32[]{:S(2)}) copy-start(bf16[64,3584]{1,0:T(8,128)(2,1)} %param.15) | copy-start | bytes 1376260
  56.8 153.1 %all-gather.7.cloned.1.call-start = ((), (), s32[]{:S(2)}) async-start(), calls=%async_computation.10 | async-start | bytes 7798784 | tf_op jit(solution)/shard_map/all_gather | solution.py:67
  60.1 88.0 %copy-start = (bf16[8,8192]{1,0:T(8,128)(2,1)S(1)}, bf16[8,8192]{1,0:T(8,128)(2,1)}, u32[]{:S(2)}) copy-start(bf16[8,8192]{1,0:T(8,128)(2,1)} %param.12) | copy-start | bytes 393220
  147.5 34.2 %copy-start.6 = (f32[8192]{0:T(1024)S(1)}, f32[8192]{0:T(1024)}, u32[]{:S(2)}) copy-start(f32[8192]{0:T(1024)} %param.13) | copy-start | bytes 98308
  147.5 110.7 %all-gather.9.cloned.1.call-start = ((), (), s32[]{:S(2)}) async-start(), calls=%async_computation.11 | async-start | bytes 7798784 | tf_op jit(solution)/shard_map/all_gather | solution.py:68
  163.3 12.8 %all-to-all-start.4 = ((f32[8,1,128]{2,1,0:T(1,128)}), f32[8,1,128]{2,1,0:T(1,128)S(1)}, u32[]{:S(2)}, u32[]{:S(2)}) async-start(f32[8,1,128]{2,1,0:T(1,128)} %broadcast_in_dim.19), calls=%async_computation.5 | async-start | bytes 8192 | tf_op jit(solution)/shard_map/all_to_all | solution.py:25
  177.1 21.3 %all-to-all-start.3 = ((bf16[8,128,512]{2,1,0:T(8,128)(2,1)}), bf16[8,128,512]{2,1,0:T(8,128)(2,1)S(1)}, u32[]{:S(2)}, u32[]{:S(2)}) async-start(bf16[8,128,512]{2,1,0:T(8,128)(2,1)} %broadcast_in_dim.17), calls=%async_computation.4 | async-start | bytes 2097152 | tf_op jit(solution)/shard_map/all_to_all | solution.py:25
  180.7 135.2 %all-gather.11.cloned.1.call-start = ((), (), s32[]{:S(2)}) async-start(), calls=%async_computation.12 | async-start | bytes 5570560 | tf_op jit(solution)/shard_map/all_gather | solution.py:72
  258.2 7.5 %copy-start.7 = (bf16[1024,3584]{1,0:T(8,128)(2,1)S(1)}, bf16[1024,3584]{1,0:T(8,128)(2,1)}, u32[]{:S(2)}) copy-start(bf16[1024,3584]{1,0:T(8,128)(2,1)} %all-gather.9.cloned.1.call-done) | copy-start | bytes 22020100
  258.2 7.5 %copy-start.8 = (bf16[512,3584]{1,0:T(8,128)(2,1)S(1)}, bf16[512,3584]{1,0:T(8,128)(2,1)}, u32[]{:S(2)}) copy-start(bf16[512,3584]{1,0:T(8,128)(2,1)} %param.18) | copy-start | bytes 11010052
  271.0 33.0 %copy-start.3 = (bf16[1024,512]{1,0:T(8,128)(2,1)S(1)}, bf16[1024,512]{1,0:T(8,128)(2,1)}, u32[]{:S(2)}) copy-start(bf16[1024,512]{1,0:T(8,128)(2,1)} %fusion.2) | copy-start | bytes 3145732
  298.6 15.6 %all-to-all-start.6 = ((f32[16,9,512]{2,1,0:T(8,128)}), f32[16,9,512]{2,1,0:T(8,128)S(1)}, u32[]{:S(2)}, u32[]{:S(2)}) async-start(f32[16,9,512]{2,1,0:T(8,128)} %pad_maximum_fusion.2), calls=%async_computation.7 | async-start | bytes 1048576 | tf_op jit(solution)/shard_map/all_to_all | solution.py:94
  304.0 11.2 %copy-start.5 = (bf16[8,8192]{1,0:T(8,128)(2,1)S(1)}, bf16[8,8192]{1,0:T(8,128)(2,1)}, u32[]{:S(2)}) copy-start(bf16[8,8192]{1,0:T(8,128)(2,1)} %param.14) | copy-start | bytes 393220
Sparse Core Ops, SparseCore 0:
  10.2 45.7 all-gather.4
  58.4 86.4 reduce-scatter.1
  147.7 62.1 all-gather.6
  211.4 46.7 all-gather.8
  259.8 56.1 all-gather.10

commit v11 on v10

--- a/solution.py
+++ b/solution.py
@@ -76,24 +76,19 @@
     )
     gain_part = jnp.sum(new_rows * all_normed, axis=0)
     tokens_all = new_rows.shape[0]
-    blocks = new_rows.astype(jnp.bfloat16).reshape(rows, tokens_all // rows, tile)
+    mine = tokens_all // (rows * cols)
+    blocks = new_rows.astype(jnp.bfloat16).reshape(rows * cols, mine, tile)
     gain_high = gain_part.astype(jnp.bfloat16)
     gain_low = (gain_part - gain_high.astype(jnp.float32)).astype(jnp.bfloat16)
-    extra = jnp.zeros((rows, 8, tile), jnp.bfloat16)
-    extra = extra.at[:, 0, :].set(gain_high).at[:, 1, :].set(gain_low)
+    extra = jnp.broadcast_to(
+        jnp.stack([gain_high, gain_low])[None], (rows * cols, 2, tile)
+    )
     sent = jnp.concatenate([blocks, extra], axis=1)
-    got = lax.all_to_all(sent, "row", split_axis=0, concat_axis=0, tiled=True)
-    summed = jnp.sum(got.astype(jnp.float32), axis=0)
-    grid_back = summed[: tokens_all // rows]
-    gain_tile_grad = summed[tokens_all // rows] + summed[tokens_all // rows + 1]
-    per_col = grid_back.reshape(cols, -1, tile)
-    mine = per_col.shape[1]
-    sent2 = jnp.concatenate(
-        [per_col, jnp.broadcast_to(gain_tile_grad[None, None, :], (cols, 1, tile))], axis=1
-    )
-    got2 = lax.all_to_all(sent2, "col", split_axis=0, concat_axis=0, tiled=True)
-    normed_grad = got2[:, :mine, :].transpose(1, 0, 2).reshape(mine, cols * tile)
-    grad_gain = got2[:, mine, :].reshape(cols * tile)
+    got = lax.all_to_all(sent, ("row", "col"), split_axis=0, concat_axis=0, tiled=True)
+    got = got.reshape(rows, cols, mine + 2, tile).astype(jnp.float32)
+    summed = jnp.sum(got, axis=0)
+    normed_grad = summed[:, :mine, :].transpose(1, 0, 2).reshape(mine, cols * tile)
+    grad_gain = (summed[:, mine, :] + summed[:, mine + 1, :]).reshape(cols * tile)
     up_total = jnp.einsum("td,tf->df", all_input, up_piece, preferred_element_type=jnp.float32)
     down_late = jnp.einsum("tf,td->fd", late_piece, all_grad, preferred_element_type=jnp.float32)
     scaled_grad = normed_grad * gain

time: 331 us -> 337 us (1.018)
  waiting for transfers between devices: 159 us -> 188 us
  blocking collectives: 76.2 us -> 51 us
  starting transfers between devices: 15.6 us -> 19.2 us
    all_to_all x1 -> x0, blocking collectives: 25.1 us -> none  [local(): got = lax.all_to_all(sent, 'row', split_axis=0, concat_axis=0, tiled=True)]
    all_to_all x1, waiting for transfers between devices: 1.57 us -> 22.4 us  [local(): lax.all_to_all(sent, ('row', 'col'), split_axis=0, concat_axis=0, tiled=T...]
    all_gather x1, waiting for transfers between devices: 0.01 us -> 7.39 us  [local(): late_piece = lax.all_gather(late_block, 'col', axis=0, tiled=True)]
  transfers between devices with their start and end apart: 8 -> 8, of which waited for: 6 -> 7; matrix products, arithmetic and copies ran while one was open for 16% -> 15% of each run, Pallas kernels for 0% -> 0%
where the time goes in v11:
time: 337 us
  waiting for transfers between devices  188 us (56%)
  blocking collectives  51 us (15%)
  matrix products  50.1 us (15%)
  starting transfers between devices  19.2 us (6%)
  between operations  14 us (4%)
  other arithmetic  10.5 us (3%)
  local copies, waits for them, and re-layouts  3.65 us (1%)
    reduce_scatter x1, waiting for transfers between devices, local(): lax.psum_scatter(partial_grad, 'col', scatter_dimension=0, tiled=True)  83.6 us
    all_gather x1, waiting for transfers between devices, local(): up_piece = lax.all_gather(up_block, 'col', axis=0, tiled=True)  40.5 us
    all_to_all x1, blocking collectives, row_gather(): got = lax.all_to_all(copies, 'row', split_axis=0, concat_axis=0, tiled=True)  23.7 us
    all_to_all x2, waiting for transfers between devices, row_gather(): got = lax.all_to_all(copies, 'row', split_axis=0, concat_axis=0, tiled=True)  23.1 us
    all_to_all x1, waiting for transfers between devices, local(): lax.all_to_all(sent, ('row', 'col'), split_axis=0, concat_axis=0, tiled=T...  22.4 us
    all_to_all x1, blocking collectives, local(): lax.all_to_all(packed, 'col', split_axis=1, concat_axis=0, tiled=True)  13.9 us
    all_to_all x1, blocking collectives, local(): lax.all_to_all(grad_out, 'col', split_axis=1, concat_axis=0, tiled=True)  13.4 us
    dot_general x1, matrix products, local(): jnp.einsum('td,fd->tf', all_grad, down_weight, preferred_element_type=jnp...  11.6 us
  transfers between devices with their start and end apart: 8, of which 7 were waited for; matrix products, arithmetic and copies ran while one was open for 15% of the time, Pallas kernels for 0%

profile of v11, /device:TPU:1, one launch (start us, length us, event | category | flops | bytes accessed | tf_op | source)
XLA Modules:
  0.0 336.8 jit_solution(5394792852146012591)
XLA Ops:
  7.2 0.0 all-gather.5.cloned.1.call-start
  7.2 1.4 fusion.4
  8.6 0.7 slice.29
  9.3 0.0 all-gather.5.cloned.1.call-update
  9.3 0.0 reduce-scatter.2.cloned.1.call-start
  9.4 13.4 %all_to_all.51 = bf16[8,16,512]{2,0,1:T(8,128)(2,1)S(1)} all-to-all(bf16[8,16,512]{2,0,1:T(8,128)(2,1)} %bitcast.47), channel_id=1, replica_groups=mesh['row'=8,'col'=16] {'col'}, dimensions={1} | all-to-all | bytes 262144 | tf_op jit(solution)/shard_map/all_to_all | solution.py:39
  22.8 0.1 broadcast_in_dim.15
  22.9 23.7 %all_to_all.52 = bf16[8,128,512]{2,1,0:T(8,128)(2,1)} all-to-all(bf16[8,128,512]{2,1,0:T(8,128)(2,1)S(1)} %broadcast_in_dim.15), channel_id=1, replica_groups=mesh['row'=8,'col'=16] {'row'}, dimensions={0} | all-to-all | bytes 2097152 | tf_op jit(solution)/shard_map/all_to_all | solution.py:25
  46.5 11.6 %fusion.12 = f32[1024,3584]{1,0:T(8,128)} fusion(bf16[1024,512]{1,0:T(8,128)(2,1)} %bitcast.3, bf16[3584,512]{1,0:T(8,128)(2,1)} %param.15), kind=kOutput, calls=%fused_computation.37 | convolution fusion | flops 3758096384 | bytes 19398656 | tf_op jit(solution)/shard_map/td,fd->tf/dot_general | solution.py:55
  58.1 0.0 reduce-scatter.2.cloned.1.call-update
  58.1 0.0 all-gather.7.cloned.1.call-start
  58.2 3.2 fusion.13
  61.4 83.6 %reduce-scatter.2.cloned.1.call-done = f32[64,3584]{1,0:T(8,128)} async-done(((f32[1024,3584]{1,0:T(8,128)}), f32[64,3584]{1,0:T(8,128)}) %reduce-scatter.2.cloned.1.call-update) | async-done | bytes 917520 | tf_op jit(solution)/shard_map/reduce_scatter | solution.py:59
  145.0 2.5 multiply_convert_fusion
  147.5 0.0 all-gather.7.cloned.1.call-update
  147.5 0.0 all-gather.9.cloned.1.call-start
  147.6 0.5 all-gather.9.cloned.1.call-update
  148.2 0.2 multiply_reduce_fusion.1
  148.3 0.1 broadcast_in_dim.16
  148.5 13.9 %all_to_all.53 = f32[8,16,640]{2,0,1:T(8,128)S(1)} all-to-all(f32[8,16,640]{2,0,1:T(8,128)S(1)} %pad_maximum_fusion.2), channel_id=1, replica_groups=mesh['row'=8,'col'=16] {'col'}, dimensions={1} | all-to-all | bytes 655360 | tf_op jit(solution)/shard_map/all_to_all | solution.py:47
  162.4 0.1 slice_reduce_fusion
  162.5 0.6 broadcast_in_dim.19
  163.1 6.5 %all-to-all-start.4 = ((f32[8,1,128]{2,1,0:T(1,128)}), f32[8,1,128]{2,1,0:T(1,128)S(1)}, u32[]{:S(2)}, u32[]{:S(2)}) async-start(f32[8,1,128]{2,1,0:T(1,128)} %broadcast_in_dim.19), calls=%async_computation.5 | async-start | bytes 8192 | tf_op jit(solution)/shard_map/all_to_all | solution.py:25
  169.6 6.4 %all-to-all-done.4 = f32[8,1,128]{2,1,0:T(1,128)S(1)} async-done(((f32[8,1,128]{2,1,0:T(1,128)}), f32[8,1,128]{2,1,0:T(1,128)S(1)}, u32[]{:S(2)}, u32[]{:S(2)}) %all-to-all-start.4) | async-done | bytes 4128 | tf_op jit(solution)/shard_map/all_to_all | solution.py:25
  176.1 1.1 broadcast_in_dim.17
  177.1 3.6 %all-to-all-start.3 = ((bf16[8,128,512]{2,1,0:T(8,128)(2,1)}), bf16[8,128,512]{2,1,0:T(8,128)(2,1)S(1)}, u32[]{:S(2)}, u32[]{:S(2)}) async-start(bf16[8,128,512]{2,1,0:T(8,128)(2,1)} %broadcast_in_dim.17), calls=%async_computation.4 | async-start | bytes 2097152 | tf_op jit(solution)/shard_map/all_to_all | solution.py:25
  180.7 0.2 all-gather.11.cloned.1.call-start
  180.9 0.8 slice.30
  181.7 0.1 dynamic_slice.3
  181.8 16.7 %all-to-all-done.3 = bf16[8,128,512]{2,1,0:T(8,128)(2,1)S(1)} async-done(((bf16[8,128,512]{2,1,0:T(8,128)(2,1)}), bf16[8,128,512]{2,1,0:T(8,128)(2,1)S(1)}, u32[]{:S(2)}, u32[]{:S(2)}) %all-to-all-start.3) | async-done | bytes 1048608 | tf_op jit(solution)/shard_map/all_to_all | solution.py:25
  198.4 0.3 fusion.2
  198.8 11.0 %all-gather.7.cloned.1.call-done = bf16[1024,3584]{1,0:T(8,128)(2,1)} async-done(((bf16[64,3584]{1,0:T(8,128)(2,1)}), bf16[1024,3584]{1,0:T(8,128)(2,1)}) %all-gather.7.cloned.1.call-update) | async-done | bytes 7340048 | tf_op jit(solution)/shard_map/all_gather | solution.py:67
  209.7 8.5 %fusion.15 = bf16[512,3584]{1,0:T(8,128)(2,1)} fusion(bf16[1024,512]{1,0:T(8,128)(2,1)S(1)} %fusion.2, bf16[1024,3584]{1,0:T(8,128)(2,1)} %all-gather.7.cloned.1.call-done), kind=kOutput, calls=%fused_computation.40 | convolution fusion | flops 3758096384 | bytes 12058624 | tf_op jit(solution)/shard_map/td,tf->df/dot_general | solution.py:69
  218.3 40.5 %all-gather.9.cloned.1.call-done = bf16[1024,3584]{1,0:T(8,128)(2,1)} async-done(((bf16[64,3584]{1,0:T(8,128)(2,1)}), bf16[1024,3584]{1,0:T(8,128)(2,1)}) %all-gather.9.cloned.1.call-update) | async-done | bytes 7340048 | tf_op jit(solution)/shard_map/all_gather | solution.py:68
  258.8 7.5 %fusion.14 = f32[1024,512]{1,0:T(8,128)S(1)} fusion(bf16[1024,3584]{1,0:T(8,128)(2,1)} %all-gather.7.cloned.1.call-done, bf16[512,3584]{1,0:T(8,128)(2,1)} %param.13), kind=kOutput, calls=%fused_computation.39 | convolution fusion | flops 3758096384 | bytes 13107200 | tf_op jit(solution)/shard_map/tf,df->td/dot_general | solution.py:73
  266.3 4.1 %convert_bitcast_fusion = (bf16[128,8,512]{2,1,0:T(8,128)(2,1)S(1)}, f32[512]{0:T(512)S(1)}) fusion(f32[1024]{0:T(1024)S(1)} %bitcast.50, bf16[8,128,512]{2,1,0:T(8,128)(2,1)S(1)} %all-to-all-done.3, f32[1024,512]{1,0:T(8,128)S(1)} %fusion.14, bf16[1024,3584]{1,0:T(8,128)(2,1)S(1)} %copy-done.6, bf16[512,3584]{1,0:T(8,128)(2,1)S(1)} %copy-done.7), kind=kOutput, calls=%fused_computation.16 | convolution fusion | flops 3761241600 | bytes 15210496 | tf_op jit(solution)/shard_map/tf,df->td/dot_general | solution.py:74
  270.5 0.1 broadcast_in_dim.20
  270.7 1.8 pad_maximum_fusion.1
  272.4 8.7 %all-to-all-start.5 = ((bf16[128,10,512]{2,1,0:T(8,128)(2,1)}), bf16[128,10,512]{2,1,0:T(8,128)(2,1)S(1)}, u32[]{:S(2)}, u32[]{:S(2)}) async-start(bf16[128,10,512]{2,1,0:T(8,128)(2,1)} %pad_maximum_fusion.1), calls=%async_computation.6 | async-start | bytes 4194304 | tf_op jit(solution)/shard_map/all_to_all | solution.py:87
  281.2 9.4 %convolution_convert_fusion = bf16[512,3584]{1,0:T(8,128)(2,1)} fusion(bf16[1024,512]{1,0:T(8,128)(2,1)} %copy-done.3, bf16[1024,3584]{1,0:T(8,128)(2,1)} %all-gather.9.cloned.1.call-done), kind=kOutput, calls=%fused_computation | convolution fusion | flops 3759931392 | bytes 12058624 | tf_op jit(solution)/shard_map/td,tf->df/dot_general | solution.py:92
  290.6 22.4 %all-to-all-done.5 = bf16[128,10,512]{2,1,0:T(8,128)(2,1)S(1)} async-done(((bf16[128,10,512]{2,1,0:T(8,128)(2,1)}), bf16[128,10,512]{2,1,0:T(8,128)(2,1)S(1)}, u32[]{:S(2)}, u32[]{:S(2)}) %all-to-all-start.5) | async-done | bytes 1310752 | tf_op jit(solution)/shard_map/all_to_all | solution.py:87
  313.0 0.4 convert_reduce_fusion
  313.4 0.3 multiply_reduce_fusion
  313.6 0.6 slice_add_fusion
  314.3 0.8 add_convert_fusion
  315.1 7.4 %all-gather.11.cloned.1.call-done = bf16[1024,2560]{1,0:T(8,128)(2,1)} async-done(((bf16[64,2560]{1,0:T(8,128)(2,1)}), bf16[1024,2560]{1,0:T(8,128)(2,1)}) %all-gather.11.cloned.1.call-update) | async-done | bytes 5242896 | tf_op jit(solution)/shard_map/all_gather | solution.py:72
  322.5 5.7 %convolution_convert_fusion.1 = bf16[2560,512]{1,0:T(8,128)(2,1)S(1)} fusion(bf16[1024,2560]{1,0:T(8,128)(2,1)} %all-gather.11.cloned.1.call-done, bf16[1024,512]{1,0:T(8,128)(2,1)} %bitcast.3), kind=kOutput, calls=%fused_computation.1 | convolution fusion | flops 2685665280 | bytes 8912896 | tf_op jit(solution)/shard_map/tf,td->fd/dot_general | solution.py:93
  328.2 2.1 pad_maximum_fusion
  (27 shorter events, 0.2 us)
Async XLA Ops:
  7.2 50.9 %all-gather.5.cloned.1.call-start = ((), (), s32[]{:S(2)}) async-start(), calls=%async_computation.7 | async-start | bytes 2228224 | tf_op jit(solution)/shard_map/all_gather | solution.py:54
  9.3 135.6 %reduce-scatter.2.cloned.1.call-start = ((), (), s32[]{:S(2)}) async-start(), calls=%async_computation.8 | async-start | bytes 15597568 | tf_op jit(solution)/shard_map/reduce_scatter | solution.py:59
  58.1 86.8 %copy-start.1 = (bf16[64,3584]{1,0:T(8,128)(2,1)S(1)}, bf16[64,3584]{1,0:T(8,128)(2,1)}, u32[]{:S(2)}) copy-start(bf16[64,3584]{1,0:T(8,128)(2,1)} %param.12) | copy-start | bytes 1376260
  58.1 86.8 %copy-start.2 = (bf16[64,3584]{1,0:T(8,128)(2,1)S(1)}, bf16[64,3584]{1,0:T(8,128)(2,1)}, u32[]{:S(2)}) copy-start(bf16[64,3584]{1,0:T(8,128)(2,1)} %param.11) | copy-start | bytes 1376260
  58.1 151.6 %all-gather.7.cloned.1.call-start = ((), (), s32[]{:S(2)}) async-start(), calls=%async_computation.9 | async-start | bytes 7798784 | tf_op jit(solution)/shard_map/all_gather | solution.py:67
  61.4 86.7 %copy-start = (bf16[8,8192]{1,0:T(8,128)(2,1)S(1)}, bf16[8,8192]{1,0:T(8,128)(2,1)}, u32[]{:S(2)}) copy-start(bf16[8,8192]{1,0:T(8,128)(2,1)} %param.8) | copy-start | bytes 393220
  147.5 34.2 %copy-start.5 = (f32[8192]{0:T(1024)S(1)}, f32[8192]{0:T(1024)}, u32[]{:S(2)}) copy-start(f32[8192]{0:T(1024)} %param.9) | copy-start | bytes 98308
  147.5 111.2 %all-gather.9.cloned.1.call-start = ((), (), s32[]{:S(2)}) async-start(), calls=%async_computation.10 | async-start | bytes 7798784 | tf_op jit(solution)/shard_map/all_gather | solution.py:68
  163.1 12.9 %all-to-all-start.4 = ((f32[8,1,128]{2,1,0:T(1,128)}), f32[8,1,128]{2,1,0:T(1,128)S(1)}, u32[]{:S(2)}, u32[]{:S(2)}) async-start(f32[8,1,128]{2,1,0:T(1,128)} %broadcast_in_dim.19), calls=%async_computation.5 | async-start | bytes 8192 | tf_op jit(solution)/shard_map/all_to_all | solution.py:25
  177.1 21.3 %all-to-all-start.3 = ((bf16[8,128,512]{2,1,0:T(8,128)(2,1)}), bf16[8,128,512]{2,1,0:T(8,128)(2,1)S(1)}, u32[]{:S(2)}, u32[]{:S(2)}) async-start(bf16[8,128,512]{2,1,0:T(8,128)(2,1)} %broadcast_in_dim.17), calls=%async_computation.4 | async-start | bytes 2097152 | tf_op jit(solution)/shard_map/all_to_all | solution.py:25
  180.7 141.8 %all-gather.11.cloned.1.call-start = ((), (), s32[]{:S(2)}) async-start(), calls=%async_computation.11 | async-start | bytes 5570560 | tf_op jit(solution)/shard_map/all_gather | solution.py:72
  198.7 67.6 %copy-start.3 = (bf16[1024,512]{1,0:T(8,128)(2,1)}, bf16[1024,512]{1,0:T(8,128)(2,1)S(1)}, u32[]{:S(2)}) copy-start(bf16[1024,512]{1,0:T(8,128)(2,1)S(1)} %fusion.2) | copy-start | bytes 3145732
  258.8 7.5 %copy-start.6 = (bf16[1024,3584]{1,0:T(8,128)(2,1)S(1)}, bf16[1024,3584]{1,0:T(8,128)(2,1)}, u32[]{:S(2)}) copy-start(bf16[1024,3584]{1,0:T(8,128)(2,1)} %all-gather.9.cloned.1.call-done) | copy-start | bytes 22020100
  258.8 7.5 %copy-start.7 = (bf16[512,3584]{1,0:T(8,128)(2,1)S(1)}, bf16[512,3584]{1,0:T(8,128)(2,1)}, u32[]{:S(2)}) copy-start(bf16[512,3584]{1,0:T(8,128)(2,1)} %param.14) | copy-start | bytes 11010052
  272.4 40.5 %all-to-all-start.5 = ((bf16[128,10,512]{2,1,0:T(8,128)(2,1)}), bf16[128,10,512]{2,1,0:T(8,128)(2,1)S(1)}, u32[]{:S(2)}, u32[]{:S(2)}) async-start(bf16[128,10,512]{2,1,0:T(8,128)(2,1)} %pad_maximum_fusion.1), calls=%async_computation.6 | async-start | bytes 4194304 | tf_op jit(solution)/shard_map/all_to_all | solution.py:87
  290.6 23.7 %copy-start.4 = (bf16[8,8192]{1,0:T(8,128)(2,1)S(1)}, bf16[8,8192]{1,0:T(8,128)(2,1)}, u32[]{:S(2)}) copy-start(bf16[8,8192]{1,0:T(8,128)(2,1)} %param.10) | copy-start | bytes 393220
Sparse Core Ops, SparseCore 0:
  10.2 45.7 all-gather.4
  58.4 86.4 reduce-scatter.1
  147.7 62.0 all-gather.6
  211.9 46.8 all-gather.8
  260.3 62.1 all-gather.10

commit v12 on v10

--- a/solution.py
+++ b/solution.py
@@ -58,10 +58,12 @@
     hidden_piece, partial_grad = lax.optimization_barrier((hidden_piece, partial_grad))
     block_grad = lax.psum_scatter(partial_grad, "col", scatter_dimension=0, tiled=True)
     down_total = jnp.einsum("tf,td->fd", hidden_piece, all_grad, preferred_element_type=jnp.float32)
-    down_total, block_grad = lax.optimization_barrier((down_total, block_grad))
-    _, gate_block, up_block = swiglu_grads(block_grad, pre_gate, pre_up)
     all_tokens = row_gather(grid_tokens).astype(jnp.float32)
     all_scale = row_gather(grid_scale).reshape(-1, 1)
+    down_total, all_tokens, all_scale, block_grad = lax.optimization_barrier(
+        (down_total, all_tokens, all_scale, block_grad)
+    )
+    _, gate_block, up_block = swiglu_grads(block_grad, pre_gate, pre_up)
     all_normed = all_tokens * all_scale
     all_input = (all_normed * gain_tile).astype(jnp.bfloat16)
     gate_piece = lax.all_gather(gate_block, "col", axis=0, tiled=True)

time: 331 us -> 342 us (1.033)
  waiting for transfers between devices: 159 us -> 175 us
    reduce_scatter x1, waiting for transfers between devices: 84.9 us -> 0.01 us  [local(): lax.psum_scatter(partial_grad, 'col', scatter_dimension=0, tiled=True)]
    all_to_all x2, waiting for transfers between devices: 23.1 us -> 83.8 us  [row_gather(): got = lax.all_to_all(copies, 'row', split_axis=0, concat_axis=0, tiled=True)]
    all_gather x1, waiting for transfers between devices: 10.2 us -> 45.7 us  [local(): gate_piece = lax.all_gather(gate_block, 'col', axis=0, tiled=True)]
  transfers between devices with their start and end apart: 8 -> 8, of which waited for: 6 -> 5; matrix products, arithmetic and copies ran while one was open for 16% -> 14% of each run, Pallas kernels for 0% -> 0%
where the time goes in v12:
time: 342 us; the launch traced here: 341 us
  waiting for transfers between devices  175 us (51%)
  blocking collectives  74.7 us (22%)
  matrix products  48.9 us (14%)
  between operations  14 us (4%)
  starting transfers between devices  13.7 us (4%)
  other arithmetic  8.95 us (3%)
  local copies, waits for them, and re-layouts  5.91 us (2%)
    all_to_all x2, waiting for transfers between devices, row_gather(): got = lax.all_to_all(copies, 'row', split_axis=0, concat_axis=0, tiled=True)  83.8 us
    all_gather x1, waiting for transfers between devices, local(): gate_piece = lax.all_gather(gate_block, 'col', axis=0, tiled=True)  45.7 us
    all_gather x1, waiting for transfers between devices, local(): up_piece = lax.all_gather(up_block, 'col', axis=0, tiled=True)  41.5 us
    all_to_all x1, blocking collectives, local(): got = lax.all_to_all(sent, 'row', split_axis=0, concat_axis=0, tiled=True)  25 us
    all_to_all x1, blocking collectives, row_gather(): got = lax.all_to_all(copies, 'row', split_axis=0, concat_axis=0, tiled=True)  23.2 us
    all_to_all x1, blocking collectives, local(): lax.all_to_all(grad_out, 'col', split_axis=1, concat_axis=0, tiled=True)  13.4 us
    all_to_all x1, blocking collectives, local(): lax.all_to_all(packed, 'col', split_axis=1, concat_axis=0, tiled=True)  13.1 us
    dot_general x1, matrix products, local(): jnp.einsum('td,fd->tf', all_grad, down_weight, preferred_element_type=jnp...  9.77 us
  transfers between devices with their start and end apart: 8, of which 5 were waited for; matrix products, arithmetic and copies ran while one was open for 14% of the time, Pallas kernels for 0%

profile of v12, /device:TPU:1, one launch (start us, length us, event | category | flops | bytes accessed | tf_op | source)
XLA Modules:
  0.0 341.1 jit_solution(18334850561579451915)
XLA Ops:
  7.2 0.0 all-gather.5.cloned.1.call-start
  7.2 1.4 fusion
  8.7 0.8 copy-done.1
  9.4 0.7 slice.76
  10.1 0.0 reduce-scatter.2.cloned.1.call-start
  10.2 13.4 %all_to_all.56 = bf16[8,16,512]{2,0,1:T(8,128)(2,1)S(1)} all-to-all(bf16[8,16,512]{2,0,1:T(8,128)(2,1)} %bitcast.47), channel_id=1, replica_groups=mesh['row'=8,'col'=16] {'col'}, dimensions={1} | all-to-all | bytes 262144 | tf_op jit(solution)/shard_map/all_to_all | solution.py:39
  23.6 0.1 broadcast_in_dim.15
  23.7 23.2 %all_to_all.57 = bf16[8,128,512]{2,1,0:T(8,128)(2,1)S(1)} all-to-all(bf16[8,128,512]{2,1,0:T(8,128)(2,1)S(1)} %broadcast_in_dim.15), channel_id=1, replica_groups=mesh['row'=8,'col'=16] {'row'}, dimensions={0} | all-to-all | bytes 2097152 | tf_op jit(solution)/shard_map/all_to_all | solution.py:25
  46.8 9.8 %fusion.10 = f32[1024,3584]{1,0:T(8,128)} fusion(bf16[1024,512]{1,0:T(8,128)(2,1)S(1)} %bitcast.40, bf16[3584,512]{1,0:T(8,128)(2,1)} %param.19), kind=kOutput, calls=%fused_computation.37 | convolution fusion | flops 3758096384 | bytes 19398656 | tf_op jit(solution)/shard_map/td,fd->tf/dot_general | solution.py:55
  56.6 0.0 all-gather.5.cloned.1.call-done
  56.6 0.9 copy-done
  57.5 0.2 multiply_reduce_fusion.2
  57.7 0.1 broadcast_in_dim.16
  57.8 13.1 %all_to_all.58 = f32[8,16,640]{2,0,1:T(8,128)S(1)} all-to-all(f32[8,16,640]{2,0,1:T(8,128)S(1)} %pad_maximum_fusion.3), channel_id=1, replica_groups=mesh['row'=8,'col'=16] {'col'}, dimensions={1} | all-to-all | bytes 655360 | tf_op jit(solution)/shard_map/all_to_all | solution.py:47
  70.9 1.1 broadcast_in_dim.17
  72.0 4.1 %all-to-all-start.3 = ((bf16[8,128,512]{2,1,0:T(8,128)(2,1)}), bf16[8,128,512]{2,1,0:T(8,128)(2,1)S(1)}, u32[]{:S(2)}, u32[]{:S(2)}) async-start(bf16[8,128,512]{2,1,0:T(8,128)(2,1)} %broadcast_in_dim.17), calls=%async_computation.3 | async-start | bytes 2097152 | tf_op jit(solution)/shard_map/all_to_all | solution.py:25
  76.1 0.1 slice_reduce_fusion
  76.2 81.9 %all-to-all-done.3 = bf16[8,128,512]{2,1,0:T(8,128)(2,1)S(1)} async-done(((bf16[8,128,512]{2,1,0:T(8,128)(2,1)}), bf16[8,128,512]{2,1,0:T(8,128)(2,1)S(1)}, u32[]{:S(2)}, u32[]{:S(2)}) %all-to-all-start.3) | async-done | bytes 1048608 | tf_op jit(solution)/shard_map/all_to_all | solution.py:25
  158.1 0.6 broadcast_in_dim.19
  158.7 4.0 %all-to-all-start.4 = ((f32[8,1,128]{2,1,0:T(1,128)}), f32[8,1,128]{2,1,0:T(1,128)S(1)}, u32[]{:S(2)}, u32[]{:S(2)}) async-start(f32[8,1,128]{2,1,0:T(1,128)} %broadcast_in_dim.19), calls=%async_computation.4 | async-start | bytes 8192 | tf_op jit(solution)/shard_map/all_to_all | solution.py:25
  162.7 0.0 all-gather.7.cloned.1.call-start
  162.8 0.3 bitcast_convert_fusion
  163.1 4.2 %fusion.11 = bf16[1024,512]{1,0:T(8,128)(2,1)} fusion(bf16[1024,1024]{1,0:T(8,128)(2,1)} %all-gather.5.cloned.1.call-done, bf16[1024,512]{1,0:T(8,128)(2,1)} %bitcast.41), kind=kOutput, calls=%fused_computation.38 | convolution fusion | flops 1073741824 | bytes 4194304 | tf_op jit(solution)/shard_map/tf,td->fd/dot_general | solution.py:60
  167.3 1.9 all-to-all-done.4
  169.2 2.7 multiply_convert_fusion.1
  171.9 0.0 all-gather.9.cloned.1.call-start
  171.9 0.5 all-gather.9.cloned.1.call-update
  172.5 0.0 all-gather.11.cloned.1.call-start
  172.5 0.8 slice.79
  173.3 0.1 dynamic_slice.3
  173.3 45.7 %all-gather.7.cloned.1.call-done = bf16[1024,3584]{1,0:T(8,128)(2,1)} async-done(((bf16[64,3584]{1,0:T(8,128)(2,1)}), bf16[1024,3584]{1,0:T(8,128)(2,1)}) %all-gather.7.cloned.1.call-update) | async-done | bytes 7340048 | tf_op jit(solution)/shard_map/all_gather | solution.py:69
  219.0 8.7 %fusion.8 = bf16[512,3584]{1,0:T(8,128)(2,1)} fusion(bf16[1024,3584]{1,0:T(8,128)(2,1)} %all-gather.7.cloned.1.call-done, f32[1024,512]{1,0:T(8,128)S(1)} %bitcast_convert_fusion, f32[512]{0:T(512)S(1)} %dynamic_slice.3, f32[1024]{0:T(1024)S(1)} %bitcast.50), kind=kOutput, calls=%fused_computation.35 | convolution fusion | flops 3759669248 | bytes 13113344 | tf_op jit(solution)/shard_map/td,tf->df/dot_general | solution.py:71
  227.7 41.5 %all-gather.9.cloned.1.call-done = bf16[1024,3584]{1,0:T(8,128)(2,1)} async-done(((bf16[64,3584]{1,0:T(8,128)(2,1)}), bf16[1024,3584]{1,0:T(8,128)(2,1)}) %all-gather.9.cloned.1.call-update) | async-done | bytes 7340048 | tf_op jit(solution)/shard_map/all_gather | solution.py:70
  269.2 7.5 %fusion.12 = f32[1024,512]{1,0:T(8,128)S(1)} fusion(bf16[1024,3584]{1,0:T(8,128)(2,1)} %all-gather.7.cloned.1.call-done, bf16[512,3584]{1,0:T(8,128)(2,1)} %param.17), kind=kOutput, calls=%fused_computation.39 | convolution fusion | flops 3758096384 | bytes 13107200 | tf_op jit(solution)/shard_map/tf,df->td/dot_general | solution.py:75
  276.8 4.1 %fusion.9 = (bf16[1024,512]{1,0:T(8,128)(2,1)S(1)}, f32[512]{0:T(512)S(1)}) fusion(f32[1024,512]{1,0:T(8,128)S(1)} %bitcast_convert_fusion, f32[1024]{0:T(1024)S(1)} %bitcast.51, f32[1024,512]{1,0:T(8,128)S(1)} %fusion.12, bf16[1024,3584]{1,0:T(8,128)(2,1)S(1)} %copy-done.8, bf16[512,3584]{1,0:T(8,128)(2,1)S(1)} %copy-done.9), kind=kOutput, calls=%fused_computation.36 | convolution fusion | flops 3760717312 | bytes 16259072 | tf_op jit(solution)/shard_map/tf,df->td/dot_general | solution.py:76
  280.9 0.1 scatter.9
  281.0 0.1 pad_maximum_fusion.1
  281.1 25.0 %all_to_all.59 = bf16[8,136,512]{2,1,0:T(8,128)(2,1)S(1)} all-to-all(bf16[8,136,512]{2,1,0:T(8,128)(2,1)S(1)} %pad_maximum_fusion.1), channel_id=1, replica_groups=mesh['row'=8,'col'=16] {'row'}, dimensions={0} | all-to-all | bytes 2228224 | tf_op jit(solution)/shard_map/all_to_all | solution.py:87
  306.1 0.2 convert_reduce_fusion
  306.4 0.9 pad_maximum_fusion.2
  307.2 5.4 %all-to-all-start.6 = ((f32[16,9,512]{2,1,0:T(8,128)}), f32[16,9,512]{2,1,0:T(8,128)S(1)}, u32[]{:S(2)}, u32[]{:S(2)}) async-start(f32[16,9,512]{2,1,0:T(8,128)} %pad_maximum_fusion.2), calls=%async_computation.7 | async-start | bytes 1048576 | tf_op jit(solution)/shard_map/all_to_all | solution.py:96
  312.7 8.9 %convolution_convert_fusion = bf16[512,3584]{1,0:T(8,128)(2,1)} fusion(bf16[1024,3584]{1,0:T(8,128)(2,1)} %all-gather.9.cloned.1.call-done, f32[1024,512]{1,0:T(8,128)S(1)} %bitcast_convert_fusion, f32[512]{0:T(512)S(1)} %dynamic_slice.3, f32[1024]{0:T(1024)S(1)} %bitcast.52), kind=kOutput, calls=%fused_computation | convolution fusion | flops 3761504256 | bytes 13113344 | tf_op jit(solution)/shard_map/td,tf->df/dot_general | solution.py:99
  321.6 3.3 all-to-all-done.6
  325.0 0.6 slice.84
  325.6 0.3 multiply_reduce_fusion.1
  325.9 0.8 add_convert_fusion
  326.7 5.8 %convolution_convert_fusion.1 = bf16[2560,512]{1,0:T(8,128)(2,1)S(1)} fusion(bf16[1024,2560]{1,0:T(8,128)(2,1)} %all-gather.11.cloned.1.call-done, bf16[1024,512]{1,0:T(8,128)(2,1)} %bitcast.42), kind=kOutput, calls=%fused_computation.1 | convolution fusion | flops 2685665280 | bytes 8912896 | tf_op jit(solution)/shard_map/tf,td->fd/dot_general | solution.py:100
  332.5 2.1 pad_maximum_fusion
  (37 shorter events, 0.3 us)
Async XLA Ops:
  7.2 49.4 %all-gather.5.cloned.1.call-start = ((), (), s32[]{:S(2)}) async-start(), calls=%async_computation.8 | async-start | bytes 2228224 | tf_op jit(solution)/shard_map/all_gather | solution.py:54
  8.6 0.8 copy-start.1
  10.1 159.1 %reduce-scatter.2.cloned.1.call-start = ((), (), s32[]{:S(2)}) async-start(), calls=%async_computation.9 | async-start | bytes 15597568 | tf_op jit(solution)/shard_map/reduce_scatter | solution.py:59
  46.8 9.8 %copy-start.5 = (bf16[8,128,512]{2,1,0:T(8,128)(2,1)}, bf16[8,128,512]{2,1,0:T(8,128)(2,1)S(1)}, u32[]{:S(2)}) copy-start(bf16[8,128,512]{2,1,0:T(8,128)(2,1)S(1)} %all_to_all.57) | copy-start | bytes 3145732
  56.6 0.9 copy-start
  72.0 86.1 %all-to-all-start.3 = ((bf16[8,128,512]{2,1,0:T(8,128)(2,1)}), bf16[8,128,512]{2,1,0:T(8,128)(2,1)S(1)}, u32[]{:S(2)}, u32[]{:S(2)}) async-start(bf16[8,128,512]{2,1,0:T(8,128)(2,1)} %broadcast_in_dim.17), calls=%async_computation.3 | async-start | bytes 2097152 | tf_op jit(solution)/shard_map/all_to_all | solution.py:25
  158.7 10.4 %all-to-all-start.4 = ((f32[8,1,128]{2,1,0:T(1,128)}), f32[8,1,128]{2,1,0:T(1,128)S(1)}, u32[]{:S(2)}, u32[]{:S(2)}) async-start(f32[8,1,128]{2,1,0:T(1,128)} %broadcast_in_dim.19), calls=%async_computation.4 | async-start | bytes 8192 | tf_op jit(solution)/shard_map/all_to_all | solution.py:25
  162.7 56.3 %all-gather.7.cloned.1.call-start = ((), (), s32[]{:S(2)}) async-start(), calls=%async_computation.10 | async-start | bytes 7798784 | tf_op jit(solution)/shard_map/all_gather | solution.py:69
  163.1 6.1 %copy-start.3 = (bf16[64,3584]{1,0:T(8,128)(2,1)S(1)}, bf16[64,3584]{1,0:T(8,128)(2,1)}, u32[]{:S(2)}) copy-start(bf16[64,3584]{1,0:T(8,128)(2,1)} %param.16) | copy-start | bytes 1376260
  167.3 5.2 %copy-start.2 = (bf16[64,3584]{1,0:T(8,128)(2,1)S(1)}, bf16[64,3584]{1,0:T(8,128)(2,1)}, u32[]{:S(2)}) copy-start(bf16[64,3584]{1,0:T(8,128)(2,1)} %copy-done.1) | copy-start | bytes 1376260
  167.3 6.0 %copy-start.7 = (f32[8192]{0:T(1024)S(1)}, f32[8192]{0:T(1024)}, u32[]{:S(2)}) copy-start(f32[8192]{0:T(1024)} %param.13) | copy-start | bytes 98308
  171.9 97.3 %all-gather.9.cloned.1.call-start = ((), (), s32[]{:S(2)}) async-start(), calls=%async_computation.11 | async-start | bytes 7798784 | tf_op jit(solution)/shard_map/all_gather | solution.py:70
  172.5 154.2 %all-gather.11.cloned.1.call-start = ((), (), s32[]{:S(2)}) async-start(), calls=%async_computation.12 | async-start | bytes 5570560 | tf_op jit(solution)/shard_map/all_gather | solution.py:74
  269.2 7.5 %copy-start.8 = (bf16[1024,3584]{1,0:T(8,128)(2,1)S(1)}, bf16[1024,3584]{1,0:T(8,128)(2,1)}, u32[]{:S(2)}) copy-start(bf16[1024,3584]{1,0:T(8,128)(2,1)} %all-gather.9.cloned.1.call-done) | copy-start | bytes 22020100
  269.2 7.5 %copy-start.9 = (bf16[512,3584]{1,0:T(8,128)(2,1)S(1)}, bf16[512,3584]{1,0:T(8,128)(2,1)}, u32[]{:S(2)}) copy-start(bf16[512,3584]{1,0:T(8,128)(2,1)} %param.18) | copy-start | bytes 11010052
  307.2 17.7 %all-to-all-start.6 = ((f32[16,9,512]{2,1,0:T(8,128)}), f32[16,9,512]{2,1,0:T(8,128)S(1)}, u32[]{:S(2)}, u32[]{:S(2)}) async-start(f32[16,9,512]{2,1,0:T(8,128)} %pad_maximum_fusion.2), calls=%async_computation.7 | async-start | bytes 1048576 | tf_op jit(solution)/shard_map/all_to_all | solution.py:96
  312.7 13.2 %copy-start.6 = (bf16[8,8192]{1,0:T(8,128)(2,1)S(1)}, bf16[8,8192]{1,0:T(8,128)(2,1)}, u32[]{:S(2)}) copy-start(bf16[8,8192]{1,0:T(8,128)(2,1)} %param.14) | copy-start | bytes 393220
  326.7 5.8 %copy-start.4 = (bf16[1024,512]{1,0:T(8,128)(2,1)S(1)}, bf16[1024,512]{1,0:T(8,128)(2,1)}, u32[]{:S(2)}) copy-start(bf16[1024,512]{1,0:T(8,128)(2,1)} %fusion.11) | copy-start | bytes 3145732
Sparse Core Ops, SparseCore 0:
  10.2 46.3 all-gather.4
  59.0 94.2 reduce-scatter.1
  172.0 46.9 all-gather.6
  221.2 47.9 all-gather.8
  270.7 55.8 all-gather.10

commit v13 on v10

--- a/solution.py
+++ b/solution.py
@@ -50,7 +50,7 @@
     grid_scale = grid[:, tile : tile + 1].reshape(1, cols * mine_rows)
     all_grad = row_gather(grid_grad)
     hidden_block = swiglu_grads(jnp.zeros(pre_gate.shape, jnp.float32), pre_gate, pre_up)[0]
-    split = (hidden_block.shape[1] // 448) * 128
+    split = (hidden_block.shape[1] // 512) * 128
     hidden_piece = lax.all_gather(hidden_block[:, :split], "col", axis=0, tiled=True)
     partial_grad = jnp.einsum(
         "td,fd->tf", all_grad, down_weight, preferred_element_type=jnp.float32

time: 331 us -> 332 us (level)
  waiting for transfers between devices: 159 us -> 163 us
  transfers between devices with their start and end apart: 8 -> 8, of which waited for: 6 -> 7; matrix products, arithmetic and copies ran while one was open for 16% -> 15% of each run, Pallas kernels for 0% -> 0%
where the time goes in v13:
time: 332 us; the launch traced here: 331 us
  waiting for transfers between devices  163 us (49%)
  blocking collectives  76.2 us (23%)
  matrix products  48.8 us (15%)
  starting transfers between devices  15.5 us (5%)
  between operations  14 us (4%)
  other arithmetic  9.97 us (3%)
  local copies, waits for them, and re-layouts  4.29 us (1%)
    reduce_scatter x1, waiting for transfers between devices, local(): lax.psum_scatter(partial_grad, 'col', scatter_dimension=0, tiled=True)  84.9 us
    all_gather x1, waiting for transfers between devices, local(): up_piece = lax.all_gather(up_block, 'col', axis=0, tiled=True)  40.3 us
    all_to_all x1, blocking collectives, local(): got = lax.all_to_all(sent, 'row', split_axis=0, concat_axis=0, tiled=True)  24.9 us
    all_to_all x1, blocking collectives, row_gather(): got = lax.all_to_all(copies, 'row', split_axis=0, concat_axis=0, tiled=True)  23.6 us
    all_to_all x2, waiting for transfers between devices, row_gather(): got = lax.all_to_all(copies, 'row', split_axis=0, concat_axis=0, tiled=True)  23.3 us
    all_to_all x1, blocking collectives, local(): lax.all_to_all(packed, 'col', split_axis=1, concat_axis=0, tiled=True)  14.3 us
    all_to_all x1, blocking collectives, local(): lax.all_to_all(grad_out, 'col', split_axis=1, concat_axis=0, tiled=True)  13.4 us
    all_gather x1, waiting for transfers between devices, local(): gate_piece = lax.all_gather(gate_block, 'col', axis=0, tiled=True)  11.2 us
  transfers between devices with their start and end apart: 8, of which 7 were waited for; matrix products, arithmetic and copies ran while one was open for 15% of the time, Pallas kernels for 0%

profile of v13, /device:TPU:1, one launch (start us, length us, event | category | flops | bytes accessed | tf_op | source)
XLA Modules:
  0.0 331.5 jit_solution(5552041930840474770)
XLA Ops:
  7.2 0.0 all-gather.5.cloned.1.call-start
  7.2 1.4 fusion.4
  8.6 0.7 slice.76
  9.3 0.0 reduce-scatter.2.cloned.1.call-start
  9.4 13.4 %all_to_all.56 = bf16[8,16,512]{2,0,1:T(8,128)(2,1)S(1)} all-to-all(bf16[8,16,512]{2,0,1:T(8,128)(2,1)} %bitcast.49), channel_id=1, replica_groups=mesh['row'=8,'col'=16] {'col'}, dimensions={1} | all-to-all | bytes 262144 | tf_op jit(solution)/shard_map/all_to_all | solution.py:39
  22.8 0.1 broadcast_in_dim.15
  22.9 23.6 %all_to_all.57 = bf16[8,128,512]{2,1,0:T(8,128)(2,1)S(1)} all-to-all(bf16[8,128,512]{2,1,0:T(8,128)(2,1)S(1)} %broadcast_in_dim.15), channel_id=1, replica_groups=mesh['row'=8,'col'=16] {'row'}, dimensions={0} | all-to-all | bytes 2097152 | tf_op jit(solution)/shard_map/all_to_all | solution.py:25
  46.4 9.4 %fusion.13 = f32[1024,3584]{1,0:T(8,128)} fusion(bf16[1024,512]{1,0:T(8,128)(2,1)S(1)} %bitcast.42, bf16[3584,512]{1,0:T(8,128)(2,1)} %param.19), kind=kOutput, calls=%fused_computation.38 | convolution fusion | flops 3758096384 | bytes 19398656 | tf_op jit(solution)/shard_map/td,fd->tf/dot_general | solution.py:55
  55.8 0.0 reduce-scatter.2.cloned.1.call-update
  55.8 0.0 all-gather.7.cloned.1.call-start
  55.9 3.6 %fusion.14 = bf16[896,512]{1,0:T(8,128)(2,1)} fusion(bf16[1024,896]{1,0:T(8,128)(2,1)} %all-gather.5.cloned.1.call-done, bf16[1024,512]{1,0:T(8,128)(2,1)S(1)} %bitcast.43), kind=kOutput, calls=%fused_computation.39 | convolution fusion | flops 939524096 | bytes 3801088 | tf_op jit(solution)/shard_map/tf,td->fd/dot_general | solution.py:60
  59.5 84.9 %reduce-scatter.2.cloned.1.call-done = f32[64,3584]{1,0:T(8,128)} async-done(((f32[1024,3584]{1,0:T(8,128)}), f32[64,3584]{1,0:T(8,128)}) %reduce-scatter.2.cloned.1.call-update) | async-done | bytes 917520 | tf_op jit(solution)/shard_map/reduce_scatter | solution.py:59
  144.4 2.5 multiply_convert_fusion
  147.0 0.0 all-gather.9.cloned.1.call-start
  147.0 0.5 all-gather.9.cloned.1.call-update
  147.6 0.2 multiply_reduce_fusion.1
  147.8 0.1 broadcast_in_dim.16
  147.9 14.3 %all_to_all.58 = f32[8,16,640]{2,0,1:T(8,128)S(1)} all-to-all(f32[8,16,640]{2,0,1:T(8,128)S(1)} %pad_maximum_fusion.3), channel_id=1, replica_groups=mesh['row'=8,'col'=16] {'col'}, dimensions={1} | all-to-all | bytes 655360 | tf_op jit(solution)/shard_map/all_to_all | solution.py:47
  162.2 0.1 slice_reduce_fusion
  162.3 0.6 broadcast_in_dim.19
  162.9 6.1 %all-to-all-start.4 = ((f32[8,1,128]{2,1,0:T(1,128)}), f32[8,1,128]{2,1,0:T(1,128)S(1)}, u32[]{:S(2)}, u32[]{:S(2)}) async-start(f32[8,1,128]{2,1,0:T(1,128)} %broadcast_in_dim.19), calls=%async_computation.5 | async-start | bytes 8192 | tf_op jit(solution)/shard_map/all_to_all | solution.py:25
  169.1 6.4 %all-to-all-done.4 = f32[8,1,128]{2,1,0:T(1,128)S(1)} async-done(((f32[8,1,128]{2,1,0:T(1,128)}), f32[8,1,128]{2,1,0:T(1,128)S(1)}, u32[]{:S(2)}, u32[]{:S(2)}) %all-to-all-start.4) | async-done | bytes 4128 | tf_op jit(solution)/shard_map/all_to_all | solution.py:25
  175.5 1.1 broadcast_in_dim.17
  176.6 3.6 %all-to-all-start.3 = ((bf16[8,128,512]{2,1,0:T(8,128)(2,1)}), bf16[8,128,512]{2,1,0:T(8,128)(2,1)S(1)}, u32[]{:S(2)}, u32[]{:S(2)}) async-start(bf16[8,128,512]{2,1,0:T(8,128)(2,1)} %broadcast_in_dim.17), calls=%async_computation.4 | async-start | bytes 2097152 | tf_op jit(solution)/shard_map/all_to_all | solution.py:25
  180.1 0.0 all-gather.11.cloned.1.call-start
  180.2 0.8 slice.77
  181.0 0.1 dynamic_slice.3
  181.0 16.9 %all-to-all-done.3 = bf16[8,128,512]{2,1,0:T(8,128)(2,1)S(1)} async-done(((bf16[8,128,512]{2,1,0:T(8,128)(2,1)}), bf16[8,128,512]{2,1,0:T(8,128)(2,1)S(1)}, u32[]{:S(2)}, u32[]{:S(2)}) %all-to-all-start.3) | async-done | bytes 1048608 | tf_op jit(solution)/shard_map/all_to_all | solution.py:25
  197.9 0.3 fusion.2
  198.2 11.2 %all-gather.7.cloned.1.call-done = bf16[1024,3584]{1,0:T(8,128)(2,1)} async-done(((bf16[64,3584]{1,0:T(8,128)(2,1)}), bf16[1024,3584]{1,0:T(8,128)(2,1)}) %all-gather.7.cloned.1.call-update) | async-done | bytes 7340048 | tf_op jit(solution)/shard_map/all_gather | solution.py:67
  209.4 8.5 %fusion.16 = bf16[512,3584]{1,0:T(8,128)(2,1)} fusion(bf16[1024,512]{1,0:T(8,128)(2,1)S(1)} %fusion.2, bf16[1024,3584]{1,0:T(8,128)(2,1)} %all-gather.7.cloned.1.call-done), kind=kOutput, calls=%fused_computation.41 | convolution fusion | flops 3758096384 | bytes 12058624 | tf_op jit(solution)/shard_map/td,tf->df/dot_general | solution.py:69
  217.9 40.3 %all-gather.9.cloned.1.call-done = bf16[1024,3584]{1,0:T(8,128)(2,1)} async-done(((bf16[64,3584]{1,0:T(8,128)(2,1)}), bf16[1024,3584]{1,0:T(8,128)(2,1)}) %all-gather.9.cloned.1.call-update) | async-done | bytes 7340048 | tf_op jit(solution)/shard_map/all_gather | solution.py:68
  258.2 7.5 %fusion.15 = f32[1024,512]{1,0:T(8,128)S(1)} fusion(bf16[1024,3584]{1,0:T(8,128)(2,1)} %all-gather.7.cloned.1.call-done, bf16[512,3584]{1,0:T(8,128)(2,1)} %param.17), kind=kOutput, calls=%fused_computation.40 | convolution fusion | flops 3758096384 | bytes 13107200 | tf_op jit(solution)/shard_map/tf,df->td/dot_general | solution.py:73
  265.8 5.1 %fusion.12 = (bf16[1024,512]{1,0:T(8,128)(2,1)}, f32[512]{0:T(512)S(1)}) fusion(f32[1024]{0:T(1024)S(1)} %bitcast.52, bf16[8,128,512]{2,1,0:T(8,128)(2,1)S(1)} %all-to-all-done.3, f32[1024,512]{1,0:T(8,128)S(1)} %fusion.15, bf16[1024,3584]{1,0:T(8,128)(2,1)S(1)} %copy-done.6, bf16[512,3584]{1,0:T(8,128)(2,1)S(1)} %copy-done.7), kind=kOutput, calls=%fused_computation.37 | convolution fusion | flops 3761241600 | bytes 15210496 | tf_op jit(solution)/shard_map/tf,df->td/dot_general | solution.py:74
  270.9 0.1 scatter.9
  271.0 1.3 pad_maximum_fusion.1
  272.3 24.9 %all_to_all.59 = bf16[8,136,512]{2,1,0:T(8,128)(2,1)S(1)} all-to-all(bf16[8,136,512]{2,1,0:T(8,128)(2,1)S(1)} %pad_maximum_fusion.1), channel_id=1, replica_groups=mesh['row'=8,'col'=16] {'row'}, dimensions={0} | all-to-all | bytes 2228224 | tf_op jit(solution)/shard_map/all_to_all | solution.py:85
  297.2 0.2 convert_reduce_fusion
  297.5 0.9 pad_maximum_fusion.2
  298.3 5.6 %all-to-all-start.6 = ((f32[16,9,512]{2,1,0:T(8,128)}), f32[16,9,512]{2,1,0:T(8,128)S(1)}, u32[]{:S(2)}, u32[]{:S(2)}) async-start(f32[16,9,512]{2,1,0:T(8,128)} %pad_maximum_fusion.2), calls=%async_computation.7 | async-start | bytes 1048576 | tf_op jit(solution)/shard_map/all_to_all | solution.py:94
  303.9 8.7 %convolution_convert_fusion = bf16[512,3584]{1,0:T(8,128)(2,1)} fusion(bf16[1024,512]{1,0:T(8,128)(2,1)S(1)} %fusion.2, bf16[1024,3584]{1,0:T(8,128)(2,1)} %all-gather.9.cloned.1.call-done), kind=kOutput, calls=%fused_computation | convolution fusion | flops 3759931392 | bytes 12058624 | tf_op jit(solution)/shard_map/td,tf->df/dot_general | solution.py:97
  312.6 2.5 all-to-all-done.6
  315.1 0.6 slice.84
  315.8 0.3 multiply_reduce_fusion
  316.0 0.8 add_convert_fusion
  316.8 0.1 all-gather.11.cloned.1.call-done
  316.9 6.0 %convolution_convert_fusion.1 = bf16[2688,512]{1,0:T(8,128)(2,1)S(1)} fusion(bf16[1024,2688]{1,0:T(8,128)(2,1)} %all-gather.11.cloned.1.call-done, bf16[1024,512]{1,0:T(8,128)(2,1)S(1)} %bitcast.44), kind=kOutput, calls=%fused_computation.1 | convolution fusion | flops 2819948544 | bytes 9306112 | tf_op jit(solution)/shard_map/tf,td->fd/dot_general | solution.py:98
  322.9 2.1 pad_maximum_fusion
  (33 shorter events, 0.3 us)
Async XLA Ops:
  7.2 48.6 %all-gather.5.cloned.1.call-start = ((), (), s32[]{:S(2)}) async-start(), calls=%async_computation.8 | async-start | bytes 1949696 | tf_op jit(solution)/shard_map/all_gather | solution.py:54
  9.3 135.1 %reduce-scatter.2.cloned.1.call-start = ((), (), s32[]{:S(2)}) async-start(), calls=%async_computation.9 | async-start | bytes 15597568 | tf_op jit(solution)/shard_map/reduce_scatter | solution.py:59
  55.8 88.6 %copy-start.1 = (bf16[64,3584]{1,0:T(8,128)(2,1)S(1)}, bf16[64,3584]{1,0:T(8,128)(2,1)}, u32[]{:S(2)}) copy-start(bf16[64,3584]{1,0:T(8,128)(2,1)} %param.16) | copy-start | bytes 1376260
  55.8 88.6 %copy-start.2 = (bf16[64,3584]{1,0:T(8,128)(2,1)S(1)}, bf16[64,3584]{1,0:T(8,128)(2,1)}, u32[]{:S(2)}) copy-start(bf16[64,3584]{1,0:T(8,128)(2,1)} %param.15) | copy-start | bytes 1376260
  55.8 153.5 %all-gather.7.cloned.1.call-start = ((), (), s32[]{:S(2)}) async-start(), calls=%async_computation.10 | async-start | bytes 7798784 | tf_op jit(solution)/shard_map/all_gather | solution.py:67
  59.5 88.0 %copy-start = (bf16[8,8192]{1,0:T(8,128)(2,1)S(1)}, bf16[8,8192]{1,0:T(8,128)(2,1)}, u32[]{:S(2)}) copy-start(bf16[8,8192]{1,0:T(8,128)(2,1)} %param.12) | copy-start | bytes 393220
  146.9 34.0 %copy-start.5 = (f32[8192]{0:T(1024)S(1)}, f32[8192]{0:T(1024)}, u32[]{:S(2)}) copy-start(f32[8192]{0:T(1024)} %param.13) | copy-start | bytes 98308
  147.0 111.2 %all-gather.9.cloned.1.call-start = ((), (), s32[]{:S(2)}) async-start(), calls=%async_computation.11 | async-start | bytes 7798784 | tf_op jit(solution)/shard_map/all_gather | solution.py:68
  162.9 12.6 %all-to-all-start.4 = ((f32[8,1,128]{2,1,0:T(1,128)}), f32[8,1,128]{2,1,0:T(1,128)S(1)}, u32[]{:S(2)}, u32[]{:S(2)}) async-start(f32[8,1,128]{2,1,0:T(1,128)} %broadcast_in_dim.19), calls=%async_computation.5 | async-start | bytes 8192 | tf_op jit(solution)/shard_map/all_to_all | solution.py:25
  176.6 21.3 %all-to-all-start.3 = ((bf16[8,128,512]{2,1,0:T(8,128)(2,1)}), bf16[8,128,512]{2,1,0:T(8,128)(2,1)S(1)}, u32[]{:S(2)}, u32[]{:S(2)}) async-start(bf16[8,128,512]{2,1,0:T(8,128)(2,1)} %broadcast_in_dim.17), calls=%async_computation.4 | async-start | bytes 2097152 | tf_op jit(solution)/shard_map/all_to_all | solution.py:25
  180.1 136.8 %all-gather.11.cloned.1.call-start = ((), (), s32[]{:S(2)}) async-start(), calls=%async_computation.12 | async-start | bytes 5849088 | tf_op jit(solution)/shard_map/all_gather | solution.py:72
  258.2 7.5 %copy-start.6 = (bf16[1024,3584]{1,0:T(8,128)(2,1)S(1)}, bf16[1024,3584]{1,0:T(8,128)(2,1)}, u32[]{:S(2)}) copy-start(bf16[1024,3584]{1,0:T(8,128)(2,1)} %all-gather.9.cloned.1.call-done) | copy-start | bytes 22020100
  258.2 7.5 %copy-start.7 = (bf16[512,3584]{1,0:T(8,128)(2,1)S(1)}, bf16[512,3584]{1,0:T(8,128)(2,1)}, u32[]{:S(2)}) copy-start(bf16[512,3584]{1,0:T(8,128)(2,1)} %param.18) | copy-start | bytes 11010052
  298.3 16.8 %all-to-all-start.6 = ((f32[16,9,512]{2,1,0:T(8,128)}), f32[16,9,512]{2,1,0:T(8,128)S(1)}, u32[]{:S(2)}, u32[]{:S(2)}) async-start(f32[16,9,512]{2,1,0:T(8,128)} %pad_maximum_fusion.2), calls=%async_computation.7 | async-start | bytes 1048576 | tf_op jit(solution)/shard_map/all_to_all | solution.py:94
  303.9 12.1 %copy-start.4 = (bf16[8,8192]{1,0:T(8,128)(2,1)S(1)}, bf16[8,8192]{1,0:T(8,128)(2,1)}, u32[]{:S(2)}) copy-start(bf16[8,8192]{1,0:T(8,128)(2,1)} %param.14) | copy-start | bytes 393220
  316.8 6.0 %copy-start.3 = (bf16[896,512]{1,0:T(8,128)(2,1)S(1)}, bf16[896,512]{1,0:T(8,128)(2,1)}, u32[]{:S(2)}) copy-start(bf16[896,512]{1,0:T(8,128)(2,1)} %fusion.14) | copy-start | bytes 2752516
Sparse Core Ops, SparseCore 0:
  10.2 45.3 all-gather.4
  58.1 86.3 reduce-scatter.1
  147.1 62.2 all-gather.6
  211.5 46.6 all-gather.8
  259.8 57.0 all-gather.10
